TPU v7x, 32 devices: a whole 2x2x4 slice. The times are simulated.
32 devices in a mesh: grp: 2 (over y), shot: 4 (over x, core), cable: 4 (over z).
Axes of the slice: x: 2, y: 2, z: 4, core: 2. Of those that a mesh axis runs over, the one named last changes fastest.
Arguments:
- features: bfloat16 [4, 128, 32, 8, 128], P('cable', None, ('grp', 'shot')), parts along dimension 2, may hold values from -6 to 6
- counts: int32 [32, 4], P('grp', 'cable'), parts along dimension 0, may hold values from 64 to 128, as said below
- first_weight: bfloat16 [5, 3, 5, 64, 64], replicated, may hold values from -0.09375 to 0.09375
- second_weight: bfloat16 [5, 3, 5, 64, 64], replicated, may hold values from -0.09375 to 0.09375
Outputs:
- denoised: bfloat16 [4, 128, 32, 8, 128], P('cable', 'shot', 'grp'), parts along dimension 2
There are 2 independent parts, one for each index of `grp`. A program takes and returns all parts, laid end to end along the dimension named above; an argument that names none is the same for every part. Nothing has to cross between parts.
Inputs may be any that keep to these rules, and one draw needn't show every extreme that they name: counts[s, c] is the number of live receivers of streamer c in shot s; receivers j < counts[s, c] are live; in every draw some gather has all 128 receivers live.
All inputs are finite; a program needn't handle non-finite values.
Results may differ from a plain program's by a relative error of at most 0.003.
Values may be sent and summed in bfloat16 or wider, within the bound.
No kernel may reach another device: no remote copies, remote signals or barrier semaphores. Data moves between devices by JAX's collectives and lax.ppermute only.
A program may use at most 128 MiB of HBM per device.

v0:
```python
import jax
import jax.numpy as jnp
from jax import lax
from jax.sharding import PartitionSpec as P


def extended(block, sides, width):
    for axis, dim in sides:
        count = lax.axis_size(axis)
        forward = [(i, i + 1) for i in range(count - 1)]
        backward = [(target, source) for source, target in forward]
        low = lax.ppermute(
            lax.slice_in_dim(block, block.shape[dim] - width, None, axis=dim), axis, forward
        )
        high = lax.ppermute(lax.slice_in_dim(block, 0, width, axis=dim), axis, backward)
        block = jnp.concatenate([low, block, high], axis=dim)
    return block


def pair_weights(weight):
    channels = weight.shape[3]
    zeroed = jnp.zeros(weight.shape[:2] + (channels, channels), weight.dtype)
    row_blocks = []
    for time_step in range(3):
        for in_phase in range(2):
            column_blocks = []
            for out_phase in range(2):
                tap_time = 2 * time_step + in_phase - out_phase
                if 0 <= tap_time <= 4:
                    column_blocks.append(weight[:, :, tap_time])
                else:
                    column_blocks.append(zeroed)
            row_blocks.append(jnp.concatenate(column_blocks, axis=3))
    return jnp.concatenate(row_blocks, axis=2)


def convolve(padded, weight_pairs, dilation, row_count, shot_count):
    frames = padded.shape[3] - 2
    stacked = jnp.concatenate(
        [
            padded[:, :, :, 0:frames],
            padded[:, :, :, 1 : frames + 1],
            padded[:, :, :, 2 : frames + 2],
        ],
        axis=4,
    )
    summed = jnp.zeros(
        (padded.shape[0], row_count, shot_count, frames, weight_pairs.shape[3]), jnp.float32
    )
    for tap_row in range(5):
        for tap_shot in range(3):
            window = stacked[
                :,
                tap_row * dilation : tap_row * dilation + row_count,
                tap_shot : tap_shot + shot_count,
            ]
            summed = summed + jnp.einsum(
                "arsuk,kl->arsul",
                window,
                weight_pairs[tap_row, tap_shot],
                preferred_element_type=jnp.float32,
            )
    return summed


def residual_layer(inputs, padded, weight_pairs, dilation, alive_mask):
    convolved = convolve(padded, weight_pairs, dilation, inputs.shape[1], inputs.shape[2])
    return (alive_mask * (inputs.astype(jnp.float32) + jnp.maximum(convolved, 0.0))).astype(
        jnp.bfloat16
    )


def live_mask(counts, row_count, shot_start, shot_count):
    chosen = lax.dynamic_slice_in_dim(counts[:, 0], shot_start, shot_count)
    receiver_ids = jnp.arange(row_count, dtype=jnp.int32)
    alive_grid = receiver_ids[:, None] < chosen[None, :]
    return alive_grid.astype(jnp.float32)[None, :, :, None, None]


def body(features, counts, first_weight, second_weight):
    receivers = features.shape[1]
    shot_local = features.shape[2]
    shot_index = lax.axis_index("shot")
    first_pairs = pair_weights(first_weight)
    second_pairs = pair_weights(second_weight)
    shot_mask = live_mask(counts, receivers, shot_index * shot_local, shot_local)
    inputs = features * shot_mask.astype(jnp.bfloat16)
    bordered = extended(inputs, (("shot", 2),), 1)
    padded = jnp.pad(bordered, ((0, 0), (2, 2), (0, 0), (1, 1), (0, 0)))
    hidden = residual_layer(inputs, padded, first_pairs, 1, shot_mask)
    edged = extended(hidden, (("shot", 2),), 1)
    framed = jnp.pad(edged, ((0, 0), (8, 8), (0, 0), (1, 1), (0, 0)))
    result = residual_layer(hidden, framed, second_pairs, 4, shot_mask)
    return lax.all_to_all(result, "shot", split_axis=1, concat_axis=2, tiled=True)


def solution(mesh):
    placed = (P("cable", None, ("grp", "shot"), None, None), P("grp", "cable"), P(), P())
    return jax.shard_map(
        body,
        mesh=mesh,
        in_specs=placed,
        out_specs=P("cable", "shot", "grp", None, None),
        check_vma=False,
    )
```

profile of v0, /device:TPU:0, one launch (start us, length us, event | category | flops | bytes accessed | tf_op | source)
XLA Modules:
  0.0 121.2 jit_solution(1254893385038334431)
XLA Ops:
  0.0 0.7 copy-done
  0.7 0.1 dynamic-slice_bitcast_fusion
  0.7 0.1 fusion.46
  0.8 1.5 %copy_multiply_fusion = bf16[1,128,4,8,128]{4,1,3,2,0:T(8,128)(2,1)S(1)} fusion(bf16[1,128,4,8,128]{4,3,2,1,0:T(8,128)(2,1)} %param.4, bf16[128,4]{0,1:T(4,128)(2,1)S(1)} %get-tuple-element.26), kind=kLoop, calls=%fused_computation.92 | loop fusion | flops 524288 | bytes 2098176 | tf_op jit(solution)/shard_map/mul | solution.py:87
  2.4 2.4 %collective-permute-start = (bf16[1,128,1,8,128]{4,1,3,2,0:T(8,128)(2,1)S(1)}, bf16[1,128,1,8,128]{4,1,3,2,0:T(8,128)(2,1)S(1)}, u32[]{:S(2)}, u32[]{:S(2)}) collective-permute-start(bf16[1,128,1,8,128]{4,1,3,2,0:T(8,128)(2,1)S(1)} %get-tuple-element.23), channel_id=1, source_target_pairs={{0,4},{4,8},{8,12},{1,5},{5,9},{9,13},{2,6},{6,10},{10,14},{3,7},{... | collective-permute-start | bytes 786440 | tf_op jit(solution)/shard_map/ppermute | solution.py:12
  4.8 1.3 %collective-permute-start.1 = (bf16[1,128,1,8,128]{4,1,3,2,0:T(8,128)(2,1)S(1)}, bf16[1,128,1,8,128]{4,1,3,2,0:T(8,128)(2,1)S(1)}, u32[]{:S(2)}, u32[]{:S(2)}) collective-permute-start(bf16[1,128,1,8,128]{4,1,3,2,0:T(8,128)(2,1)S(1)} %get-tuple-element.24), channel_id=1, source_target_pairs={{4,0},{8,4},{12,8},{5,1},{9,5},{13,9},{6,2},{10,6},{14,10},{7,3},{... | collective-permute-start | bytes 786440 | tf_op jit(solution)/shard_map/ppermute | solution.py:15
  6.1 0.1 slice_bitcast_fusion.69
  6.2 0.1 pad_dynamic-update-slice_fusion.3
  6.3 0.2 maximum_dynamic-update-slice_fusion.3
  6.5 0.2 maximum_dynamic-update-slice_fusion.2
  6.7 0.2 maximum_dynamic-update-slice_fusion.1
  6.9 0.2 maximum_dynamic-update-slice_fusion
  7.1 0.2 pad_dynamic-update-slice_fusion.2
  7.3 0.2 copy-done.4
  7.5 0.1 slice_bitcast_fusion.64
  7.6 0.1 pad_dynamic-update-slice_fusion.1
  7.7 0.2 maximum_dynamic-update-slice_fusion.7
  7.9 0.2 maximum_dynamic-update-slice_fusion.6
  8.1 2.3 %collective-permute-done.1 = bf16[1,128,1,8,128]{4,1,3,2,0:T(8,128)(2,1)S(1)} collective-permute-done((bf16[1,128,1,8,128]{4,1,3,2,0:T(8,128)(2,1)S(1)}, bf16[1,128,1,8,128]{4,1,3,2,0:T(8,128)(2,1)S(1)}, u32[]{:S(2)}, u32[]{:S(2)}) %collective-permute-start.1) | collective-permute-done | bytes 262176 | tf_op jit(solution)/shard_map/ppermute | solution.py:15
  10.3 1.4 %select_maximum_fusion.2 = bf16[1,132,6,10,128]{4,1,3,2,0:T(8,128)(2,1)S(1)} fusion(bf16[1,128,1,8,128]{4,1,3,2,0:T(8,128)(2,1)S(1)} %collective-permute-done.1, bf16[1,128,4,8,128]{4,1,3,2,0:T(8,128)(2,1)S(1)} %copy_multiply_fusion, bf16[1,128,1,8,128]{4,1,3,2,0:T(8,128)(2,1)S(1)} %collective-permute-done), kind=kLoop, calls=%fused_computation.87 | loop fusion | flops 19261440 | bytes 3600384 | tf_op jit(solution)/shard_map/concatenate | solution.py:16
  11.7 0.7 fusion.49
  12.4 0.9 pad_maximum_fusion.1
  13.3 1.0 fusion.28
  14.3 2.4 %fusion.29 = f32[128,4,8,128]{3,0,2,1:T(8,128)} fusion(bf16[1,132,6,8,384]{4,1,3,2,0:T(8,128)(2,1)S(1)} %pad_maximum_fusion.1, bf16[5,3,384,128]{3,2,1,0:T(8,128)(2,1)S(1)} %pad_dynamic-update-slice_fusion.2), kind=kOutput, calls=%fused_computation.63 | convolution fusion | flops 402653184 | bytes 5341184 | tf_op jit(solution)/shard_map/arsuk,kl->arsul/dot_general | solution.py:57
  16.7 2.3 %fusion.30 = f32[128,4,8,128]{3,0,2,1:T(8,128)} fusion(bf16[1,132,6,8,384]{4,1,3,2,0:T(8,128)(2,1)S(1)} %pad_maximum_fusion.1, bf16[5,3,384,128]{3,2,1,0:T(8,128)(2,1)S(1)} %pad_dynamic-update-slice_fusion.2), kind=kOutput, calls=%fused_computation.65 | convolution fusion | flops 402653184 | bytes 5341184 | tf_op jit(solution)/shard_map/arsuk,kl->arsul/dot_general | solution.py:57
  19.0 2.4 %fusion.31 = f32[128,4,8,128]{3,0,2,1:T(8,128)} fusion(bf16[1,132,6,8,384]{4,1,3,2,0:T(8,128)(2,1)S(1)} %pad_maximum_fusion.1, bf16[5,3,384,128]{3,2,1,0:T(8,128)(2,1)S(1)} %pad_dynamic-update-slice_fusion.2), kind=kOutput, calls=%fused_computation.67 | convolution fusion | flops 402653184 | bytes 5341184 | tf_op jit(solution)/shard_map/arsuk,kl->arsul/dot_general | solution.py:57
  21.4 2.3 %fusion.32 = f32[128,4,8,128]{3,0,2,1:T(8,128)} fusion(bf16[1,132,6,8,384]{4,1,3,2,0:T(8,128)(2,1)S(1)} %pad_maximum_fusion.1, bf16[5,3,384,128]{3,2,1,0:T(8,128)(2,1)S(1)} %pad_dynamic-update-slice_fusion.2), kind=kOutput, calls=%fused_computation.69 | convolution fusion | flops 402653184 | bytes 5341184 | tf_op jit(solution)/shard_map/arsuk,kl->arsul/dot_general | solution.py:57
  23.7 1.0 fusion.33
  24.7 1.0 fusion.34
  25.7 1.0 fusion.35
  26.7 2.3 %fusion.27 = f32[128,4,8,128]{3,0,2,1:T(8,128)} fusion(bf16[1,132,6,8,384]{4,1,3,2,0:T(8,128)(2,1)S(1)} %pad_maximum_fusion.1, bf16[5,3,384,128]{3,2,1,0:T(8,128)(2,1)S(1)} %pad_dynamic-update-slice_fusion.2), kind=kOutput, calls=%fused_computation.59 | convolution fusion | flops 402653184 | bytes 5341184 | tf_op jit(solution)/shard_map/arsuk,kl->arsul/dot_general | solution.py:57
  29.0 2.4 %fusion.26 = f32[128,4,8,128]{3,0,2,1:T(8,128)} fusion(bf16[1,132,6,8,384]{4,1,3,2,0:T(8,128)(2,1)S(1)} %pad_maximum_fusion.1, bf16[5,3,384,128]{3,2,1,0:T(8,128)(2,1)S(1)} %pad_dynamic-update-slice_fusion.2), kind=kOutput, calls=%fused_computation.57 | convolution fusion | flops 402653184 | bytes 5341184 | tf_op jit(solution)/shard_map/arsuk,kl->arsul/dot_general | solution.py:57
  31.5 2.4 %fusion.25 = f32[128,4,8,128]{3,0,2,1:T(8,128)} fusion(bf16[1,132,6,8,384]{4,1,3,2,0:T(8,128)(2,1)S(1)} %pad_maximum_fusion.1, bf16[5,3,384,128]{3,2,1,0:T(8,128)(2,1)S(1)} %pad_dynamic-update-slice_fusion.2), kind=kOutput, calls=%fused_computation.55 | convolution fusion | flops 402653184 | bytes 5341184 | tf_op jit(solution)/shard_map/arsuk,kl->arsul/dot_general | solution.py:57
  33.8 2.4 %fusion.24 = f32[128,4,8,128]{3,0,2,1:T(8,128)} fusion(bf16[1,132,6,8,384]{4,1,3,2,0:T(8,128)(2,1)S(1)} %pad_maximum_fusion.1, bf16[5,3,384,128]{3,2,1,0:T(8,128)(2,1)S(1)} %pad_dynamic-update-slice_fusion.2), kind=kOutput, calls=%fused_computation.53 | convolution fusion | flops 402653184 | bytes 5341184 | tf_op jit(solution)/shard_map/arsuk,kl->arsul/dot_general | solution.py:57
  36.2 2.6 %fusion.23 = f32[128,4,8,128]{3,0,2,1:T(8,128)} fusion(bf16[1,132,6,8,384]{4,1,3,2,0:T(8,128)(2,1)S(1)} %pad_maximum_fusion.1, bf16[5,3,384,128]{3,2,1,0:T(8,128)(2,1)S(1)} %pad_dynamic-update-slice_fusion.2), kind=kOutput, calls=%fused_computation.51 | convolution fusion | flops 402653184 | bytes 5341184 | tf_op jit(solution)/shard_map/arsuk,kl->arsul/dot_general | solution.py:57
  38.8 2.4 %fusion.22 = f32[128,4,8,128]{3,0,2,1:T(8,128)} fusion(bf16[1,132,6,8,384]{4,1,3,2,0:T(8,128)(2,1)S(1)} %pad_maximum_fusion.1, bf16[5,3,384,128]{3,2,1,0:T(8,128)(2,1)S(1)} %pad_dynamic-update-slice_fusion.2), kind=kOutput, calls=%fused_computation.49 | convolution fusion | flops 402653184 | bytes 5341184 | tf_op jit(solution)/shard_map/arsuk,kl->arsul/dot_general | solution.py:57
  41.2 8.5 %fusion.42 = bf16[1,128,4,8,128]{4,1,3,2,0:T(8,128)(2,1)S(1)} fusion(f32[128,4,8,128]{3,0,2,1:T(8,128)} %fusion.22, f32[128,4,8,128]{3,0,2,1:T(8,128)} %fusion.23, f32[128,4,8,128]{3,0,2,1:T(8,128)} %fusion.24, f32[128,4,8,128]{3,0,2,1:T(8,128)} %fusion.25, f32[128,4,8,128]{3,0,2,1:T(8,128)} %fusion.26, f32[128,4,8,128]{3,0,2,1:T(8,128)} %fusion.27, ...), kind=kOutput, calls=%fused_computation.86 | convolution fusion | flops 412614656 | bytes 34703360 | tf_op jit(solution)/shard_map/arsuk,kl->arsul/dot_general | solution.py:57
  49.8 6.7 %collective-permute-start.2 = (bf16[1,128,1,8,128]{4,1,3,2,0:T(8,128)(2,1)S(1)}, bf16[1,128,1,8,128]{4,1,3,2,0:T(8,128)(2,1)S(1)}, u32[]{:S(2)}, u32[]{:S(2)}) collective-permute-start(bf16[1,128,1,8,128]{4,1,3,2,0:T(8,128)(2,1)S(1)} %get-tuple-element.21), channel_id=1, source_target_pairs={{0,4},{4,8},{8,12},{1,5},{5,9},{9,13},{2,6},{6,10},{10,14},{3,7},{... | collective-permute-start | bytes 786440 | tf_op jit(solution)/shard_map/ppermute | solution.py:12
  56.5 1.3 %collective-permute-start.3 = (bf16[1,128,1,8,128]{4,1,3,2,0:T(8,128)(2,1)S(1)}, bf16[1,128,1,8,128]{4,1,3,2,0:T(8,128)(2,1)S(1)}, u32[]{:S(2)}, u32[]{:S(2)}) collective-permute-start(bf16[1,128,1,8,128]{4,1,3,2,0:T(8,128)(2,1)S(1)} %get-tuple-element.22), channel_id=1, source_target_pairs={{4,0},{8,4},{12,8},{5,1},{9,5},{13,9},{6,2},{10,6},{14,10},{7,3},{... | collective-permute-start | bytes 786440 | tf_op jit(solution)/shard_map/ppermute | solution.py:15
  57.8 0.9 maximum_dynamic-update-slice_fusion.5
  58.6 0.8 maximum_dynamic-update-slice_fusion.4
  59.5 0.8 pad_dynamic-update-slice_fusion
  60.3 0.8 select_maximum_fusion
  61.2 0.7 fusion.48
  61.9 0.8 pad_maximum_fusion
  62.7 0.6 copy-done.6
  63.3 1.0 fusion.13
  64.2 1.0 fusion.14
  65.2 2.4 %fusion.15 = f32[128,4,8,128]{3,0,2,1:T(8,128)} fusion(bf16[1,144,6,8,384]{4,1,3,2,0:T(8,128)(2,1)S(1)} %pad_maximum_fusion, bf16[5,3,384,128]{3,2,1,0:T(8,128)(2,1)S(1)} %copy-done.6), kind=kOutput, calls=%fused_computation.35 | convolution fusion | flops 402653184 | bytes 5341184 | tf_op jit(solution)/shard_map/arsuk,kl->arsul/dot_general | solution.py:57
  67.6 2.3 %fusion.16 = f32[128,4,8,128]{3,0,2,1:T(8,128)} fusion(bf16[1,144,6,8,384]{4,1,3,2,0:T(8,128)(2,1)S(1)} %pad_maximum_fusion, bf16[5,3,384,128]{3,2,1,0:T(8,128)(2,1)S(1)} %copy-done.6), kind=kOutput, calls=%fused_computation.37 | convolution fusion | flops 402653184 | bytes 5341184 | tf_op jit(solution)/shard_map/arsuk,kl->arsul/dot_general | solution.py:57
  69.9 2.3 %fusion.17 = f32[128,4,8,128]{3,0,2,1:T(8,128)} fusion(bf16[1,144,6,8,384]{4,1,3,2,0:T(8,128)(2,1)S(1)} %pad_maximum_fusion, bf16[5,3,384,128]{3,2,1,0:T(8,128)(2,1)S(1)} %copy-done.6), kind=kOutput, calls=%fused_computation.39 | convolution fusion | flops 402653184 | bytes 5341184 | tf_op jit(solution)/shard_map/arsuk,kl->arsul/dot_general | solution.py:57
  72.2 1.0 fusion.18
  73.2 1.0 fusion.19
  74.2 1.0 fusion.20
  75.2 2.3 %fusion.12 = f32[128,4,8,128]{3,0,2,1:T(8,128)} fusion(bf16[1,144,6,8,384]{4,1,3,2,0:T(8,128)(2,1)S(1)} %pad_maximum_fusion, bf16[5,3,384,128]{3,2,1,0:T(8,128)(2,1)S(1)} %copy-done.6), kind=kOutput, calls=%fused_computation.29 | convolution fusion | flops 402653184 | bytes 5341184 | tf_op jit(solution)/shard_map/arsuk,kl->arsul/dot_general | solution.py:57
  77.5 2.4 %fusion.11 = f32[128,4,8,128]{3,0,2,1:T(8,128)} fusion(bf16[1,144,6,8,384]{4,1,3,2,0:T(8,128)(2,1)S(1)} %pad_maximum_fusion, bf16[5,3,384,128]{3,2,1,0:T(8,128)(2,1)S(1)} %copy-done.6), kind=kOutput, calls=%fused_computation.27 | convolution fusion | flops 402653184 | bytes 5341184 | tf_op jit(solution)/shard_map/arsuk,kl->arsul/dot_general | solution.py:57
  79.9 2.4 %fusion.10 = f32[128,4,8,128]{3,0,2,1:T(8,128)} fusion(bf16[1,144,6,8,384]{4,1,3,2,0:T(8,128)(2,1)S(1)} %pad_maximum_fusion, bf16[5,3,384,128]{3,2,1,0:T(8,128)(2,1)S(1)} %copy-done.6), kind=kOutput, calls=%fused_computation.25 | convolution fusion | flops 402653184 | bytes 5341184 | tf_op jit(solution)/shard_map/arsuk,kl->arsul/dot_general | solution.py:57
  82.3 2.4 %fusion.9 = f32[128,4,8,128]{3,0,2,1:T(8,128)} fusion(bf16[1,144,6,8,384]{4,1,3,2,0:T(8,128)(2,1)S(1)} %pad_maximum_fusion, bf16[5,3,384,128]{3,2,1,0:T(8,128)(2,1)S(1)} %copy-done.6), kind=kOutput, calls=%fused_computation.23 | convolution fusion | flops 402653184 | bytes 5341184 | tf_op jit(solution)/shard_map/arsuk,kl->arsul/dot_general | solution.py:57
  84.7 2.3 %fusion.8 = f32[128,4,8,128]{3,0,2,1:T(8,128)} fusion(bf16[1,144,6,8,384]{4,1,3,2,0:T(8,128)(2,1)S(1)} %pad_maximum_fusion, bf16[5,3,384,128]{3,2,1,0:T(8,128)(2,1)S(1)} %copy-done.6), kind=kOutput, calls=%fused_computation.21 | convolution fusion | flops 402653184 | bytes 5341184 | tf_op jit(solution)/shard_map/arsuk,kl->arsul/dot_general | solution.py:57
  87.0 2.6 %fusion.7 = f32[128,4,8,128]{3,0,2,1:T(8,128)} fusion(bf16[1,144,6,8,384]{4,1,3,2,0:T(8,128)(2,1)S(1)} %pad_maximum_fusion, bf16[5,3,384,128]{3,2,1,0:T(8,128)(2,1)S(1)} %copy-done.6), kind=kOutput, calls=%fused_computation.19 | convolution fusion | flops 402653184 | bytes 5341184 | tf_op jit(solution)/shard_map/arsuk,kl->arsul/dot_general | solution.py:57
  89.6 9.2 %fusion.40 = bf16[1,128,4,8,128]{4,1,3,2,0:T(8,128)(2,1)} fusion(f32[128,4,8,128]{3,0,2,1:T(8,128)} %fusion.7, f32[128,4,8,128]{3,0,2,1:T(8,128)} %fusion.8, f32[128,4,8,128]{3,0,2,1:T(8,128)} %fusion.9, f32[128,4,8,128]{3,0,2,1:T(8,128)} %fusion.10, f32[128,4,8,128]{3,0,2,1:T(8,128)} %fusion.11, f32[128,4,8,128]{3,0,2,1:T(8,128)} %fusion.12, ...), kind=kOutput, calls=%fused_computation.83 | convolution fusion | flops 412614656 | bytes 34703360 | tf_op jit(solution)/shard_map/arsuk,kl->arsul/dot_general | solution.py:57
  98.8 1.9 %copy.28 = bf16[1,128,4,8,128]{4,3,2,0,1:T(8,128)(2,1)S(1)} copy(bf16[1,128,4,8,128]{4,1,3,2,0:T(8,128)(2,1)} %fusion.40) | data formatting | bytes 2097152 | tf_op jit(solution)/shard_map/convert_element_type | solution.py:68
  100.8 19.3 %all_to_all.18 = bf16[1,128,4,8,128]{4,3,2,0,1:T(8,128)(2,1)S(1)} all-to-all(bf16[1,128,4,8,128]{4,3,2,0,1:T(8,128)(2,1)S(1)} %copy.28), channel_id=1, replica_groups=mesh['grp'=2,'shot'=4,'cable'=4] {'shot'}, dimensions={1} | all-to-all | bytes 2097152 | tf_op jit(solution)/shard_map/all_to_all | solution.py:94
  120.1 1.1 copy.29
  (18 shorter events, 0.1 us)
Async XLA Ops:
  0.0 0.7 copy-start
  0.0 6.1 %copy-start.3 = (bf16[5,3,5,64,64]{4,3,2,1,0:T(8,128)(2,1)S(1)}, bf16[5,3,5,64,64]{4,3,2,1,0:T(8,128)(2,1)}, u32[]{:S(2)}) copy-start(bf16[5,3,5,64,64]{4,3,2,1,0:T(8,128)(2,1)} %param.6) | copy-start | bytes 1843204
  2.4 5.7 %collective-permute-start = (bf16[1,128,1,8,128]{4,1,3,2,0:T(8,128)(2,1)S(1)}, bf16[1,128,1,8,128]{4,1,3,2,0:T(8,128)(2,1)S(1)}, u32[]{:S(2)}, u32[]{:S(2)}) collective-permute-start(bf16[1,128,1,8,128]{4,1,3,2,0:T(8,128)(2,1)S(1)} %get-tuple-element.23), channel_id=1, source_target_pairs={{0,4},{4,8},{8,12},{1,5},{5,9},{9,13},{2,6},{6,10},{10,14},{3,7},{... | collective-permute-start | bytes 786440 | tf_op jit(solution)/shard_map/ppermute | solution.py:12
  4.8 5.5 %collective-permute-start.1 = (bf16[1,128,1,8,128]{4,1,3,2,0:T(8,128)(2,1)S(1)}, bf16[1,128,1,8,128]{4,1,3,2,0:T(8,128)(2,1)S(1)}, u32[]{:S(2)}, u32[]{:S(2)}) collective-permute-start(bf16[1,128,1,8,128]{4,1,3,2,0:T(8,128)(2,1)S(1)} %get-tuple-element.24), channel_id=1, source_target_pairs={{4,0},{8,4},{12,8},{5,1},{9,5},{13,9},{6,2},{10,6},{14,10},{7,3},{... | collective-permute-start | bytes 786440 | tf_op jit(solution)/shard_map/ppermute | solution.py:15
  6.2 1.3 %copy-start.4 = (bf16[5,3,5,64,64]{4,3,2,1,0:T(8,128)(2,1)S(1)}, bf16[5,3,5,64,64]{4,3,2,1,0:T(8,128)(2,1)}, u32[]{:S(2)}) copy-start(bf16[5,3,5,64,64]{4,3,2,1,0:T(8,128)(2,1)} %param.7) | copy-start | bytes 1843204
  7.5 31.3 %copy-start.7 = (bf16[5,3,384,128]{3,2,1,0:T(8,128)(2,1)}, bf16[5,3,384,128]{3,2,1,0:T(8,128)(2,1)S(1)}, u32[]{:S(2)}) copy-start(bf16[5,3,384,128]{3,2,1,0:T(8,128)(2,1)S(1)} %pad_dynamic-update-slice_fusion.2) | copy-start | bytes 4423684
  8.1 4.4 %copy-start.5 = (bf16[5,3,384,128]{3,2,1,0:T(8,128)(2,1)}, bf16[5,3,384,128]{3,2,1,0:T(8,128)(2,1)S(1)}, u32[]{:S(2)}) copy-start(bf16[5,3,384,128]{3,2,1,0:T(8,128)(2,1)S(1)} %maximum_dynamic-update-slice_fusion.6) | copy-start | bytes 4423684
  49.7 11.4 %copy-start.2 = (bf16[1,128,4,8,128]{4,1,3,2,0:T(8,128)(2,1)}, bf16[1,128,4,8,128]{4,1,3,2,0:T(8,128)(2,1)S(1)}, u32[]{:S(2)}) copy-start(bf16[1,128,4,8,128]{4,1,3,2,0:T(8,128)(2,1)S(1)} %fusion.42) | copy-start | bytes 3145732
  49.8 10.5 %collective-permute-start.2 = (bf16[1,128,1,8,128]{4,1,3,2,0:T(8,128)(2,1)S(1)}, bf16[1,128,1,8,128]{4,1,3,2,0:T(8,128)(2,1)S(1)}, u32[]{:S(2)}, u32[]{:S(2)}) collective-permute-start(bf16[1,128,1,8,128]{4,1,3,2,0:T(8,128)(2,1)S(1)} %get-tuple-element.21), channel_id=1, source_target_pairs={{0,4},{4,8},{8,12},{1,5},{5,9},{9,13},{2,6},{6,10},{10,14},{3,7},{... | collective-permute-start | bytes 786440 | tf_op jit(solution)/shard_map/ppermute | solution.py:12
  56.5 3.9 %collective-permute-start.3 = (bf16[1,128,1,8,128]{4,1,3,2,0:T(8,128)(2,1)S(1)}, bf16[1,128,1,8,128]{4,1,3,2,0:T(8,128)(2,1)S(1)}, u32[]{:S(2)}, u32[]{:S(2)}) collective-permute-start(bf16[1,128,1,8,128]{4,1,3,2,0:T(8,128)(2,1)S(1)} %get-tuple-element.22), channel_id=1, source_target_pairs={{4,0},{8,4},{12,8},{5,1},{9,5},{13,9},{6,2},{10,6},{14,10},{7,3},{... | collective-permute-start | bytes 786440 | tf_op jit(solution)/shard_map/ppermute | solution.py:15
  61.9 1.4 %copy-start.6 = (bf16[5,3,384,128]{3,2,1,0:T(8,128)(2,1)S(1)}, bf16[5,3,384,128]{3,2,1,0:T(8,128)(2,1)}, u32[]{:S(2)}) copy-start(bf16[5,3,384,128]{3,2,1,0:T(8,128)(2,1)} %pad_dynamic-update-slice_fusion) | copy-start | bytes 4423684
  98.8 22.4 %copy-start.1 = (s32[16,1]{0,1:T(1,128)S(1)}, s32[16,1]{0,1:T(1,128)}, u32[]{:S(2)}) copy-start(s32[16,1]{0,1:T(1,128)} %param.5) | copy-start | bytes 196
where the time goes:
time: 122 us; the launch traced here: 121 us
  matrix products  71.9 us (59%)
  blocking collectives  19.3 us (16%)
  starting transfers between devices  11.7 us (10%)
  other arithmetic  8.32 us (7%)
  local copies, waits for them, and re-layouts  7.38 us (6%)
  waiting for transfers between devices  2.26 us (2%)
    dot_general x30, matrix products, convolve(): jnp.einsum('arsuk,kl->arsul', window, weight_pairs[tap_row, tap_shot], pr...  71.9 us
    all_to_all x1, blocking collectives, body(): lax.all_to_all(result, 'shot', split_axis=1, concat_axis=2, tiled=True)  19.3 us
    ppermute x2, starting transfers between devices, extended(): lax.ppermute(lax.slice_in_dim(block, block.shape[dim] - width, None, axis...  9.08 us
    unnamed x8, other arithmetic  2.84 us
    ppermute x2, starting transfers between devices, extended(): lax.ppermute(lax.slice_in_dim(block, 0, width, axis=dim), axis, backward)  2.58 us
  transfers between devices with their start and end apart: 4, of which 1 were waited for; matrix products, arithmetic and copies ran while one was open for 3% of the time, Pallas kernels for 0%

commit v1 on v0

v1 whole, which is shorter than its diff:
```python
import functools

import jax
import jax.numpy as jnp
from jax import lax
from jax.experimental import pallas as pl
from jax.experimental.pallas import tpu as pltpu
from jax.sharding import PartitionSpec as P


def extended(block, axis, dim, width):
    count = lax.axis_size(axis)
    forward = [(i, i + 1) for i in range(count - 1)]
    backward = [(target, source) for source, target in forward]
    low = lax.ppermute(
        lax.slice_in_dim(block, block.shape[dim] - width, None, axis=dim), axis, forward
    )
    high = lax.ppermute(lax.slice_in_dim(block, 0, width, axis=dim), axis, backward)
    return jnp.concatenate([low, block, high], axis=dim)


def pair_weights(weight):
    channels = weight.shape[3]
    zeroed = jnp.zeros(weight.shape[:2] + (channels, channels), weight.dtype)
    row_blocks = []
    for time_step in range(3):
        for in_phase in range(2):
            column_blocks = []
            for out_phase in range(2):
                tap_time = 2 * time_step + in_phase - out_phase
                if 0 <= tap_time <= 4:
                    column_blocks.append(weight[:, :, tap_time])
                else:
                    column_blocks.append(zeroed)
            row_blocks.append(jnp.concatenate(column_blocks, axis=3))
    stacked = jnp.concatenate(row_blocks, axis=2)
    return stacked.reshape((-1,) + stacked.shape[2:])


def stack_time(block, dilation):
    pairs = block.shape[2]
    padded = jnp.pad(block, ((0, 0), (2 * dilation, 2 * dilation), (1, 1), (0, 0)))
    stacked = jnp.concatenate(
        [padded[:, :, 0:pairs], padded[:, :, 1 : pairs + 1], padded[:, :, 2 : pairs + 2]],
        axis=3,
    )
    return stacked.reshape(stacked.shape[0], -1, stacked.shape[3])


def conv_kernel(counts_ref, xs_ref, w_ref, res_ref, out_ref, acc_ref, *, dilation, pairs):
    s = pl.program_id(0)
    rows = acc_ref.shape[0]
    for a in range(5):
        for b in range(3):
            lhs = xs_ref[s + b, pl.ds(a * dilation * pairs, rows), :]
            contrib = jnp.dot(lhs, w_ref[a * 3 + b], preferred_element_type=jnp.float32)
            if a == 0 and b == 0:
                acc_ref[...] = contrib
            else:
                acc_ref[...] += contrib
    receiver = lax.broadcasted_iota(jnp.int32, acc_ref.shape, 0) // pairs
    live = receiver < counts_ref[s]
    value = res_ref[0].astype(jnp.float32) + jnp.maximum(acc_ref[...], 0.0)
    out_ref[0] = jnp.where(live, value, 0.0).astype(out_ref.dtype)


def conv_layer(counts, bordered, residual, weights, dilation):
    shots, receivers, pairs, lanes = residual.shape
    rows = receivers * pairs
    xs = stack_time(bordered, dilation)
    flat = residual.reshape(shots, rows, lanes)
    out = pl.pallas_call(
        functools.partial(conv_kernel, dilation=dilation, pairs=pairs),
        grid_spec=pltpu.PrefetchScalarGridSpec(
            num_scalar_prefetch=1,
            grid=(shots,),
            in_specs=[
                pl.BlockSpec(xs.shape, lambda s, c: (0, 0, 0)),
                pl.BlockSpec(weights.shape, lambda s, c: (0, 0, 0)),
                pl.BlockSpec((1, rows, lanes), lambda s, c: (s, 0, 0)),
            ],
            out_specs=pl.BlockSpec((1, rows, lanes), lambda s, c: (s, 0, 0)),
            scratch_shapes=[pltpu.VMEM((rows, lanes), jnp.float32)],
        ),
        out_shape=jax.ShapeDtypeStruct((shots, rows, lanes), jnp.bfloat16),
        compiler_params=pltpu.CompilerParams(vmem_limit_bytes=48 * 1024 * 1024),
    )(counts, xs, weights, flat)
    return out.reshape(shots, receivers, pairs, lanes)


def body(features, counts, first_weight, second_weight):
    receivers = features.shape[1]
    shot_local = features.shape[2]
    shot_index = lax.axis_index("shot")
    chosen = lax.dynamic_slice_in_dim(counts[:, 0], shot_index * shot_local, shot_local)
    first_pairs = pair_weights(first_weight)
    second_pairs = pair_weights(second_weight)
    volume = jnp.transpose(features[0], (1, 0, 2, 3))
    alive = jnp.arange(receivers, dtype=jnp.int32)[None, :] < chosen[:, None]
    inputs = volume * alive.astype(volume.dtype)[:, :, None, None]
    bordered = extended(inputs, "shot", 0, 1)
    hidden = conv_layer(chosen, bordered, inputs, first_pairs, 1)
    edged = extended(hidden, "shot", 0, 1)
    result = conv_layer(chosen, edged, hidden, second_pairs, 4)
    moved = lax.all_to_all(result, "shot", split_axis=1, concat_axis=0, tiled=True)
    return jnp.transpose(moved, (1, 0, 2, 3))[None]


def solution(mesh):
    placed = (P("cable", None, ("grp", "shot"), None, None), P("grp", "cable"), P(), P())
    return jax.shard_map(
        body,
        mesh=mesh,
        in_specs=placed,
        out_specs=P("cable", "shot", "grp", None, None),
        check_vma=False,
    )
```

time: 122 us -> 88.2 us (0.72)
  matrix products: 71.9 us -> 0 us
  Pallas kernels: 0 us -> 32.6 us
  other arithmetic: 8.32 us -> 15.5 us
  local copies, waits for them, and re-layouts: 7.38 us -> 5.55 us
    dot_general x30 -> x0, matrix products: 71.9 us -> none  [convolve(): jnp.einsum('arsuk,kl->arsul', window, weight_pairs[tap_row, tap_shot], pr...]
    pallas_call x0 -> x2, Pallas kernels: none -> 32.6 us  [conv_layer(): pl.pallas_call(functools.partial(conv_kernel, dilation=dilation, pairs=pa...]
    reshape x0 -> x3, other arithmetic: none -> 6.21 us  [the longest x2 5.52 us: stack_time(): return stacked.reshape(stacked.shape[0], -1, stacked.shape[3])]
    concatenate x4 -> x2, other arithmetic: 3.86 us -> 6.12 us  [extended(): return jnp.concatenate([low, block, high], axis=dim)]
    convert_element_type x1 -> x0, local copies, waits for them, and re-layouts: 1.91 us -> none  [residual_layer(): (alive_mask * (inputs.astype(jnp.float32) + jnp.maximum(convolved, 0.0)))...]
    unnamed x8, other arithmetic: 2.84 us -> 1.45 us
  transfers between devices with their start and end apart: 4 -> 4, of which waited for: 1 -> 2; matrix products, arithmetic and copies ran while one was open for 3% -> 3% of each run, Pallas kernels for 0% -> 0%
where the time goes in v1:
time: 88.2 us; the launch traced here: 87.8 us
  Pallas kernels  32.6 us (37%)
  blocking collectives  19.8 us (22%)
  other arithmetic  15.5 us (18%)
  starting transfers between devices  11.9 us (13%)
  local copies, waits for them, and re-layouts  5.55 us (6%)
  waiting for transfers between devices  2.22 us (3%)
    pallas_call x2, Pallas kernels, conv_layer(): pl.pallas_call(functools.partial(conv_kernel, dilation=dilation, pairs=pa...  32.6 us
    all_to_all x1, blocking collectives, body(): lax.all_to_all(result, 'shot', split_axis=1, concat_axis=0, tiled=True)  19.8 us
    ppermute x2, starting transfers between devices, extended(): lax.ppermute(lax.slice_in_dim(block, block.shape[dim] - width, None, axis...  9.09 us
    concatenate x2, other arithmetic, extended(): return jnp.concatenate([low, block, high], axis=dim)  6.12 us
    reshape x2, other arithmetic, stack_time(): return stacked.reshape(stacked.shape[0], -1, stacked.shape[3])  5.52 us
    ppermute x2, starting transfers between devices, extended(): lax.ppermute(lax.slice_in_dim(block, 0, width, axis=dim), axis, backward)  2.76 us
    ppermute x2, waiting for transfers between devices, extended(): lax.ppermute(lax.slice_in_dim(block, 0, width, axis=dim), axis, backward)  2.21 us
    unnamed x10, local copies, waits for them, and re-layouts  1.83 us
  transfers between devices with their start and end apart: 4, of which 2 were waited for; matrix products, arithmetic and copies ran while one was open for 3% of the time, Pallas kernels for 0%

profile of v1, /device:TPU:0, one launch (start us, length us, event | category | flops | bytes accessed | tf_op | source)
XLA Modules:
  0.0 87.8 jit_solution(7571590458221192685)
XLA Ops:
  0.0 0.0 copy-start
  0.0 0.0 copy-start.2
  0.0 0.7 copy-done
  0.7 0.1 dynamic-slice_bitcast_fusion.counts_ref
  0.7 1.7 %bitcast_multiply_fusion = bf16[4,128,8,128]{3,2,0,1:T(8,128)(2,1)S(1)} fusion(bf16[1,128,4,8,128]{4,3,2,1,0:T(8,128)(2,1)} %param.4, bf16[4,128]{0,1:T(8,128)(2,1)S(1)} %fusion.12), kind=kLoop, calls=%fused_computation.27 | loop fusion | flops 524288 | bytes 2098176 | tf_op jit(solution)/shard_map/mul | solution.py:100
  2.5 2.4 %collective-permute-start = (bf16[1,128,8,128]{3,2,0,1:T(8,128)(2,1)S(1)}, bf16[1,128,8,128]{3,2,0,1:T(8,128)(2,1)S(1)}, u32[]{:S(2)}, u32[]{:S(2)}) collective-permute-start(bf16[1,128,8,128]{3,2,0,1:T(8,128)(2,1)S(1)} %get-tuple-element.23), channel_id=1, source_target_pairs={{0,4},{4,8},{8,12},{1,5},{5,9},{9,13},{2,6},{6,10},{10,14},{3,7},{... | collective-permute-start | bytes 786440 | tf_op jit(solution)/shard_map/ppermute | solution.py:15
  5.0 1.3 %collective-permute-start.1 = (bf16[1,128,8,128]{3,2,0,1:T(8,128)(2,1)S(1)}, bf16[1,128,8,128]{3,2,0,1:T(8,128)(2,1)S(1)}, u32[]{:S(2)}, u32[]{:S(2)}) collective-permute-start(bf16[1,128,8,128]{3,2,0,1:T(8,128)(2,1)S(1)} %get-tuple-element.24), channel_id=1, source_target_pairs={{4,0},{8,4},{12,8},{5,1},{9,5},{13,9},{6,2},{10,6},{14,10},{7,3},{... | collective-permute-start | bytes 786440 | tf_op jit(solution)/shard_map/ppermute | solution.py:18
  6.3 0.0 copy-done.2
  6.3 0.1 slice_bitcast_fusion.7
  6.4 0.1 pad_dynamic-update-slice_fusion.3
  6.4 0.0 copy-start.3
  6.5 0.2 maximum_dynamic-update-slice_fusion.3
  6.6 0.2 maximum_dynamic-update-slice_fusion.2
  6.8 0.2 maximum_dynamic-update-slice_fusion.1
  7.0 0.2 maximum_dynamic-update-slice_fusion
  7.2 0.2 pad_dynamic-update-slice_fusion.2
  7.4 0.4 copy-done.3
  7.7 0.0 copy-start.1
  7.7 0.1 slice_bitcast_fusion.2
  7.8 0.1 pad_dynamic-update-slice_fusion.1
  7.9 0.2 maximum_dynamic-update-slice_fusion.7
  8.1 0.2 maximum_dynamic-update-slice_fusion.6
  8.3 0.7 copy-done.1
  9.0 0.7 copy_bitcast_fusion.1.res_ref
  9.7 0.0 collective-permute-done
  9.7 0.8 collective-permute-done.1
  10.5 3.5 %select_maximum_fusion.2 = bf16[6,132,10,128]{3,2,0,1:T(8,128)(2,1)S(1)} fusion(bf16[1,128,8,128]{3,2,0,1:T(8,128)(2,1)S(1)} %collective-permute-done.1, bf16[4,128,8,128]{3,2,0,1:T(8,128)(2,1)S(1)} %bitcast_multiply_fusion, bf16[1,128,8,128]{3,2,0,1:T(8,128)(2,1)S(1)} %collective-permute-done), kind=kLoop, calls=%fused_computation.22 | loop fusion | flops 19261440 | bytes 3600384 | tf_op jit(solution)/shard_map/concatenate | solution.py:19
  14.0 0.9 fusion.14
  14.9 2.5 %copy_bitcast_fusion.xs_ref = bf16[6,1056,384]{2,1,0:T(8,128)(2,1)} fusion(bf16[6,132,8,128]{3,2,0,1:T(8,128)(2,1)S(1)} %get-tuple-element.10, bf16[6,132,8,128]{3,2,0,1:T(8,128)(2,1)S(1)} %get-tuple-element.9, bf16[6,132,8,128]{3,2,0,1:T(8,128)(2,1)S(1)} %get-tuple-element.8), kind=kLoop, calls=%fused_computation.16 | loop fusion | flops 14598144 | bytes 9732096 | tf_op jit(solution)/shard_map/reshape | solution.py:47
  17.4 16.3 %shard_map.46.res_ref = bf16[4,1024,128]{2,1,0:T(8,128)(2,1)S(1)} custom-call(s32[4]{0:T(128)S(1)} %dynamic-slice_bitcast_fusion.counts_ref, bf16[6,1056,384]{2,1,0:T(8,128)(2,1)} %copy_bitcast_fusion.xs_ref, bf16[15,384,128]{2,1,0:T(8,128)(2,1)S(1)} %bitcast.68, bf16[4,1024,128]{2,1,0:T(8,128)(2,1)S(1)} %copy_bitcast_fusion.1.res_ref), custom_call_target="tpu_custom_call" | custom-call | tf_op jit(solution)/shard_map/pallas_call | solution.py:72
  33.8 6.7 %collective-permute-start.2 = (bf16[1,128,8,128]{3,2,1,0:T(8,128)(2,1)S(1)}, bf16[1,128,8,128]{3,2,1,0:T(8,128)(2,1)S(1)}, u32[]{:S(2)}, u32[]{:S(2)}) collective-permute-start(bf16[1,128,8,128]{3,2,1,0:T(8,128)(2,1)S(1)} %get-tuple-element.21), channel_id=1, source_target_pairs={{0,4},{4,8},{8,12},{1,5},{5,9},{9,13},{2,6},{6,10},{10,14},{3,7},{... | collective-permute-start | bytes 786440 | tf_op jit(solution)/shard_map/ppermute | solution.py:15
  40.5 1.5 %collective-permute-start.3 = (bf16[1,128,8,128]{3,2,1,0:T(8,128)(2,1)S(1)}, bf16[1,128,8,128]{3,2,1,0:T(8,128)(2,1)S(1)}, u32[]{:S(2)}, u32[]{:S(2)}) collective-permute-start(bf16[1,128,8,128]{3,2,1,0:T(8,128)(2,1)S(1)} %get-tuple-element.22), channel_id=1, source_target_pairs={{4,0},{8,4},{12,8},{5,1},{9,5},{13,9},{6,2},{10,6},{14,10},{7,3},{... | collective-permute-start | bytes 786440 | tf_op jit(solution)/shard_map/ppermute | solution.py:18
  42.0 0.2 maximum_dynamic-update-slice_fusion.5
  42.1 0.2 maximum_dynamic-update-slice_fusion.4
  42.3 0.2 pad_dynamic-update-slice_fusion
  42.5 0.0 collective-permute-done.2
  42.5 1.4 %collective-permute-done.3 = bf16[1,128,8,128]{3,2,1,0:T(8,128)(2,1)S(1)} collective-permute-done((bf16[1,128,8,128]{3,2,1,0:T(8,128)(2,1)S(1)}, bf16[1,128,8,128]{3,2,1,0:T(8,128)(2,1)S(1)}, u32[]{:S(2)}, u32[]{:S(2)}) %collective-permute-start.3) | collective-permute-done | bytes 262176 | tf_op jit(solution)/shard_map/ppermute | solution.py:18
  43.9 2.6 %select_maximum_fusion = bf16[6,144,10,128]{3,2,1,0:T(8,128)(2,1)S(1)} fusion(bf16[1,128,8,128]{3,2,1,0:T(8,128)(2,1)S(1)} %collective-permute-done.3, bf16[4,128,8,128]{3,2,1,0:T(8,128)(2,1)S(1)} %bitcast.65, bf16[1,128,8,128]{3,2,1,0:T(8,128)(2,1)S(1)} %collective-permute-done.2), kind=kLoop, calls=%fused_computation.17 | loop fusion | flops 21012480 | bytes 3784704 | tf_op jit(solution)/shard_map/concatenate | solution.py:19
  46.5 0.9 %fusion.13 = (bf16[6,144,8,128]{3,2,1,0:T(8,128)(2,1)S(1)}, bf16[6,144,8,128]{3,2,1,0:T(8,128)(2,1)S(1)}, bf16[6,144,8,128]{3,2,1,0:T(8,128)(2,1)S(1)}) fusion(bf16[6,144,10,128]{3,2,1,0:T(8,128)(2,1)S(1)} %select_maximum_fusion), kind=kLoop, calls=%fused_computation.56 | loop fusion | bytes 10616832 | tf_op jit(solution)/shard_map/slice | solution.py:44
  47.5 3.0 %maximum_bitcast_fusion.xs_ref = bf16[6,1152,384]{2,1,0:T(8,128)(2,1)} fusion(bf16[6,144,8,128]{3,2,1,0:T(8,128)(2,1)S(1)} %get-tuple-element.7, bf16[6,144,8,128]{3,2,1,0:T(8,128)(2,1)S(1)} %get-tuple-element.6, bf16[6,144,8,128]{3,2,1,0:T(8,128)(2,1)S(1)} %get-tuple-element.5), kind=kLoop, calls=%fused_computation.14 | loop fusion | flops 15925248 | bytes 10616832 | tf_op jit(solution)/shard_map/reshape | solution.py:47
  50.5 16.3 %shard_map.47 = bf16[4,1024,128]{2,1,0:T(8,128)(2,1)S(1)} custom-call(s32[4]{0:T(128)S(1)} %dynamic-slice_bitcast_fusion.counts_ref, bf16[6,1152,384]{2,1,0:T(8,128)(2,1)} %maximum_bitcast_fusion.xs_ref, bf16[15,384,128]{2,1,0:T(8,128)(2,1)S(1)} %bitcast.67, bf16[4,1024,128]{2,1,0:T(8,128)(2,1)S(1)} %shard_map.46.res_ref), custom_call_target="tpu_custom_call" | custom-call | tf_op jit(solution)/shard_map/pallas_call | solution.py:72
  66.7 0.2 copy.26
  66.9 19.8 %all_to_all.18 = bf16[4,128,8,128]{3,2,0,1:T(8,128)(2,1)S(1)} all-to-all(bf16[4,128,8,128]{3,2,0,1:T(8,128)(2,1)S(1)} %copy.26), channel_id=1, replica_groups=mesh['grp'=2,'shot'=4,'cable'=4] {'shot'}, dimensions={1} | all-to-all | bytes 2097152 | tf_op jit(solution)/shard_map/all_to_all | solution.py:105
  86.7 1.1 %copy.27 = bf16[4,4,32,8,128]{4,3,1,0,2:T(8,128)(2,1)} copy(bf16[4,4,32,8,128]{4,3,1,2,0:T(8,128)(2,1)S(1)} %bitcast.69) | data formatting | bytes 2097152 | tf_op jit(solution)/shard_map/all_to_all | solution.py:105
  (3 shorter events, 0.1 us)
Async XLA Ops:
  0.0 0.7 copy-start
  0.0 6.3 %copy-start.2 = (bf16[5,3,5,64,64]{4,3,2,1,0:T(8,128)(2,1)S(1)}, bf16[5,3,5,64,64]{4,3,2,1,0:T(8,128)(2,1)}, u32[]{:S(2)}) copy-start(bf16[5,3,5,64,64]{4,3,2,1,0:T(8,128)(2,1)} %param.6) | copy-start | bytes 1843204
  2.5 7.1 %collective-permute-start = (bf16[1,128,8,128]{3,2,0,1:T(8,128)(2,1)S(1)}, bf16[1,128,8,128]{3,2,0,1:T(8,128)(2,1)S(1)}, u32[]{:S(2)}, u32[]{:S(2)}) collective-permute-start(bf16[1,128,8,128]{3,2,0,1:T(8,128)(2,1)S(1)} %get-tuple-element.23), channel_id=1, source_target_pairs={{0,4},{4,8},{8,12},{1,5},{5,9},{9,13},{2,6},{6,10},{10,14},{3,7},{... | collective-permute-start | bytes 786440 | tf_op jit(solution)/shard_map/ppermute | solution.py:15
  5.0 5.5 %collective-permute-start.1 = (bf16[1,128,8,128]{3,2,0,1:T(8,128)(2,1)S(1)}, bf16[1,128,8,128]{3,2,0,1:T(8,128)(2,1)S(1)}, u32[]{:S(2)}, u32[]{:S(2)}) collective-permute-start(bf16[1,128,8,128]{3,2,0,1:T(8,128)(2,1)S(1)} %get-tuple-element.24), channel_id=1, source_target_pairs={{4,0},{8,4},{12,8},{5,1},{9,5},{13,9},{6,2},{10,6},{14,10},{7,3},{... | collective-permute-start | bytes 786440 | tf_op jit(solution)/shard_map/ppermute | solution.py:18
  6.4 1.3 %copy-start.3 = (bf16[5,3,5,64,64]{4,3,2,1,0:T(8,128)(2,1)S(1)}, bf16[5,3,5,64,64]{4,3,2,1,0:T(8,128)(2,1)}, u32[]{:S(2)}) copy-start(bf16[5,3,5,64,64]{4,3,2,1,0:T(8,128)(2,1)} %param.7) | copy-start | bytes 1843204
  7.7 1.2 %copy-start.1 = (bf16[1,128,4,8,128]{4,3,2,1,0:T(8,128)(2,1)S(1)}, bf16[1,128,4,8,128]{4,3,2,1,0:T(8,128)(2,1)}, u32[]{:S(2)}) copy-start(bf16[1,128,4,8,128]{4,3,2,1,0:T(8,128)(2,1)} %param.4) | copy-start | bytes 3145732
  33.8 8.7 %collective-permute-start.2 = (bf16[1,128,8,128]{3,2,1,0:T(8,128)(2,1)S(1)}, bf16[1,128,8,128]{3,2,1,0:T(8,128)(2,1)S(1)}, u32[]{:S(2)}, u32[]{:S(2)}) collective-permute-start(bf16[1,128,8,128]{3,2,1,0:T(8,128)(2,1)S(1)} %get-tuple-element.21), channel_id=1, source_target_pairs={{0,4},{4,8},{8,12},{1,5},{5,9},{9,13},{2,6},{6,10},{10,14},{3,7},{... | collective-permute-start | bytes 786440 | tf_op jit(solution)/shard_map/ppermute | solution.py:15
  40.5 3.4 %collective-permute-start.3 = (bf16[1,128,8,128]{3,2,1,0:T(8,128)(2,1)S(1)}, bf16[1,128,8,128]{3,2,1,0:T(8,128)(2,1)S(1)}, u32[]{:S(2)}, u32[]{:S(2)}) collective-permute-start(bf16[1,128,8,128]{3,2,1,0:T(8,128)(2,1)S(1)} %get-tuple-element.22), channel_id=1, source_target_pairs={{4,0},{8,4},{12,8},{5,1},{9,5},{13,9},{6,2},{10,6},{14,10},{7,3},{... | collective-permute-start | bytes 786440 | tf_op jit(solution)/shard_map/ppermute | solution.py:18

commit v2 on v1

--- a/solution.py
+++ b/solution.py
@@ -47,7 +47,7 @@
     return stacked.reshape(stacked.shape[0], -1, stacked.shape[3])
 
 
-def conv_kernel(counts_ref, xs_ref, w_ref, res_ref, out_ref, acc_ref, *, dilation, pairs):
+def conv_kernel(scalars_ref, xs_ref, w_ref, res_ref, out_ref, acc_ref, *, dilation, pairs):
     s = pl.program_id(0)
     rows = acc_ref.shape[0]
     for a in range(5):
@@ -58,52 +58,80 @@
                 acc_ref[...] = contrib
             else:
                 acc_ref[...] += contrib
-    receiver = lax.broadcasted_iota(jnp.int32, acc_ref.shape, 0) // pairs
-    live = receiver < counts_ref[s]
+    first = scalars_ref[0] * (rows // pairs)
+    receiver = first + lax.broadcasted_iota(jnp.int32, acc_ref.shape, 0) // pairs
+    live = receiver < scalars_ref[1 + s]
     value = res_ref[0].astype(jnp.float32) + jnp.maximum(acc_ref[...], 0.0)
     out_ref[0] = jnp.where(live, value, 0.0).astype(out_ref.dtype)
 
 
-def conv_layer(counts, bordered, residual, weights, dilation):
-    shots, receivers, pairs, lanes = residual.shape
-    rows = receivers * pairs
-    xs = stack_time(bordered, dilation)
-    flat = residual.reshape(shots, rows, lanes)
-    out = pl.pallas_call(
+def conv_call(xs, weights, flat, counts, dilation, pairs, block, block_rows):
+    shots, _, lanes = flat.shape
+    window = block_rows + 4 * dilation * pairs
+    scalars = jnp.concatenate([jnp.reshape(block, (1,)).astype(jnp.int32), counts])
+    flops = 2 * shots * 15 * block_rows * xs.shape[2] * lanes
+    return pl.pallas_call(
         functools.partial(conv_kernel, dilation=dilation, pairs=pairs),
         grid_spec=pltpu.PrefetchScalarGridSpec(
             num_scalar_prefetch=1,
             grid=(shots,),
             in_specs=[
-                pl.BlockSpec(xs.shape, lambda s, c: (0, 0, 0)),
+                pl.BlockSpec(
+                    (pl.Element(xs.shape[0]), pl.Element(window), pl.Element(xs.shape[2])),
+                    lambda s, c: (0, c[0] * block_rows, 0),
+                ),
                 pl.BlockSpec(weights.shape, lambda s, c: (0, 0, 0)),
-                pl.BlockSpec((1, rows, lanes), lambda s, c: (s, 0, 0)),
+                pl.BlockSpec((1, block_rows, lanes), lambda s, c: (s, c[0], 0)),
             ],
-            out_specs=pl.BlockSpec((1, rows, lanes), lambda s, c: (s, 0, 0)),
-            scratch_shapes=[pltpu.VMEM((rows, lanes), jnp.float32)],
+            out_specs=pl.BlockSpec((1, block_rows, lanes), lambda s, c: (s, 0, 0)),
+            scratch_shapes=[pltpu.VMEM((block_rows, lanes), jnp.float32)],
         ),
-        out_shape=jax.ShapeDtypeStruct((shots, rows, lanes), jnp.bfloat16),
+        out_shape=jax.ShapeDtypeStruct((shots, block_rows, lanes), jnp.bfloat16),
         compiler_params=pltpu.CompilerParams(vmem_limit_bytes=48 * 1024 * 1024),
-    )(counts, xs, weights, flat)
-    return out.reshape(shots, receivers, pairs, lanes)
+        cost_estimate=pl.CostEstimate(
+            flops=flops,
+            transcendentals=0,
+            bytes_accessed=xs.shape[0] * window * xs.shape[2] * 2 + weights.size * 2
+            + 4 * shots * block_rows * lanes,
+        ),
+    )(scalars, xs, weights, flat)
 
 
 def body(features, counts, first_weight, second_weight):
     receivers = features.shape[1]
     shot_local = features.shape[2]
-    shot_index = lax.axis_index("shot")
-    chosen = lax.dynamic_slice_in_dim(counts[:, 0], shot_index * shot_local, shot_local)
+    pairs = features.shape[3]
+    lanes = features.shape[4]
+    count = lax.axis_size("shot")
+    me = lax.axis_index("shot")
+    chosen = lax.dynamic_slice_in_dim(counts[:, 0], me * shot_local, shot_local)
     first_pairs = pair_weights(first_weight)
     second_pairs = pair_weights(second_weight)
     volume = jnp.transpose(features[0], (1, 0, 2, 3))
     alive = jnp.arange(receivers, dtype=jnp.int32)[None, :] < chosen[:, None]
     inputs = volume * alive.astype(volume.dtype)[:, :, None, None]
     bordered = extended(inputs, "shot", 0, 1)
-    hidden = conv_layer(chosen, bordered, inputs, first_pairs, 1)
+    xs1 = stack_time(bordered, 1)
+    flat1 = inputs.reshape(shot_local, receivers * pairs, lanes)
+    hidden = conv_call(xs1, first_pairs, flat1, chosen, 1, pairs, 0, receivers * pairs)
+    hidden = hidden.reshape(shot_local, receivers, pairs, lanes)
     edged = extended(hidden, "shot", 0, 1)
-    result = conv_layer(chosen, edged, hidden, second_pairs, 4)
-    moved = lax.all_to_all(result, "shot", split_axis=1, concat_axis=0, tiled=True)
-    return jnp.transpose(moved, (1, 0, 2, 3))[None]
+    xs2 = stack_time(edged, 4)
+    flat2 = hidden.reshape(shot_local, receivers * pairs, lanes)
+    span = receivers // count
+    arrived = []
+    for shift in list(range(1, count)) + [0]:
+        target = lax.rem(me + shift, count)
+        piece = conv_call(xs2, second_pairs, flat2, chosen, 4, pairs, target, span * pairs)
+        if shift:
+            pairs_list = [(i, (i + shift) % count) for i in range(count)]
+            piece = lax.ppermute(piece, "shot", pairs_list)
+        arrived.append((shift, piece))
+    by_shift = jnp.stack([piece for _, piece in sorted(arrived, key=lambda t: t[0])])
+    order = lax.rem(me - jnp.arange(count, dtype=jnp.int32) + count, count)
+    ordered = jnp.take(by_shift, order, axis=0)
+    ordered = ordered.reshape(count * shot_local, span, pairs, lanes)
+    return jnp.transpose(ordered, (1, 0, 2, 3))[None]
 
 
 def solution(mesh):

time: 88.2 us -> 85.7 us (0.972)
  blocking collectives: 19.8 us -> 0 us
  Pallas kernels: 32.6 us -> 39.8 us
  starting transfers between devices: 11.9 us -> 18.3 us
  other arithmetic: 15.5 us -> 19.1 us
    all_to_all x1 -> x0, blocking collectives: 19.8 us -> none  [body(): lax.all_to_all(result, 'shot', split_axis=1, concat_axis=0, tiled=True)]
    pallas_call x2 -> x5, Pallas kernels: 32.6 us -> 39.8 us  [conv_call(): pl.pallas_call(functools.partial(conv_kernel, dilation=dilation, pairs=pa...]
    ppermute x0 -> x3, starting transfers between devices: none -> 5.78 us  [body(): piece = lax.ppermute(piece, 'shot', pairs_list)]
    broadcast_in_dim x0 -> x1, other arithmetic: none -> 1.25 us  [body(): return jnp.transpose(ordered, (1, 0, 2, 3))[None]]
    another operation x0 -> x1, other arithmetic: none -> 1.24 us  [body(): jnp.stack([piece for _, piece in sorted(arrived, key=lambda t: t[0])])]
    all_to_all x1 -> x0, local copies, waits for them, and re-layouts: 1.09 us -> none  [body(): lax.all_to_all(result, 'shot', split_axis=1, concat_axis=0, tiled=True)]
    concatenate x2, other arithmetic: 6.12 us -> 7.12 us  [extended(): return jnp.concatenate([low, block, high], axis=dim)]
  transfers between devices with their start and end apart: 4 -> 7, of which waited for: 2 -> 2; matrix products, arithmetic and copies ran while one was open for 3% -> 4% of each run, Pallas kernels for 0% -> 21%
where the time goes in v2:
time: 85.7 us; the launch traced here: 85.2 us
  Pallas kernels  39.8 us (46%)
  other arithmetic  19.1 us (22%)
  starting transfers between devices  18.3 us (21%)
  local copies, waits for them, and re-layouts  5.82 us (7%)
  waiting for transfers between devices  1.96 us (2%)
    pallas_call x5, Pallas kernels, conv_call(): pl.pallas_call(functools.partial(conv_kernel, dilation=dilation, pairs=pa...  39.8 us
    ppermute x2, starting transfers between devices, extended(): lax.ppermute(lax.slice_in_dim(block, block.shape[dim] - width, None, axis...  9.75 us
    concatenate x2, other arithmetic, extended(): return jnp.concatenate([low, block, high], axis=dim)  7.12 us
    ppermute x3, starting transfers between devices, body(): piece = lax.ppermute(piece, 'shot', pairs_list)  5.78 us
    reshape x2, other arithmetic, stack_time(): return stacked.reshape(stacked.shape[0], -1, stacked.shape[3])  5.5 us
    ppermute x2, starting transfers between devices, extended(): lax.ppermute(lax.slice_in_dim(block, 0, width, axis=dim), axis, backward)  2.75 us
    ppermute x2, waiting for transfers between devices, extended(): lax.ppermute(lax.slice_in_dim(block, 0, width, axis=dim), axis, backward)  1.95 us
    slice x2, local copies, waits for them, and re-layouts, stack_time(): padded[:, :, 0:pairs]  1.79 us
  transfers between devices with their start and end apart: 7, of which 2 were waited for; matrix products, arithmetic and copies ran while one was open for 4% of the time, Pallas kernels for 21%

profile of v2, /device:TPU:0, one launch (start us, length us, event | category | flops | bytes accessed | tf_op | source)
XLA Modules:
  0.0 85.2 jit_solution(15488663470073100649)
XLA Ops:
  0.0 0.0 copy-start
  0.0 0.0 copy-start.2
  0.0 0.7 copy-done
  0.7 0.1 dynamic-slice_bitcast_fusion
  0.7 1.7 %bitcast_multiply_fusion = bf16[4,128,8,128]{3,2,0,1:T(8,128)(2,1)S(1)} fusion(bf16[1,128,4,8,128]{4,3,2,1,0:T(8,128)(2,1)} %param.4, bf16[4,128]{0,1:T(8,128)(2,1)S(1)} %fusion.13), kind=kLoop, calls=%fused_computation.29 | loop fusion | flops 524288 | bytes 2098176 | tf_op jit(solution)/shard_map/mul | solution.py:112
  2.5 0.8 fusion.19
  3.3 3.1 %collective-permute-start = (bf16[1,128,8,128]{3,2,0,1:T(8,128)(2,1)}, bf16[1,128,8,128]{3,2,0,1:T(8,128)(2,1)}, u32[]{:S(2)}, u32[]{:S(2)}) collective-permute-start(bf16[1,128,8,128]{3,2,0,1:T(8,128)(2,1)} %get-tuple-element.23), channel_id=1, source_target_pairs={{0,4},{4,8},{8,12},{1,5},{5,9},{9,13},{2,6},{6,10},{10,14},{3,7},{... | collective-permute-start | bytes 786440 | tf_op jit(solution)/shard_map/ppermute | solution.py:15
  6.4 1.3 %collective-permute-start.1 = (bf16[1,128,8,128]{3,2,0,1:T(8,128)(2,1)}, bf16[1,128,8,128]{3,2,0,1:T(8,128)(2,1)}, u32[]{:S(2)}, u32[]{:S(2)}) collective-permute-start(bf16[1,128,8,128]{3,2,0,1:T(8,128)(2,1)} %get-tuple-element.24), channel_id=1, source_target_pairs={{4,0},{8,4},{12,8},{5,1},{9,5},{13,9},{6,2},{10,6},{14,10},{7,3},{... | collective-permute-start | bytes 786440 | tf_op jit(solution)/shard_map/ppermute | solution.py:18
  7.7 0.0 copy-done.2
  7.7 0.1 slice_bitcast_fusion.7
  7.8 0.1 pad_dynamic-update-slice_fusion.3
  7.9 0.0 copy-start.3
  7.9 0.2 maximum_dynamic-update-slice_fusion.3
  8.1 0.2 maximum_dynamic-update-slice_fusion.2
  8.3 0.2 maximum_dynamic-update-slice_fusion.1
  8.4 0.2 maximum_dynamic-update-slice_fusion
  8.6 0.2 pad_dynamic-update-slice_fusion.2
  8.8 0.4 copy-done.3
  9.2 0.1 slice_bitcast_fusion.2
  9.3 0.0 copy-start.1
  9.3 0.1 pad_dynamic-update-slice_fusion.1
  9.3 0.2 maximum_dynamic-update-slice_fusion.7
  9.5 0.2 maximum_dynamic-update-slice_fusion.6
  9.7 0.2 maximum_dynamic-update-slice_fusion.5
  9.9 0.1 pad_add_fusion
  10.0 0.5 copy-done.1
  10.5 0.7 copy_bitcast_fusion.1.res_ref
  11.2 0.0 collective-permute-done
  11.2 0.4 collective-permute-done.1
  11.6 4.5 %select_maximum_fusion.2 = bf16[6,132,10,128]{3,2,0,1:T(8,128)(2,1)S(1)} fusion(bf16[1,128,8,128]{3,2,0,1:T(8,128)(2,1)} %collective-permute-done.1, bf16[4,128,8,128]{3,2,0,1:T(8,128)(2,1)S(1)} %bitcast_multiply_fusion, bf16[1,128,8,128]{3,2,0,1:T(8,128)(2,1)} %collective-permute-done), kind=kLoop, calls=%fused_computation.23 | loop fusion | flops 19261440 | bytes 3600384 | tf_op jit(solution)/shard_map/concatenate | solution.py:19
  16.1 0.9 %fusion.18 = (bf16[6,132,8,128]{3,2,0,1:T(8,128)(2,1)S(1)}, bf16[6,132,8,128]{3,2,0,1:T(8,128)(2,1)S(1)}, bf16[6,132,8,128]{3,2,0,1:T(8,128)(2,1)S(1)}) fusion(bf16[6,132,10,128]{3,2,0,1:T(8,128)(2,1)S(1)} %select_maximum_fusion.2), kind=kLoop, calls=%fused_computation.77 | loop fusion | bytes 9732096 | tf_op jit(solution)/shard_map/slice | solution.py:44
  17.0 2.5 %copy_bitcast_fusion.xs_ref = bf16[6,1056,384]{2,1,0:T(8,128)(2,1)} fusion(bf16[6,132,8,128]{3,2,0,1:T(8,128)(2,1)S(1)} %get-tuple-element.10, bf16[6,132,8,128]{3,2,0,1:T(8,128)(2,1)S(1)} %get-tuple-element.9, bf16[6,132,8,128]{3,2,0,1:T(8,128)(2,1)S(1)} %get-tuple-element.8), kind=kLoop, calls=%fused_computation.17 | loop fusion | flops 14598144 | bytes 9732096 | tf_op jit(solution)/shard_map/reshape | solution.py:47
  19.5 16.4 %shard_map.46.res_ref = bf16[4,1024,128]{2,1,0:T(8,128)(2,1)S(1)} custom-call(s32[5]{0:T(128)S(1)} %get-tuple-element.26.scalars_ref, bf16[6,1056,384]{2,1,0:T(8,128)(2,1)} %copy_bitcast_fusion.xs_ref, bf16[15,384,128]{2,1,0:T(8,128)(2,1)S(1)} %bitcast.77, bf16[4,1024,128]{2,1,0:T(8,128)(2,1)S(1)} %copy_bitcast_fusion.1.res_ref), custom_call_target="tpu_custom_call" | custom-call | flops 6039797760 | bytes 8437760 | tf_op jit(solution)/shard_map/pallas_call | solution.py:73
  35.9 6.7 %collective-permute-start.2 = (bf16[1,128,8,128]{3,2,1,0:T(8,128)(2,1)S(1)}, bf16[1,128,8,128]{3,2,1,0:T(8,128)(2,1)S(1)}, u32[]{:S(2)}, u32[]{:S(2)}) collective-permute-start(bf16[1,128,8,128]{3,2,1,0:T(8,128)(2,1)S(1)} %get-tuple-element.21), channel_id=1, source_target_pairs={{0,4},{4,8},{8,12},{1,5},{5,9},{9,13},{2,6},{6,10},{10,14},{3,7},{... | collective-permute-start | bytes 786440 | tf_op jit(solution)/shard_map/ppermute | solution.py:15
  42.6 1.5 %collective-permute-start.3 = (bf16[1,128,8,128]{3,2,1,0:T(8,128)(2,1)S(1)}, bf16[1,128,8,128]{3,2,1,0:T(8,128)(2,1)S(1)}, u32[]{:S(2)}, u32[]{:S(2)}) collective-permute-start(bf16[1,128,8,128]{3,2,1,0:T(8,128)(2,1)S(1)} %get-tuple-element.22), channel_id=1, source_target_pairs={{4,0},{8,4},{12,8},{5,1},{9,5},{13,9},{6,2},{10,6},{14,10},{7,3},{... | collective-permute-start | bytes 786440 | tf_op jit(solution)/shard_map/ppermute | solution.py:18
  44.1 0.2 maximum_dynamic-update-slice_fusion.4
  44.3 0.2 pad_dynamic-update-slice_fusion
  44.4 0.0 collective-permute-done.2
  44.4 1.6 %collective-permute-done.3 = bf16[1,128,8,128]{3,2,1,0:T(8,128)(2,1)S(1)} collective-permute-done((bf16[1,128,8,128]{3,2,1,0:T(8,128)(2,1)S(1)}, bf16[1,128,8,128]{3,2,1,0:T(8,128)(2,1)S(1)}, u32[]{:S(2)}, u32[]{:S(2)}) %collective-permute-start.3) | collective-permute-done | bytes 262176 | tf_op jit(solution)/shard_map/ppermute | solution.py:18
  46.0 2.6 %select_maximum_fusion = bf16[6,144,10,128]{3,2,1,0:T(8,128)(2,1)S(1)} fusion(bf16[1,128,8,128]{3,2,1,0:T(8,128)(2,1)S(1)} %collective-permute-done.3, bf16[4,128,8,128]{3,2,1,0:T(8,128)(2,1)S(1)} %bitcast.71, bf16[1,128,8,128]{3,2,1,0:T(8,128)(2,1)S(1)} %collective-permute-done.2), kind=kLoop, calls=%fused_computation.18 | loop fusion | flops 21012480 | bytes 3784704 | tf_op jit(solution)/shard_map/concatenate | solution.py:19
  48.6 0.9 %fusion.17 = (bf16[6,144,8,128]{3,2,1,0:T(8,128)(2,1)S(1)}, bf16[6,144,8,128]{3,2,1,0:T(8,128)(2,1)S(1)}, bf16[6,144,8,128]{3,2,1,0:T(8,128)(2,1)S(1)}) fusion(bf16[6,144,10,128]{3,2,1,0:T(8,128)(2,1)S(1)} %select_maximum_fusion), kind=kLoop, calls=%fused_computation.76 | loop fusion | bytes 10616832 | tf_op jit(solution)/shard_map/slice | solution.py:44
  49.6 3.0 %maximum_bitcast_fusion.xs_ref = bf16[6,1152,384]{2,1,0:T(8,128)(2,1)} fusion(bf16[6,144,8,128]{3,2,1,0:T(8,128)(2,1)S(1)} %get-tuple-element.7, bf16[6,144,8,128]{3,2,1,0:T(8,128)(2,1)S(1)} %get-tuple-element.6, bf16[6,144,8,128]{3,2,1,0:T(8,128)(2,1)S(1)} %get-tuple-element.5), kind=kLoop, calls=%fused_computation.15 | loop fusion | flops 15925248 | bytes 10616832 | tf_op jit(solution)/shard_map/reshape | solution.py:47
  52.5 5.9 %shard_map.48 = bf16[4,256,128]{2,1,0:T(8,128)(2,1)S(1)} custom-call(s32[5]{0:T(128)S(1)} %get-tuple-element.27.scalars_ref, bf16[6,1152,384]{2,1,0:T(8,128)(2,1)} %maximum_bitcast_fusion.xs_ref, bf16[15,384,128]{2,1,0:T(8,128)(2,1)S(1)} %bitcast.72, bf16[4,1024,128]{2,1,0:T(8,128)(2,1)S(1)} %shard_map.46.res_ref), custom_call_target="tpu_custom_call" | custom-call | flops 1509949440 | bytes 3768320 | tf_op jit(solution)/shard_map/pallas_call | solution.py:73
  58.4 4.3 %collective-permute-start.4 = (bf16[4,256,128]{2,1,0:T(8,128)(2,1)S(1)}, bf16[4,256,128]{2,1,0:T(8,128)(2,1)}, u32[]{:S(2)}, u32[]{:S(2)}) collective-permute-start(bf16[4,256,128]{2,1,0:T(8,128)(2,1)S(1)} %shard_map.48), channel_id=1, source_target_pairs={{0,4},{4,8},{8,12},{12,0},{1,5},{5,9},{9,13},{13,1},{2,6},{6,10},{... | collective-permute-start | bytes 786440 | tf_op jit(solution)/shard_map/ppermute | solution.py:128
  62.7 5.9 %shard_map.49 = bf16[4,256,128]{2,1,0:T(8,128)(2,1)S(1)} custom-call(s32[5]{0:T(128)S(1)} %get-tuple-element.28.scalars_ref, bf16[6,1152,384]{2,1,0:T(8,128)(2,1)} %maximum_bitcast_fusion.xs_ref, bf16[15,384,128]{2,1,0:T(8,128)(2,1)S(1)} %bitcast.73, bf16[4,1024,128]{2,1,0:T(8,128)(2,1)S(1)} %shard_map.46.res_ref), custom_call_target="tpu_custom_call" | custom-call | flops 1509949440 | bytes 3768320 | tf_op jit(solution)/shard_map/pallas_call | solution.py:73
  68.6 0.1 collective-permute-start.5
  68.6 5.9 %shard_map.50 = bf16[4,256,128]{2,1,0:T(8,128)(2,1)S(1)} custom-call(s32[5]{0:T(128)S(1)} %get-tuple-element.29.scalars_ref, bf16[6,1152,384]{2,1,0:T(8,128)(2,1)} %maximum_bitcast_fusion.xs_ref, bf16[15,384,128]{2,1,0:T(8,128)(2,1)S(1)} %bitcast.74, bf16[4,1024,128]{2,1,0:T(8,128)(2,1)S(1)} %shard_map.46.res_ref), custom_call_target="tpu_custom_call" | custom-call | flops 1509949440 | bytes 3768320 | tf_op jit(solution)/shard_map/pallas_call | solution.py:73
  74.5 1.4 %collective-permute-start.6 = (bf16[4,256,128]{2,1,0:T(8,128)(2,1)S(1)}, bf16[4,256,128]{2,1,0:T(8,128)(2,1)}, u32[]{:S(2)}, u32[]{:S(2)}) collective-permute-start(bf16[4,256,128]{2,1,0:T(8,128)(2,1)S(1)} %shard_map.50), channel_id=1, source_target_pairs={{0,12},{4,0},{8,4},{12,8},{1,13},{5,1},{9,5},{13,9},{2,14},{6,2},{... | collective-permute-start | bytes 786440 | tf_op jit(solution)/shard_map/ppermute | solution.py:128
  75.9 0.1 broadcast_in_dim.20
  76.0 0.1 broadcast_in_dim.21
  76.1 5.9 %shard_map.47 = bf16[4,256,128]{2,1,0:T(8,128)(2,1)S(1)} custom-call(s32[5]{0:T(128)S(1)} %get-tuple-element.25.scalars_ref, bf16[6,1152,384]{2,1,0:T(8,128)(2,1)} %maximum_bitcast_fusion.xs_ref, bf16[15,384,128]{2,1,0:T(8,128)(2,1)S(1)} %bitcast.75, bf16[4,1024,128]{2,1,0:T(8,128)(2,1)S(1)} %shard_map.46.res_ref), custom_call_target="tpu_custom_call" | custom-call | flops 1509949440 | bytes 3768320 | tf_op jit(solution)/shard_map/pallas_call | solution.py:73
  82.0 0.0 collective-permute-done.4
  82.0 0.0 collective-permute-done.5
  82.0 0.0 collective-permute-done.6
  82.0 1.2 %pad_maximum_fusion.1 = bf16[4,4,256,128]{3,2,1,0:T(8,128)(2,1)S(1)} fusion(bf16[1,4,256,128]{3,2,1,0:T(8,128)(2,1)} %bitcast.28, bf16[1,4,256,128]{3,2,1,0:T(8,128)(2,1)} %bitcast.26, bf16[1,4,256,128]{3,2,1,0:T(8,128)(2,1)} %bitcast.24, bf16[1,4,256,128]{3,2,1,0:T(8,128)(2,1)S(1)} %bitcast.76), kind=kLoop, calls=%fused_computation.28 | loop fusion | flops 1572864 | bytes 2097152 | tf_op jit(solution)/shard_map/stack | solution.py:130
  83.2 0.7 gather_fusion
  84.0 1.3 %fusion.12 = bf16[1,32,16,8,128]{4,3,2,1,0:T(8,128)(2,1)} fusion(bf16[16,32,8,128]{3,2,1,0:T(8,128)(2,1)S(1)} %bitcast.78, pred[16]{0:T(512)(128)(4,1)S(1)} %broadcast_in_dim.21), kind=kLoop, calls=%fused_computation.31 | loop fusion | flops 524288 | bytes 2097168 | tf_op jit(solution)/shard_map/broadcast_in_dim | solution.py:134
  (5 shorter events, 0.1 us)
Async XLA Ops:
  0.0 0.7 copy-start
  0.0 7.7 %copy-start.2 = (bf16[5,3,5,64,64]{4,3,2,1,0:T(8,128)(2,1)S(1)}, bf16[5,3,5,64,64]{4,3,2,1,0:T(8,128)(2,1)}, u32[]{:S(2)}) copy-start(bf16[5,3,5,64,64]{4,3,2,1,0:T(8,128)(2,1)} %param.6) | copy-start | bytes 1843204
  3.3 7.9 %collective-permute-start = (bf16[1,128,8,128]{3,2,0,1:T(8,128)(2,1)}, bf16[1,128,8,128]{3,2,0,1:T(8,128)(2,1)}, u32[]{:S(2)}, u32[]{:S(2)}) collective-permute-start(bf16[1,128,8,128]{3,2,0,1:T(8,128)(2,1)} %get-tuple-element.23), channel_id=1, source_target_pairs={{0,4},{4,8},{8,12},{1,5},{5,9},{9,13},{2,6},{6,10},{10,14},{3,7},{... | collective-permute-start | bytes 786440 | tf_op jit(solution)/shard_map/ppermute | solution.py:15
  6.4 5.2 %collective-permute-start.1 = (bf16[1,128,8,128]{3,2,0,1:T(8,128)(2,1)}, bf16[1,128,8,128]{3,2,0,1:T(8,128)(2,1)}, u32[]{:S(2)}, u32[]{:S(2)}) collective-permute-start(bf16[1,128,8,128]{3,2,0,1:T(8,128)(2,1)} %get-tuple-element.24), channel_id=1, source_target_pairs={{4,0},{8,4},{12,8},{5,1},{9,5},{13,9},{6,2},{10,6},{14,10},{7,3},{... | collective-permute-start | bytes 786440 | tf_op jit(solution)/shard_map/ppermute | solution.py:18
  7.9 1.3 %copy-start.3 = (bf16[5,3,5,64,64]{4,3,2,1,0:T(8,128)(2,1)S(1)}, bf16[5,3,5,64,64]{4,3,2,1,0:T(8,128)(2,1)}, u32[]{:S(2)}) copy-start(bf16[5,3,5,64,64]{4,3,2,1,0:T(8,128)(2,1)} %param.7) | copy-start | bytes 1843204
  9.3 1.2 %copy-start.1 = (bf16[1,128,4,8,128]{4,3,2,1,0:T(8,128)(2,1)S(1)}, bf16[1,128,4,8,128]{4,3,2,1,0:T(8,128)(2,1)}, u32[]{:S(2)}) copy-start(bf16[1,128,4,8,128]{4,3,2,1,0:T(8,128)(2,1)} %param.4) | copy-start | bytes 3145732
  35.9 8.5 %collective-permute-start.2 = (bf16[1,128,8,128]{3,2,1,0:T(8,128)(2,1)S(1)}, bf16[1,128,8,128]{3,2,1,0:T(8,128)(2,1)S(1)}, u32[]{:S(2)}, u32[]{:S(2)}) collective-permute-start(bf16[1,128,8,128]{3,2,1,0:T(8,128)(2,1)S(1)} %get-tuple-element.21), channel_id=1, source_target_pairs={{0,4},{4,8},{8,12},{1,5},{5,9},{9,13},{2,6},{6,10},{10,14},{3,7},{... | collective-permute-start | bytes 786440 | tf_op jit(solution)/shard_map/ppermute | solution.py:15
  42.6 3.4 %collective-permute-start.3 = (bf16[1,128,8,128]{3,2,1,0:T(8,128)(2,1)S(1)}, bf16[1,128,8,128]{3,2,1,0:T(8,128)(2,1)S(1)}, u32[]{:S(2)}, u32[]{:S(2)}) collective-permute-start(bf16[1,128,8,128]{3,2,1,0:T(8,128)(2,1)S(1)} %get-tuple-element.22), channel_id=1, source_target_pairs={{4,0},{8,4},{12,8},{5,1},{9,5},{13,9},{6,2},{10,6},{14,10},{7,3},{... | collective-permute-start | bytes 786440 | tf_op jit(solution)/shard_map/ppermute | solution.py:18
  58.4 23.6 %collective-permute-start.4 = (bf16[4,256,128]{2,1,0:T(8,128)(2,1)S(1)}, bf16[4,256,128]{2,1,0:T(8,128)(2,1)}, u32[]{:S(2)}, u32[]{:S(2)}) collective-permute-start(bf16[4,256,128]{2,1,0:T(8,128)(2,1)S(1)} %shard_map.48), channel_id=1, source_target_pairs={{0,4},{4,8},{8,12},{12,0},{1,5},{5,9},{9,13},{13,1},{2,6},{6,10},{... | collective-permute-start | bytes 786440 | tf_op jit(solution)/shard_map/ppermute | solution.py:128
  68.6 13.4 %collective-permute-start.5 = (bf16[4,256,128]{2,1,0:T(8,128)(2,1)S(1)}, bf16[4,256,128]{2,1,0:T(8,128)(2,1)}, u32[]{:S(2)}, u32[]{:S(2)}) collective-permute-start(bf16[4,256,128]{2,1,0:T(8,128)(2,1)S(1)} %shard_map.49), channel_id=1, source_target_pairs={{0,8},{4,12},{8,0},{12,4},{1,9},{5,13},{9,1},{13,5},{2,10},{6,14},... | collective-permute-start | bytes 786440 | tf_op jit(solution)/shard_map/ppermute | solution.py:128
  74.5 7.5 %collective-permute-start.6 = (bf16[4,256,128]{2,1,0:T(8,128)(2,1)S(1)}, bf16[4,256,128]{2,1,0:T(8,128)(2,1)}, u32[]{:S(2)}, u32[]{:S(2)}) collective-permute-start(bf16[4,256,128]{2,1,0:T(8,128)(2,1)S(1)} %shard_map.50), channel_id=1, source_target_pairs={{0,12},{4,0},{8,4},{12,8},{1,13},{5,1},{9,5},{13,9},{2,14},{6,2},{... | collective-permute-start | bytes 786440 | tf_op jit(solution)/shard_map/ppermute | solution.py:128

commit v3 on v2

--- a/solution.py
+++ b/solution.py
@@ -45,6 +45,49 @@
         axis=3,
     )
     return stacked.reshape(stacked.shape[0], -1, stacked.shape[3])
+
+
+def spread_call(xs, weights, flat, counts, dilation, pairs):
+    shots, rows, lanes = flat.shape
+    scalars = jnp.concatenate([jnp.zeros((1,), jnp.int32), counts])
+    flops = 2 * shots * 15 * xs.shape[1] * xs.shape[2] * weights.shape[2]
+    return pl.pallas_call(
+        functools.partial(spread_kernel, dilation=dilation, pairs=pairs),
+        grid_spec=pltpu.PrefetchScalarGridSpec(
+            num_scalar_prefetch=1,
+            grid=(shots,),
+            in_specs=[
+                pl.BlockSpec(xs.shape, lambda s, c: (0, 0, 0)),
+                pl.BlockSpec(weights.shape, lambda s, c: (0, 0, 0)),
+                pl.BlockSpec((1, rows, lanes), lambda s, c: (s, 0, 0)),
+            ],
+            out_specs=pl.BlockSpec((1, rows, lanes), lambda s, c: (s, 0, 0)),
+        ),
+        out_shape=jax.ShapeDtypeStruct((shots, rows, lanes), jnp.bfloat16),
+        compiler_params=pltpu.CompilerParams(vmem_limit_bytes=48 * 1024 * 1024),
+        cost_estimate=pl.CostEstimate(
+            flops=flops,
+            transcendentals=0,
+            bytes_accessed=xs.size * 2 + weights.size * 2 + 4 * shots * rows * lanes,
+        ),
+    )(scalars, xs, weights, flat)
+
+
+def spread_kernel(scalars_ref, xs_ref, w_ref, res_ref, out_ref, *, dilation, pairs):
+    s = pl.program_id(0)
+    rows, lanes = out_ref.shape[1:]
+    total = None
+    for b in range(3):
+        taps = jnp.concatenate([w_ref[a * 3 + b] for a in range(5)], axis=1)
+        spread = jnp.dot(xs_ref[s + b], taps, preferred_element_type=jnp.float32)
+        for a in range(5):
+            part = spread[a * dilation * pairs : a * dilation * pairs + rows, a * lanes : (a + 1) * lanes]
+            total = part if total is None else total + part
+    first = scalars_ref[0] * (rows // pairs)
+    receiver = first + lax.broadcasted_iota(jnp.int32, (rows, lanes), 0) // pairs
+    live = receiver < scalars_ref[1 + s]
+    value = res_ref[0].astype(jnp.float32) + jnp.maximum(total, 0.0)
+    out_ref[0] = jnp.where(live, value, 0.0).astype(out_ref.dtype)
 
 
 def conv_kernel(scalars_ref, xs_ref, w_ref, res_ref, out_ref, acc_ref, *, dilation, pairs):
@@ -113,7 +156,7 @@
     bordered = extended(inputs, "shot", 0, 1)
     xs1 = stack_time(bordered, 1)
     flat1 = inputs.reshape(shot_local, receivers * pairs, lanes)
-    hidden = conv_call(xs1, first_pairs, flat1, chosen, 1, pairs, 0, receivers * pairs)
+    hidden = spread_call(xs1, first_pairs, flat1, chosen, 1, pairs)
     hidden = hidden.reshape(shot_local, receivers, pairs, lanes)
     edged = extended(hidden, "shot", 0, 1)
     xs2 = stack_time(edged, 4)

time: 85.7 us -> 82.6 us (0.964)
  Pallas kernels: 39.8 us -> 36.5 us
    pallas_call x5 -> x4, Pallas kernels: 39.8 us -> 23.4 us  [conv_call(): pl.pallas_call(functools.partial(conv_kernel, dilation=dilation, pairs=pa...]
    pallas_call x0 -> x1, Pallas kernels: none -> 13.1 us  [spread_call(): pl.pallas_call(functools.partial(spread_kernel, dilation=dilation, pairs=...]
where the time goes in v3:
time: 82.6 us; the launch traced here: 82.1 us
  Pallas kernels  36.5 us (44%)
  other arithmetic  19.1 us (23%)
  starting transfers between devices  18.3 us (22%)
  local copies, waits for them, and re-layouts  5.82 us (7%)
  waiting for transfers between devices  2.14 us (3%)
    pallas_call x4, Pallas kernels, conv_call(): pl.pallas_call(functools.partial(conv_kernel, dilation=dilation, pairs=pa...  23.4 us
    pallas_call x1, Pallas kernels, spread_call(): pl.pallas_call(functools.partial(spread_kernel, dilation=dilation, pairs=...  13.1 us
    ppermute x2, starting transfers between devices, extended(): lax.ppermute(lax.slice_in_dim(block, block.shape[dim] - width, None, axis...  9.75 us
    concatenate x2, other arithmetic, extended(): return jnp.concatenate([low, block, high], axis=dim)  7.12 us
    ppermute x3, starting transfers between devices, body(): piece = lax.ppermute(piece, 'shot', pairs_list)  5.95 us
    reshape x2, other arithmetic, stack_time(): return stacked.reshape(stacked.shape[0], -1, stacked.shape[3])  5.5 us
    ppermute x2, starting transfers between devices, extended(): lax.ppermute(lax.slice_in_dim(block, 0, width, axis=dim), axis, backward)  2.57 us
    ppermute x2, waiting for transfers between devices, extended(): lax.ppermute(lax.slice_in_dim(block, 0, width, axis=dim), axis, backward)  2.13 us
  transfers between devices with their start and end apart: 7, of which 2 were waited for; matrix products, arithmetic and copies ran while one was open for 4% of the time, Pallas kernels for 21%

profile of v3, /device:TPU:0, one launch (start us, length us, event | category | flops | bytes accessed | tf_op | source)
XLA Modules:
  0.0 82.1 jit_solution(6009513971327888748)
XLA Ops:
  0.0 0.0 copy-start
  0.0 0.0 copy-start.2
  0.0 0.7 copy-done
  0.7 0.1 dynamic-slice_bitcast_fusion
  0.7 1.7 %bitcast_multiply_fusion = bf16[4,128,8,128]{3,2,0,1:T(8,128)(2,1)S(1)} fusion(bf16[1,128,4,8,128]{4,3,2,1,0:T(8,128)(2,1)} %param.4, bf16[4,128]{0,1:T(8,128)(2,1)S(1)} %fusion.13), kind=kLoop, calls=%fused_computation.29 | loop fusion | flops 524288 | bytes 2098176 | tf_op jit(solution)/shard_map/mul | solution.py:155
  2.5 0.8 fusion.19
  3.3 3.1 %collective-permute-start = (bf16[1,128,8,128]{3,2,0,1:T(8,128)(2,1)}, bf16[1,128,8,128]{3,2,0,1:T(8,128)(2,1)}, u32[]{:S(2)}, u32[]{:S(2)}) collective-permute-start(bf16[1,128,8,128]{3,2,0,1:T(8,128)(2,1)} %get-tuple-element.23), channel_id=1, source_target_pairs={{0,4},{4,8},{8,12},{1,5},{5,9},{9,13},{2,6},{6,10},{10,14},{3,7},{... | collective-permute-start | bytes 786440 | tf_op jit(solution)/shard_map/ppermute | solution.py:15
  6.4 1.3 %collective-permute-start.1 = (bf16[1,128,8,128]{3,2,0,1:T(8,128)(2,1)}, bf16[1,128,8,128]{3,2,0,1:T(8,128)(2,1)}, u32[]{:S(2)}, u32[]{:S(2)}) collective-permute-start(bf16[1,128,8,128]{3,2,0,1:T(8,128)(2,1)} %get-tuple-element.24), channel_id=1, source_target_pairs={{4,0},{8,4},{12,8},{5,1},{9,5},{13,9},{6,2},{10,6},{14,10},{7,3},{... | collective-permute-start | bytes 786440 | tf_op jit(solution)/shard_map/ppermute | solution.py:18
  7.7 0.0 copy-done.2
  7.7 0.1 slice_bitcast_fusion.7
  7.8 0.1 pad_dynamic-update-slice_fusion.3
  7.9 0.0 copy-start.3
  7.9 0.2 maximum_dynamic-update-slice_fusion.3
  8.1 0.2 maximum_dynamic-update-slice_fusion.2
  8.3 0.2 maximum_dynamic-update-slice_fusion.1
  8.4 0.2 maximum_dynamic-update-slice_fusion
  8.6 0.2 pad_dynamic-update-slice_fusion.2
  8.8 0.4 copy-done.3
  9.2 0.1 slice_bitcast_fusion.2
  9.3 0.0 copy-start.1
  9.3 0.1 pad_dynamic-update-slice_fusion.1
  9.3 0.2 maximum_dynamic-update-slice_fusion.7
  9.5 0.2 maximum_dynamic-update-slice_fusion.6
  9.7 0.2 maximum_dynamic-update-slice_fusion.5
  9.9 0.1 pad_add_fusion
  10.0 0.5 copy-done.1
  10.5 0.7 copy_bitcast_fusion.1.res_ref
  11.2 0.0 collective-permute-done
  11.2 0.4 collective-permute-done.1
  11.6 4.5 %select_maximum_fusion.2 = bf16[6,132,10,128]{3,2,0,1:T(8,128)(2,1)S(1)} fusion(bf16[1,128,8,128]{3,2,0,1:T(8,128)(2,1)} %collective-permute-done.1, bf16[4,128,8,128]{3,2,0,1:T(8,128)(2,1)S(1)} %bitcast_multiply_fusion, bf16[1,128,8,128]{3,2,0,1:T(8,128)(2,1)} %collective-permute-done), kind=kLoop, calls=%fused_computation.23 | loop fusion | flops 19261440 | bytes 3600384 | tf_op jit(solution)/shard_map/concatenate | solution.py:19
  16.1 0.9 %fusion.18 = (bf16[6,132,8,128]{3,2,0,1:T(8,128)(2,1)S(1)}, bf16[6,132,8,128]{3,2,0,1:T(8,128)(2,1)S(1)}, bf16[6,132,8,128]{3,2,0,1:T(8,128)(2,1)S(1)}) fusion(bf16[6,132,10,128]{3,2,0,1:T(8,128)(2,1)S(1)} %select_maximum_fusion.2), kind=kLoop, calls=%fused_computation.77 | loop fusion | bytes 9732096 | tf_op jit(solution)/shard_map/slice | solution.py:44
  17.0 2.5 %copy_bitcast_fusion.xs_ref = bf16[6,1056,384]{2,1,0:T(8,128)(2,1)} fusion(bf16[6,132,8,128]{3,2,0,1:T(8,128)(2,1)S(1)} %get-tuple-element.10, bf16[6,132,8,128]{3,2,0,1:T(8,128)(2,1)S(1)} %get-tuple-element.9, bf16[6,132,8,128]{3,2,0,1:T(8,128)(2,1)S(1)} %get-tuple-element.8), kind=kLoop, calls=%fused_computation.17 | loop fusion | flops 14598144 | bytes 9732096 | tf_op jit(solution)/shard_map/reshape | solution.py:47
  19.5 13.1 %shard_map.46.res_ref = bf16[4,1024,128]{2,1,0:T(8,128)(2,1)S(1)} custom-call(s32[5]{0:T(128)S(1)} %get-tuple-element.26.scalars_ref, bf16[6,1056,384]{2,1,0:T(8,128)(2,1)} %copy_bitcast_fusion.xs_ref, bf16[15,384,128]{2,1,0:T(8,128)(2,1)S(1)} %bitcast.77, bf16[4,1024,128]{2,1,0:T(8,128)(2,1)S(1)} %copy_bitcast_fusion.1.res_ref), custom_call_target="tpu_custom_call" | custom-call | flops 6228541440 | bytes 8437760 | tf_op jit(solution)/shard_map/pallas_call | solution.py:54
  32.6 6.7 %collective-permute-start.2 = (bf16[1,128,8,128]{3,2,1,0:T(8,128)(2,1)S(1)}, bf16[1,128,8,128]{3,2,1,0:T(8,128)(2,1)S(1)}, u32[]{:S(2)}, u32[]{:S(2)}) collective-permute-start(bf16[1,128,8,128]{3,2,1,0:T(8,128)(2,1)S(1)} %get-tuple-element.21), channel_id=1, source_target_pairs={{0,4},{4,8},{8,12},{1,5},{5,9},{9,13},{2,6},{6,10},{10,14},{3,7},{... | collective-permute-start | bytes 786440 | tf_op jit(solution)/shard_map/ppermute | solution.py:15
  39.3 1.3 %collective-permute-start.3 = (bf16[1,128,8,128]{3,2,1,0:T(8,128)(2,1)S(1)}, bf16[1,128,8,128]{3,2,1,0:T(8,128)(2,1)S(1)}, u32[]{:S(2)}, u32[]{:S(2)}) collective-permute-start(bf16[1,128,8,128]{3,2,1,0:T(8,128)(2,1)S(1)} %get-tuple-element.22), channel_id=1, source_target_pairs={{4,0},{8,4},{12,8},{5,1},{9,5},{13,9},{6,2},{10,6},{14,10},{7,3},{... | collective-permute-start | bytes 786440 | tf_op jit(solution)/shard_map/ppermute | solution.py:18
  40.6 0.2 maximum_dynamic-update-slice_fusion.4
  40.8 0.2 pad_dynamic-update-slice_fusion
  41.0 0.0 collective-permute-done.2
  41.0 1.7 %collective-permute-done.3 = bf16[1,128,8,128]{3,2,1,0:T(8,128)(2,1)S(1)} collective-permute-done((bf16[1,128,8,128]{3,2,1,0:T(8,128)(2,1)S(1)}, bf16[1,128,8,128]{3,2,1,0:T(8,128)(2,1)S(1)}, u32[]{:S(2)}, u32[]{:S(2)}) %collective-permute-start.3) | collective-permute-done | bytes 262176 | tf_op jit(solution)/shard_map/ppermute | solution.py:18
  42.7 2.6 %select_maximum_fusion = bf16[6,144,10,128]{3,2,1,0:T(8,128)(2,1)S(1)} fusion(bf16[1,128,8,128]{3,2,1,0:T(8,128)(2,1)S(1)} %collective-permute-done.3, bf16[4,128,8,128]{3,2,1,0:T(8,128)(2,1)S(1)} %bitcast.71, bf16[1,128,8,128]{3,2,1,0:T(8,128)(2,1)S(1)} %collective-permute-done.2), kind=kLoop, calls=%fused_computation.18 | loop fusion | flops 21012480 | bytes 3784704 | tf_op jit(solution)/shard_map/concatenate | solution.py:19
  45.3 0.9 %fusion.17 = (bf16[6,144,8,128]{3,2,1,0:T(8,128)(2,1)S(1)}, bf16[6,144,8,128]{3,2,1,0:T(8,128)(2,1)S(1)}, bf16[6,144,8,128]{3,2,1,0:T(8,128)(2,1)S(1)}) fusion(bf16[6,144,10,128]{3,2,1,0:T(8,128)(2,1)S(1)} %select_maximum_fusion), kind=kLoop, calls=%fused_computation.76 | loop fusion | bytes 10616832 | tf_op jit(solution)/shard_map/slice | solution.py:44
  46.3 3.0 %maximum_bitcast_fusion.xs_ref = bf16[6,1152,384]{2,1,0:T(8,128)(2,1)} fusion(bf16[6,144,8,128]{3,2,1,0:T(8,128)(2,1)S(1)} %get-tuple-element.7, bf16[6,144,8,128]{3,2,1,0:T(8,128)(2,1)S(1)} %get-tuple-element.6, bf16[6,144,8,128]{3,2,1,0:T(8,128)(2,1)S(1)} %get-tuple-element.5), kind=kLoop, calls=%fused_computation.15 | loop fusion | flops 15925248 | bytes 10616832 | tf_op jit(solution)/shard_map/reshape | solution.py:47
  49.2 5.9 %shard_map.48 = bf16[4,256,128]{2,1,0:T(8,128)(2,1)S(1)} custom-call(s32[5]{0:T(128)S(1)} %get-tuple-element.27.scalars_ref, bf16[6,1152,384]{2,1,0:T(8,128)(2,1)} %maximum_bitcast_fusion.xs_ref, bf16[15,384,128]{2,1,0:T(8,128)(2,1)S(1)} %bitcast.72, bf16[4,1024,128]{2,1,0:T(8,128)(2,1)S(1)} %shard_map.46.res_ref), custom_call_target="tpu_custom_call" | custom-call | flops 1509949440 | bytes 3768320 | tf_op jit(solution)/shard_map/pallas_call | solution.py:116
  55.1 4.5 %collective-permute-start.4 = (bf16[4,256,128]{2,1,0:T(8,128)(2,1)S(1)}, bf16[4,256,128]{2,1,0:T(8,128)(2,1)}, u32[]{:S(2)}, u32[]{:S(2)}) collective-permute-start(bf16[4,256,128]{2,1,0:T(8,128)(2,1)S(1)} %shard_map.48), channel_id=1, source_target_pairs={{0,4},{4,8},{8,12},{12,0},{1,5},{5,9},{9,13},{13,1},{2,6},{6,10},{... | collective-permute-start | bytes 786440 | tf_op jit(solution)/shard_map/ppermute | solution.py:171
  59.6 5.9 %shard_map.49 = bf16[4,256,128]{2,1,0:T(8,128)(2,1)S(1)} custom-call(s32[5]{0:T(128)S(1)} %get-tuple-element.28.scalars_ref, bf16[6,1152,384]{2,1,0:T(8,128)(2,1)} %maximum_bitcast_fusion.xs_ref, bf16[15,384,128]{2,1,0:T(8,128)(2,1)S(1)} %bitcast.73, bf16[4,1024,128]{2,1,0:T(8,128)(2,1)S(1)} %shard_map.46.res_ref), custom_call_target="tpu_custom_call" | custom-call | flops 1509949440 | bytes 3768320 | tf_op jit(solution)/shard_map/pallas_call | solution.py:116
  65.5 0.1 collective-permute-start.5
  65.5 5.9 %shard_map.50 = bf16[4,256,128]{2,1,0:T(8,128)(2,1)S(1)} custom-call(s32[5]{0:T(128)S(1)} %get-tuple-element.29.scalars_ref, bf16[6,1152,384]{2,1,0:T(8,128)(2,1)} %maximum_bitcast_fusion.xs_ref, bf16[15,384,128]{2,1,0:T(8,128)(2,1)S(1)} %bitcast.74, bf16[4,1024,128]{2,1,0:T(8,128)(2,1)S(1)} %shard_map.46.res_ref), custom_call_target="tpu_custom_call" | custom-call | flops 1509949440 | bytes 3768320 | tf_op jit(solution)/shard_map/pallas_call | solution.py:116
  71.4 1.4 %collective-permute-start.6 = (bf16[4,256,128]{2,1,0:T(8,128)(2,1)S(1)}, bf16[4,256,128]{2,1,0:T(8,128)(2,1)}, u32[]{:S(2)}, u32[]{:S(2)}) collective-permute-start(bf16[4,256,128]{2,1,0:T(8,128)(2,1)S(1)} %shard_map.50), channel_id=1, source_target_pairs={{0,12},{4,0},{8,4},{12,8},{1,13},{5,1},{9,5},{13,9},{2,14},{6,2},{... | collective-permute-start | bytes 786440 | tf_op jit(solution)/shard_map/ppermute | solution.py:171
  72.8 0.1 broadcast_in_dim.20
  72.9 0.1 broadcast_in_dim.21
  73.0 5.9 %shard_map.47 = bf16[4,256,128]{2,1,0:T(8,128)(2,1)S(1)} custom-call(s32[5]{0:T(128)S(1)} %get-tuple-element.25.scalars_ref, bf16[6,1152,384]{2,1,0:T(8,128)(2,1)} %maximum_bitcast_fusion.xs_ref, bf16[15,384,128]{2,1,0:T(8,128)(2,1)S(1)} %bitcast.75, bf16[4,1024,128]{2,1,0:T(8,128)(2,1)S(1)} %shard_map.46.res_ref), custom_call_target="tpu_custom_call" | custom-call | flops 1509949440 | bytes 3768320 | tf_op jit(solution)/shard_map/pallas_call | solution.py:116
  78.9 0.0 collective-permute-done.4
  78.9 0.0 collective-permute-done.5
  78.9 0.0 collective-permute-done.6
  78.9 1.2 %pad_maximum_fusion.1 = bf16[4,4,256,128]{3,2,1,0:T(8,128)(2,1)S(1)} fusion(bf16[1,4,256,128]{3,2,1,0:T(8,128)(2,1)} %bitcast.28, bf16[1,4,256,128]{3,2,1,0:T(8,128)(2,1)} %bitcast.26, bf16[1,4,256,128]{3,2,1,0:T(8,128)(2,1)} %bitcast.24, bf16[1,4,256,128]{3,2,1,0:T(8,128)(2,1)S(1)} %bitcast.76), kind=kLoop, calls=%fused_computation.28 | loop fusion | flops 1572864 | bytes 2097152 | tf_op jit(solution)/shard_map/stack | solution.py:173
  80.1 0.7 gather_fusion
  80.9 1.3 %fusion.12 = bf16[1,32,16,8,128]{4,3,2,1,0:T(8,128)(2,1)} fusion(bf16[16,32,8,128]{3,2,1,0:T(8,128)(2,1)S(1)} %bitcast.78, pred[16]{0:T(512)(128)(4,1)S(1)} %broadcast_in_dim.21), kind=kLoop, calls=%fused_computation.31 | loop fusion | flops 524288 | bytes 2097168 | tf_op jit(solution)/shard_map/broadcast_in_dim | solution.py:177
  (5 shorter events, 0.1 us)
Async XLA Ops:
  0.0 0.7 copy-start
  0.0 7.7 %copy-start.2 = (bf16[5,3,5,64,64]{4,3,2,1,0:T(8,128)(2,1)S(1)}, bf16[5,3,5,64,64]{4,3,2,1,0:T(8,128)(2,1)}, u32[]{:S(2)}) copy-start(bf16[5,3,5,64,64]{4,3,2,1,0:T(8,128)(2,1)} %param.6) | copy-start | bytes 1843204
  3.3 7.9 %collective-permute-start = (bf16[1,128,8,128]{3,2,0,1:T(8,128)(2,1)}, bf16[1,128,8,128]{3,2,0,1:T(8,128)(2,1)}, u32[]{:S(2)}, u32[]{:S(2)}) collective-permute-start(bf16[1,128,8,128]{3,2,0,1:T(8,128)(2,1)} %get-tuple-element.23), channel_id=1, source_target_pairs={{0,4},{4,8},{8,12},{1,5},{5,9},{9,13},{2,6},{6,10},{10,14},{3,7},{... | collective-permute-start | bytes 786440 | tf_op jit(solution)/shard_map/ppermute | solution.py:15
  6.4 5.2 %collective-permute-start.1 = (bf16[1,128,8,128]{3,2,0,1:T(8,128)(2,1)}, bf16[1,128,8,128]{3,2,0,1:T(8,128)(2,1)}, u32[]{:S(2)}, u32[]{:S(2)}) collective-permute-start(bf16[1,128,8,128]{3,2,0,1:T(8,128)(2,1)} %get-tuple-element.24), channel_id=1, source_target_pairs={{4,0},{8,4},{12,8},{5,1},{9,5},{13,9},{6,2},{10,6},{14,10},{7,3},{... | collective-permute-start | bytes 786440 | tf_op jit(solution)/shard_map/ppermute | solution.py:18
  7.9 1.3 %copy-start.3 = (bf16[5,3,5,64,64]{4,3,2,1,0:T(8,128)(2,1)S(1)}, bf16[5,3,5,64,64]{4,3,2,1,0:T(8,128)(2,1)}, u32[]{:S(2)}) copy-start(bf16[5,3,5,64,64]{4,3,2,1,0:T(8,128)(2,1)} %param.7) | copy-start | bytes 1843204
  9.3 1.2 %copy-start.1 = (bf16[1,128,4,8,128]{4,3,2,1,0:T(8,128)(2,1)S(1)}, bf16[1,128,4,8,128]{4,3,2,1,0:T(8,128)(2,1)}, u32[]{:S(2)}) copy-start(bf16[1,128,4,8,128]{4,3,2,1,0:T(8,128)(2,1)} %param.4) | copy-start | bytes 3145732
  32.6 8.3 %collective-permute-start.2 = (bf16[1,128,8,128]{3,2,1,0:T(8,128)(2,1)S(1)}, bf16[1,128,8,128]{3,2,1,0:T(8,128)(2,1)S(1)}, u32[]{:S(2)}, u32[]{:S(2)}) collective-permute-start(bf16[1,128,8,128]{3,2,1,0:T(8,128)(2,1)S(1)} %get-tuple-element.21), channel_id=1, source_target_pairs={{0,4},{4,8},{8,12},{1,5},{5,9},{9,13},{2,6},{6,10},{10,14},{3,7},{... | collective-permute-start | bytes 786440 | tf_op jit(solution)/shard_map/ppermute | solution.py:15
  39.3 3.4 %collective-permute-start.3 = (bf16[1,128,8,128]{3,2,1,0:T(8,128)(2,1)S(1)}, bf16[1,128,8,128]{3,2,1,0:T(8,128)(2,1)S(1)}, u32[]{:S(2)}, u32[]{:S(2)}) collective-permute-start(bf16[1,128,8,128]{3,2,1,0:T(8,128)(2,1)S(1)} %get-tuple-element.22), channel_id=1, source_target_pairs={{4,0},{8,4},{12,8},{5,1},{9,5},{13,9},{6,2},{10,6},{14,10},{7,3},{... | collective-permute-start | bytes 786440 | tf_op jit(solution)/shard_map/ppermute | solution.py:18
  55.1 23.7 %collective-permute-start.4 = (bf16[4,256,128]{2,1,0:T(8,128)(2,1)S(1)}, bf16[4,256,128]{2,1,0:T(8,128)(2,1)}, u32[]{:S(2)}, u32[]{:S(2)}) collective-permute-start(bf16[4,256,128]{2,1,0:T(8,128)(2,1)S(1)} %shard_map.48), channel_id=1, source_target_pairs={{0,4},{4,8},{8,12},{12,0},{1,5},{5,9},{9,13},{13,1},{2,6},{6,10},{... | collective-permute-start | bytes 786440 | tf_op jit(solution)/shard_map/ppermute | solution.py:171
  65.5 13.4 %collective-permute-start.5 = (bf16[4,256,128]{2,1,0:T(8,128)(2,1)S(1)}, bf16[4,256,128]{2,1,0:T(8,128)(2,1)}, u32[]{:S(2)}, u32[]{:S(2)}) collective-permute-start(bf16[4,256,128]{2,1,0:T(8,128)(2,1)S(1)} %shard_map.49), channel_id=1, source_target_pairs={{0,8},{4,12},{8,0},{12,4},{1,9},{5,13},{9,1},{13,5},{2,10},{6,14},... | collective-permute-start | bytes 786440 | tf_op jit(solution)/shard_map/ppermute | solution.py:171
  71.4 7.5 %collective-permute-start.6 = (bf16[4,256,128]{2,1,0:T(8,128)(2,1)S(1)}, bf16[4,256,128]{2,1,0:T(8,128)(2,1)}, u32[]{:S(2)}, u32[]{:S(2)}) collective-permute-start(bf16[4,256,128]{2,1,0:T(8,128)(2,1)S(1)} %shard_map.50), channel_id=1, source_target_pairs={{0,12},{4,0},{8,4},{12,8},{1,13},{5,1},{9,5},{13,9},{2,14},{6,2},{... | collective-permute-start | bytes 786440 | tf_op jit(solution)/shard_map/ppermute | solution.py:171

commit v4 on v3

--- a/solution.py
+++ b/solution.py
@@ -162,10 +162,11 @@
     xs2 = stack_time(edged, 4)
     flat2 = hidden.reshape(shot_local, receivers * pairs, lanes)
     span = receivers // count
+    whole = spread_call(xs2, second_pairs, flat2, chosen, 4, pairs)
     arrived = []
-    for shift in list(range(1, count)) + [0]:
+    for shift in range(count):
         target = lax.rem(me + shift, count)
-        piece = conv_call(xs2, second_pairs, flat2, chosen, 4, pairs, target, span * pairs)
+        piece = lax.dynamic_slice_in_dim(whole, target * span * pairs, span * pairs, axis=1)
         if shift:
             pairs_list = [(i, (i + shift) % count) for i in range(count)]
             piece = lax.ppermute(piece, "shot", pairs_list)

time: 82.6 us -> 80.7 us (0.977)
  waiting for transfers between devices: 2.14 us -> 12.4 us
  Pallas kernels: 36.5 us -> 27.1 us
  other arithmetic: 19.1 us -> 17 us
    pallas_call x4 -> x0, Pallas kernels: 23.4 us -> none  [conv_call(): pl.pallas_call(functools.partial(conv_kernel, dilation=dilation, pairs=pa...]
    pallas_call x1 -> x2, Pallas kernels: 13.1 us -> 27.1 us  [spread_call(): pl.pallas_call(functools.partial(spread_kernel, dilation=dilation, pairs=...]
    ppermute x3, waiting for transfers between devices: 0.01 us -> 9.99 us  [body(): piece = lax.ppermute(piece, 'shot', pairs_list)]
    another operation x1, other arithmetic: 1.24 us -> 0.13 us  [body(): jnp.stack([piece for _, piece in sorted(arrived, key=lambda t: t[0])])]
    concatenate x2, other arithmetic: 7.12 us -> 6.12 us  [extended(): return jnp.concatenate([low, block, high], axis=dim)]
  transfers between devices with their start and end apart: 7 -> 7, of which waited for: 2 -> 4; matrix products, arithmetic and copies ran while one was open for 4% -> 4% of each run, Pallas kernels for 21% -> 0%
where the time goes in v4:
time: 80.7 us; the launch traced here: 80.4 us
  Pallas kernels  27.1 us (34%)
  starting transfers between devices  17.6 us (22%)
  other arithmetic  17 us (21%)
  waiting for transfers between devices  12.4 us (15%)
  local copies, waits for them, and re-layouts  6.01 us (7%)
    pallas_call x2, Pallas kernels, spread_call(): pl.pallas_call(functools.partial(spread_kernel, dilation=dilation, pairs=...  27.1 us
    ppermute x3, waiting for transfers between devices, body(): piece = lax.ppermute(piece, 'shot', pairs_list)  9.99 us
    ppermute x2, starting transfers between devices, extended(): lax.ppermute(lax.slice_in_dim(block, block.shape[dim] - width, None, axis...  9.08 us
    concatenate x2, other arithmetic, extended(): return jnp.concatenate([low, block, high], axis=dim)  6.12 us
    ppermute x3, starting transfers between devices, body(): piece = lax.ppermute(piece, 'shot', pairs_list)  5.74 us
    reshape x2, other arithmetic, stack_time(): return stacked.reshape(stacked.shape[0], -1, stacked.shape[3])  5.48 us
    ppermute x2, starting transfers between devices, extended(): lax.ppermute(lax.slice_in_dim(block, 0, width, axis=dim), axis, backward)  2.76 us
    ppermute x2, waiting for transfers between devices, extended(): lax.ppermute(lax.slice_in_dim(block, 0, width, axis=dim), axis, backward)  2.39 us
  transfers between devices with their start and end apart: 7, of which 4 were waited for; matrix products, arithmetic and copies ran while one was open for 4% of the time, Pallas kernels for 0%

profile of v4, /device:TPU:0, one launch (start us, length us, event | category | flops | bytes accessed | tf_op | source)
XLA Modules:
  0.0 80.4 jit_solution(3744921361195731342)
XLA Ops:
  0.0 0.0 copy-start
  0.0 0.0 copy-start.2
  0.0 0.7 copy-done
  0.7 0.1 fusion.14
  0.7 1.7 %bitcast_multiply_fusion = bf16[4,128,8,128]{3,2,0,1:T(8,128)(2,1)S(1)} fusion(bf16[1,128,4,8,128]{4,3,2,1,0:T(8,128)(2,1)} %param.4, bf16[4,128]{0,1:T(8,128)(2,1)S(1)} %fusion.13), kind=kLoop, calls=%fused_computation.29 | loop fusion | flops 524288 | bytes 2098176 | tf_op jit(solution)/shard_map/mul | solution.py:155
  2.5 2.4 %collective-permute-start = (bf16[1,128,8,128]{3,2,0,1:T(8,128)(2,1)S(1)}, bf16[1,128,8,128]{3,2,0,1:T(8,128)(2,1)S(1)}, u32[]{:S(2)}, u32[]{:S(2)}) collective-permute-start(bf16[1,128,8,128]{3,2,0,1:T(8,128)(2,1)S(1)} %get-tuple-element.27), channel_id=1, source_target_pairs={{0,4},{4,8},{8,12},{1,5},{5,9},{9,13},{2,6},{6,10},{10,14},{3,7},{... | collective-permute-start | bytes 786440 | tf_op jit(solution)/shard_map/ppermute | solution.py:15
  5.0 1.3 %collective-permute-start.1 = (bf16[1,128,8,128]{3,2,0,1:T(8,128)(2,1)S(1)}, bf16[1,128,8,128]{3,2,0,1:T(8,128)(2,1)S(1)}, u32[]{:S(2)}, u32[]{:S(2)}) collective-permute-start(bf16[1,128,8,128]{3,2,0,1:T(8,128)(2,1)S(1)} %get-tuple-element.28), channel_id=1, source_target_pairs={{4,0},{8,4},{12,8},{5,1},{9,5},{13,9},{6,2},{10,6},{14,10},{7,3},{... | collective-permute-start | bytes 786440 | tf_op jit(solution)/shard_map/ppermute | solution.py:18
  6.3 0.0 copy-done.2
  6.3 0.1 slice_bitcast_fusion.7
  6.4 0.1 pad_dynamic-update-slice_fusion.3
  6.4 0.0 copy-start.3
  6.5 0.2 maximum_dynamic-update-slice_fusion.3
  6.6 0.2 maximum_dynamic-update-slice_fusion.2
  6.8 0.2 maximum_dynamic-update-slice_fusion.1
  7.0 0.2 maximum_dynamic-update-slice_fusion
  7.2 0.2 pad_dynamic-update-slice_fusion.2
  7.3 0.1 pad_add_fusion.scalars_ref
  7.4 0.3 copy-done.3
  7.7 0.0 copy-start.1
  7.7 0.1 slice_bitcast_fusion.2
  7.8 0.1 pad_dynamic-update-slice_fusion.1
  7.9 0.2 maximum_dynamic-update-slice_fusion.7
  8.1 0.2 maximum_dynamic-update-slice_fusion.6
  8.3 0.7 copy-done.1
  9.0 0.7 copy_bitcast_fusion.1.res_ref
  9.7 0.0 collective-permute-done
  9.7 0.8 %collective-permute-done.1 = bf16[1,128,8,128]{3,2,0,1:T(8,128)(2,1)S(1)} collective-permute-done((bf16[1,128,8,128]{3,2,0,1:T(8,128)(2,1)S(1)}, bf16[1,128,8,128]{3,2,0,1:T(8,128)(2,1)S(1)}, u32[]{:S(2)}, u32[]{:S(2)}) %collective-permute-start.1) | collective-permute-done | bytes 262176 | tf_op jit(solution)/shard_map/ppermute | solution.py:18
  10.5 3.5 %select_maximum_fusion.2 = bf16[6,132,10,128]{3,2,0,1:T(8,128)(2,1)S(1)} fusion(bf16[1,128,8,128]{3,2,0,1:T(8,128)(2,1)S(1)} %collective-permute-done.1, bf16[4,128,8,128]{3,2,0,1:T(8,128)(2,1)S(1)} %bitcast_multiply_fusion, bf16[1,128,8,128]{3,2,0,1:T(8,128)(2,1)S(1)} %collective-permute-done), kind=kLoop, calls=%fused_computation.23 | loop fusion | flops 19261440 | bytes 3600384 | tf_op jit(solution)/shard_map/concatenate | solution.py:19
  14.0 0.9 %fusion.19 = (bf16[6,132,8,128]{3,2,0,1:T(8,128)(2,1)S(1)}, bf16[6,132,8,128]{3,2,0,1:T(8,128)(2,1)S(1)}, bf16[6,132,8,128]{3,2,0,1:T(8,128)(2,1)S(1)}) fusion(bf16[6,132,10,128]{3,2,0,1:T(8,128)(2,1)S(1)} %select_maximum_fusion.2), kind=kLoop, calls=%fused_computation.78 | loop fusion | bytes 9732096 | tf_op jit(solution)/shard_map/slice | solution.py:44
  14.9 2.5 %copy_bitcast_fusion.xs_ref = bf16[6,1056,384]{2,1,0:T(8,128)(2,1)} fusion(bf16[6,132,8,128]{3,2,0,1:T(8,128)(2,1)S(1)} %get-tuple-element.10, bf16[6,132,8,128]{3,2,0,1:T(8,128)(2,1)S(1)} %get-tuple-element.9, bf16[6,132,8,128]{3,2,0,1:T(8,128)(2,1)S(1)} %get-tuple-element.8), kind=kLoop, calls=%fused_computation.17 | loop fusion | flops 14598144 | bytes 9732096 | tf_op jit(solution)/shard_map/reshape | solution.py:47
  17.4 13.1 %shard_map.46.res_ref = bf16[4,1024,128]{2,1,0:T(8,128)(2,1)S(1)} custom-call(s32[5]{0:T(128)S(1)} %pad_add_fusion.scalars_ref, bf16[6,1056,384]{2,1,0:T(8,128)(2,1)} %copy_bitcast_fusion.xs_ref, bf16[15,384,128]{2,1,0:T(8,128)(2,1)S(1)} %bitcast.69, bf16[4,1024,128]{2,1,0:T(8,128)(2,1)S(1)} %copy_bitcast_fusion.1.res_ref), custom_call_target="tpu_custom_call" | custom-call | flops 6228541440 | bytes 8437760 | tf_op jit(solution)/shard_map/pallas_call | solution.py:54
  30.5 0.8 %slice_bitcast_fusion.1 = (bf16[1,128,8,128]{3,2,1,0:T(8,128)(2,1)}, bf16[1,128,8,128]{3,2,1,0:T(8,128)(2,1)}) fusion(bf16[4,1024,128]{2,1,0:T(8,128)(2,1)S(1)} %shard_map.46.res_ref), kind=kLoop, calls=%fused_computation.34 | loop fusion | bytes 1048576 | tf_op jit(solution)/shard_map/slice | solution.py:16
  31.3 6.7 %collective-permute-start.2 = (bf16[1,128,8,128]{3,2,1,0:T(8,128)(2,1)}, bf16[1,128,8,128]{3,2,1,0:T(8,128)(2,1)S(1)}, u32[]{:S(2)}, u32[]{:S(2)}) collective-permute-start(bf16[1,128,8,128]{3,2,1,0:T(8,128)(2,1)} %get-tuple-element.25), channel_id=1, source_target_pairs={{0,4},{4,8},{8,12},{1,5},{5,9},{9,13},{2,6},{6,10},{10,14},{3,7},{... | collective-permute-start | bytes 786440 | tf_op jit(solution)/shard_map/ppermute | solution.py:15
  38.0 1.5 %collective-permute-start.3 = (bf16[1,128,8,128]{3,2,1,0:T(8,128)(2,1)}, bf16[1,128,8,128]{3,2,1,0:T(8,128)(2,1)S(1)}, u32[]{:S(2)}, u32[]{:S(2)}) collective-permute-start(bf16[1,128,8,128]{3,2,1,0:T(8,128)(2,1)} %get-tuple-element.26), channel_id=1, source_target_pairs={{4,0},{8,4},{12,8},{5,1},{9,5},{13,9},{6,2},{10,6},{14,10},{7,3},{... | collective-permute-start | bytes 786440 | tf_op jit(solution)/shard_map/ppermute | solution.py:18
  39.5 0.2 maximum_dynamic-update-slice_fusion.5
  39.7 0.2 maximum_dynamic-update-slice_fusion.4
  39.9 0.2 pad_dynamic-update-slice_fusion
  40.0 0.0 collective-permute-done.2
  40.0 1.6 %collective-permute-done.3 = bf16[1,128,8,128]{3,2,1,0:T(8,128)(2,1)S(1)} collective-permute-done((bf16[1,128,8,128]{3,2,1,0:T(8,128)(2,1)}, bf16[1,128,8,128]{3,2,1,0:T(8,128)(2,1)S(1)}, u32[]{:S(2)}, u32[]{:S(2)}) %collective-permute-start.3) | collective-permute-done | bytes 262176 | tf_op jit(solution)/shard_map/ppermute | solution.py:18
  41.6 2.6 %select_maximum_fusion = bf16[6,144,10,128]{3,2,1,0:T(8,128)(2,1)S(1)} fusion(bf16[1,128,8,128]{3,2,1,0:T(8,128)(2,1)S(1)} %collective-permute-done.3, bf16[4,128,8,128]{3,2,1,0:T(8,128)(2,1)S(1)} %bitcast.68, bf16[1,128,8,128]{3,2,1,0:T(8,128)(2,1)S(1)} %collective-permute-done.2), kind=kLoop, calls=%fused_computation.18 | loop fusion | flops 21012480 | bytes 3784704 | tf_op jit(solution)/shard_map/concatenate | solution.py:19
  44.2 0.9 %fusion.18 = (bf16[6,144,8,128]{3,2,1,0:T(8,128)(2,1)S(1)}, bf16[6,144,8,128]{3,2,1,0:T(8,128)(2,1)S(1)}, bf16[6,144,8,128]{3,2,1,0:T(8,128)(2,1)S(1)}) fusion(bf16[6,144,10,128]{3,2,1,0:T(8,128)(2,1)S(1)} %select_maximum_fusion), kind=kLoop, calls=%fused_computation.77 | loop fusion | bytes 10616832 | tf_op jit(solution)/shard_map/slice | solution.py:44
  45.2 3.0 %maximum_bitcast_fusion.xs_ref = bf16[6,1152,384]{2,1,0:T(8,128)(2,1)} fusion(bf16[6,144,8,128]{3,2,1,0:T(8,128)(2,1)S(1)} %get-tuple-element.7, bf16[6,144,8,128]{3,2,1,0:T(8,128)(2,1)S(1)} %get-tuple-element.6, bf16[6,144,8,128]{3,2,1,0:T(8,128)(2,1)S(1)} %get-tuple-element.5), kind=kLoop, calls=%fused_computation.15 | loop fusion | flops 15925248 | bytes 10616832 | tf_op jit(solution)/shard_map/reshape | solution.py:47
  48.1 14.0 %shard_map.47 = bf16[4,1024,128]{2,1,0:T(8,128)(2,1)S(1)} custom-call(s32[5]{0:T(128)S(1)} %pad_add_fusion.scalars_ref, bf16[6,1152,384]{2,1,0:T(8,128)(2,1)} %maximum_bitcast_fusion.xs_ref, bf16[15,384,128]{2,1,0:T(8,128)(2,1)S(1)} %bitcast.70, bf16[4,1024,128]{2,1,0:T(8,128)(2,1)S(1)} %shard_map.46.res_ref), custom_call_target="tpu_custom_call" | custom-call | flops 6794772480 | bytes 8880128 | tf_op jit(solution)/shard_map/pallas_call | solution.py:54
  62.2 0.1 dynamic-slice_bitcast_fusion
  62.3 4.3 %collective-permute-start.4 = (bf16[4,256,128]{2,1,0:T(8,128)(2,1)S(1)}, bf16[4,256,128]{2,1,0:T(8,128)(2,1)S(1)}, u32[]{:S(2)}, u32[]{:S(2)}) collective-permute-start(bf16[4,256,128]{2,1,0:T(8,128)(2,1)S(1)} %get-tuple-element.24), channel_id=1, source_target_pairs={{0,4},{4,8},{8,12},{12,0},{1,5},{5,9},{9,13},{13,1},{2,6},{6,10},{... | collective-permute-start | bytes 786440 | tf_op jit(solution)/shard_map/ppermute | solution.py:172
  66.6 0.0 collective-permute-start.5
  66.6 1.4 %collective-permute-start.6 = (bf16[4,256,128]{2,1,0:T(8,128)(2,1)S(1)}, bf16[4,256,128]{2,1,0:T(8,128)(2,1)S(1)}, u32[]{:S(2)}, u32[]{:S(2)}) collective-permute-start(bf16[4,256,128]{2,1,0:T(8,128)(2,1)S(1)} %get-tuple-element.22), channel_id=1, source_target_pairs={{0,12},{4,0},{8,4},{12,8},{1,13},{5,1},{9,5},{13,9},{2,14},{6,2},{... | collective-permute-start | bytes 786440 | tf_op jit(solution)/shard_map/ppermute | solution.py:172
  68.0 0.1 broadcast_in_dim.20
  68.1 0.1 broadcast_in_dim.21
  68.2 0.0 collective-permute-done.4
  68.2 6.6 %collective-permute-done.5 = bf16[4,256,128]{2,1,0:T(8,128)(2,1)S(1)} collective-permute-done((bf16[4,256,128]{2,1,0:T(8,128)(2,1)S(1)}, bf16[4,256,128]{2,1,0:T(8,128)(2,1)S(1)}, u32[]{:S(2)}, u32[]{:S(2)}) %collective-permute-start.5) | collective-permute-done | bytes 262176 | tf_op jit(solution)/shard_map/ppermute | solution.py:172
  74.9 3.3 %collective-permute-done.6 = bf16[4,256,128]{2,1,0:T(8,128)(2,1)S(1)} collective-permute-done((bf16[4,256,128]{2,1,0:T(8,128)(2,1)S(1)}, bf16[4,256,128]{2,1,0:T(8,128)(2,1)S(1)}, u32[]{:S(2)}, u32[]{:S(2)}) %collective-permute-start.6) | collective-permute-done | bytes 262176 | tf_op jit(solution)/shard_map/ppermute | solution.py:172
  78.2 0.1 pad_maximum_fusion.1
  78.4 0.7 gather_fusion
  79.1 1.3 %fusion.12 = bf16[1,32,16,8,128]{4,3,2,1,0:T(8,128)(2,1)} fusion(bf16[16,32,8,128]{3,2,1,0:T(8,128)(2,1)S(1)} %bitcast.71, pred[16]{0:T(512)(128)(4,1)S(1)} %broadcast_in_dim.21), kind=kLoop, calls=%fused_computation.31 | loop fusion | flops 524288 | bytes 2097168 | tf_op jit(solution)/shard_map/broadcast_in_dim | solution.py:178
  (5 shorter events, 0.1 us)
Async XLA Ops:
  0.0 0.7 copy-start
  0.0 6.3 %copy-start.2 = (bf16[5,3,5,64,64]{4,3,2,1,0:T(8,128)(2,1)S(1)}, bf16[5,3,5,64,64]{4,3,2,1,0:T(8,128)(2,1)}, u32[]{:S(2)}) copy-start(bf16[5,3,5,64,64]{4,3,2,1,0:T(8,128)(2,1)} %param.6) | copy-start | bytes 1843204
  2.5 7.1 %collective-permute-start = (bf16[1,128,8,128]{3,2,0,1:T(8,128)(2,1)S(1)}, bf16[1,128,8,128]{3,2,0,1:T(8,128)(2,1)S(1)}, u32[]{:S(2)}, u32[]{:S(2)}) collective-permute-start(bf16[1,128,8,128]{3,2,0,1:T(8,128)(2,1)S(1)} %get-tuple-element.27), channel_id=1, source_target_pairs={{0,4},{4,8},{8,12},{1,5},{5,9},{9,13},{2,6},{6,10},{10,14},{3,7},{... | collective-permute-start | bytes 786440 | tf_op jit(solution)/shard_map/ppermute | solution.py:15
  5.0 5.5 %collective-permute-start.1 = (bf16[1,128,8,128]{3,2,0,1:T(8,128)(2,1)S(1)}, bf16[1,128,8,128]{3,2,0,1:T(8,128)(2,1)S(1)}, u32[]{:S(2)}, u32[]{:S(2)}) collective-permute-start(bf16[1,128,8,128]{3,2,0,1:T(8,128)(2,1)S(1)} %get-tuple-element.28), channel_id=1, source_target_pairs={{4,0},{8,4},{12,8},{5,1},{9,5},{13,9},{6,2},{10,6},{14,10},{7,3},{... | collective-permute-start | bytes 786440 | tf_op jit(solution)/shard_map/ppermute | solution.py:18
  6.4 1.3 %copy-start.3 = (bf16[5,3,5,64,64]{4,3,2,1,0:T(8,128)(2,1)S(1)}, bf16[5,3,5,64,64]{4,3,2,1,0:T(8,128)(2,1)}, u32[]{:S(2)}) copy-start(bf16[5,3,5,64,64]{4,3,2,1,0:T(8,128)(2,1)} %param.7) | copy-start | bytes 1843204
  7.7 1.2 %copy-start.1 = (bf16[1,128,4,8,128]{4,3,2,1,0:T(8,128)(2,1)S(1)}, bf16[1,128,4,8,128]{4,3,2,1,0:T(8,128)(2,1)}, u32[]{:S(2)}) copy-start(bf16[1,128,4,8,128]{4,3,2,1,0:T(8,128)(2,1)} %param.4) | copy-start | bytes 3145732
  31.3 8.7 %collective-permute-start.2 = (bf16[1,128,8,128]{3,2,1,0:T(8,128)(2,1)}, bf16[1,128,8,128]{3,2,1,0:T(8,128)(2,1)S(1)}, u32[]{:S(2)}, u32[]{:S(2)}) collective-permute-start(bf16[1,128,8,128]{3,2,1,0:T(8,128)(2,1)} %get-tuple-element.25), channel_id=1, source_target_pairs={{0,4},{4,8},{8,12},{1,5},{5,9},{9,13},{2,6},{6,10},{10,14},{3,7},{... | collective-permute-start | bytes 786440 | tf_op jit(solution)/shard_map/ppermute | solution.py:15
  38.0 3.6 %collective-permute-start.3 = (bf16[1,128,8,128]{3,2,1,0:T(8,128)(2,1)}, bf16[1,128,8,128]{3,2,1,0:T(8,128)(2,1)S(1)}, u32[]{:S(2)}, u32[]{:S(2)}) collective-permute-start(bf16[1,128,8,128]{3,2,1,0:T(8,128)(2,1)} %get-tuple-element.26), channel_id=1, source_target_pairs={{4,0},{8,4},{12,8},{5,1},{9,5},{13,9},{6,2},{10,6},{14,10},{7,3},{... | collective-permute-start | bytes 786440 | tf_op jit(solution)/shard_map/ppermute | solution.py:18
  62.3 6.0 %collective-permute-start.4 = (bf16[4,256,128]{2,1,0:T(8,128)(2,1)S(1)}, bf16[4,256,128]{2,1,0:T(8,128)(2,1)S(1)}, u32[]{:S(2)}, u32[]{:S(2)}) collective-permute-start(bf16[4,256,128]{2,1,0:T(8,128)(2,1)S(1)} %get-tuple-element.24), channel_id=1, source_target_pairs={{0,4},{4,8},{8,12},{12,0},{1,5},{5,9},{9,13},{13,1},{2,6},{6,10},{... | collective-permute-start | bytes 786440 | tf_op jit(solution)/shard_map/ppermute | solution.py:172
  66.6 8.3 %collective-permute-start.5 = (bf16[4,256,128]{2,1,0:T(8,128)(2,1)S(1)}, bf16[4,256,128]{2,1,0:T(8,128)(2,1)S(1)}, u32[]{:S(2)}, u32[]{:S(2)}) collective-permute-start(bf16[4,256,128]{2,1,0:T(8,128)(2,1)S(1)} %get-tuple-element.23), channel_id=1, source_target_pairs={{0,8},{4,12},{8,0},{12,4},{1,9},{5,13},{9,1},{13,5},{2,10},{6,14},... | collective-permute-start | bytes 786440 | tf_op jit(solution)/shard_map/ppermute | solution.py:172
  66.6 11.6 %collective-permute-start.6 = (bf16[4,256,128]{2,1,0:T(8,128)(2,1)S(1)}, bf16[4,256,128]{2,1,0:T(8,128)(2,1)S(1)}, u32[]{:S(2)}, u32[]{:S(2)}) collective-permute-start(bf16[4,256,128]{2,1,0:T(8,128)(2,1)S(1)} %get-tuple-element.22), channel_id=1, source_target_pairs={{0,12},{4,0},{8,4},{12,8},{1,13},{5,1},{9,5},{13,9},{2,14},{6,2},{... | collective-permute-start | bytes 786440 | tf_op jit(solution)/shard_map/ppermute | solution.py:172

commit v5 on v4

--- a/solution.py
+++ b/solution.py
@@ -76,18 +76,43 @@
 def spread_kernel(scalars_ref, xs_ref, w_ref, res_ref, out_ref, *, dilation, pairs):
     s = pl.program_id(0)
     rows, lanes = out_ref.shape[1:]
+    lhs = jnp.concatenate([xs_ref[s + b] for b in range(3)], axis=1)
+    rhs = jnp.concatenate(
+        [jnp.concatenate([w_ref[a * 3 + b] for a in range(5)], axis=1) for b in range(3)], axis=0
+    )
+    spread = jnp.dot(lhs, rhs, preferred_element_type=jnp.float32)
     total = None
-    for b in range(3):
-        taps = jnp.concatenate([w_ref[a * 3 + b] for a in range(5)], axis=1)
-        spread = jnp.dot(xs_ref[s + b], taps, preferred_element_type=jnp.float32)
-        for a in range(5):
-            part = spread[a * dilation * pairs : a * dilation * pairs + rows, a * lanes : (a + 1) * lanes]
-            total = part if total is None else total + part
+    for a in range(5):
+        part = spread[a * dilation * pairs : a * dilation * pairs + rows, a * lanes : (a + 1) * lanes]
+        total = part if total is None else total + part
     first = scalars_ref[0] * (rows // pairs)
     receiver = first + lax.broadcasted_iota(jnp.int32, (rows, lanes), 0) // pairs
     live = receiver < scalars_ref[1 + s]
     value = res_ref[0].astype(jnp.float32) + jnp.maximum(total, 0.0)
     out_ref[0] = jnp.where(live, value, 0.0).astype(out_ref.dtype)
+
+
+def halos(block, axis):
+    count = lax.axis_size(axis)
+    forward = [(i, i + 1) for i in range(count - 1)]
+    backward = [(target, source) for source, target in forward]
+    low = lax.ppermute(block[-1:], axis, forward)
+    high = lax.ppermute(block[:1], axis, backward)
+    return low, high
+
+
+def stack_flat(inner, low, high, dilation, pairs):
+    volume = jnp.concatenate([low, inner, high], axis=0)
+    rows = volume.shape[1]
+    phase = (jnp.arange(rows, dtype=jnp.int32) % pairs)[None, :, None]
+    blank = jnp.zeros_like(volume[:, :1])
+    before = jnp.concatenate([blank, volume[:, :-1]], axis=1)
+    after = jnp.concatenate([volume[:, 1:], blank], axis=1)
+    before = jnp.where(phase == 0, jnp.zeros_like(before), before)
+    after = jnp.where(phase == pairs - 1, jnp.zeros_like(after), after)
+    stacked = jnp.concatenate([before, volume, after], axis=2)
+    margin = 2 * dilation * pairs
+    return jnp.pad(stacked, ((0, 0), (margin, margin), (0, 0)))
 
 
 def conv_kernel(scalars_ref, xs_ref, w_ref, res_ref, out_ref, acc_ref, *, dilation, pairs):
@@ -153,14 +178,12 @@
     volume = jnp.transpose(features[0], (1, 0, 2, 3))
     alive = jnp.arange(receivers, dtype=jnp.int32)[None, :] < chosen[:, None]
     inputs = volume * alive.astype(volume.dtype)[:, :, None, None]
-    bordered = extended(inputs, "shot", 0, 1)
-    xs1 = stack_time(bordered, 1)
     flat1 = inputs.reshape(shot_local, receivers * pairs, lanes)
-    hidden = spread_call(xs1, first_pairs, flat1, chosen, 1, pairs)
-    hidden = hidden.reshape(shot_local, receivers, pairs, lanes)
-    edged = extended(hidden, "shot", 0, 1)
-    xs2 = stack_time(edged, 4)
-    flat2 = hidden.reshape(shot_local, receivers * pairs, lanes)
+    low1, high1 = halos(flat1, "shot")
+    xs1 = stack_flat(flat1, low1, high1, 1, pairs)
+    flat2 = spread_call(xs1, first_pairs, flat1, chosen, 1, pairs)
+    low2, high2 = halos(flat2, "shot")
+    xs2 = stack_flat(flat2, low2, high2, 4, pairs)
     span = receivers // count
     whole = spread_call(xs2, second_pairs, flat2, chosen, 4, pairs)
     arrived = []

time: 80.7 us -> 77.6 us (0.962)
  Pallas kernels: 27.1 us -> 24.9 us
    reshape x2 -> x0, other arithmetic: 5.48 us -> none  [stack_time(): return stacked.reshape(stacked.shape[0], -1, stacked.shape[3])]
    select_n x0 -> x3, other arithmetic: none -> 2.53 us  [the longest x2 1.97 us: stack_flat(): after = jnp.where(phase == pairs - 1, jnp.zeros_like(after), after)]
    concatenate x2 -> x4, other arithmetic: 6.12 us -> 8.4 us  [the longest x2 8.02 us: stack_flat(): stacked = jnp.concatenate([before, volume, after], axis=2)]
    pallas_call x2, Pallas kernels: 27.1 us -> 24.9 us  [spread_call(): pl.pallas_call(functools.partial(spread_kernel, dilation=dilation, pairs=...]
where the time goes in v5:
time: 77.6 us; the launch traced here: 77.2 us
  Pallas kernels  24.9 us (32%)
  starting transfers between devices  17.6 us (23%)
  other arithmetic  16.4 us (21%)
  waiting for transfers between devices  12.3 us (16%)
  local copies, waits for them, and re-layouts  5.79 us (7%)
    pallas_call x2, Pallas kernels, spread_call(): pl.pallas_call(functools.partial(spread_kernel, dilation=dilation, pairs=...  24.9 us
    ppermute x3, waiting for transfers between devices, body(): piece = lax.ppermute(piece, 'shot', pairs_list)  9.99 us
    ppermute x2, starting transfers between devices, halos(): low = lax.ppermute(block[-1:], axis, forward)  9.08 us
    concatenate x2, other arithmetic, stack_flat(): stacked = jnp.concatenate([before, volume, after], axis=2)  8.02 us
    ppermute x3, starting transfers between devices, body(): piece = lax.ppermute(piece, 'shot', pairs_list)  5.74 us
    ppermute x2, starting transfers between devices, halos(): high = lax.ppermute(block[:1], axis, backward)  2.76 us
    ppermute x2, waiting for transfers between devices, halos(): high = lax.ppermute(block[:1], axis, backward)  2.26 us
    select_n x2, other arithmetic, stack_flat(): after = jnp.where(phase == pairs - 1, jnp.zeros_like(after), after)  1.97 us
  transfers between devices with their start and end apart: 7, of which 4 were waited for; matrix products, arithmetic and copies ran while one was open for 4% of the time, Pallas kernels for 0%

profile of v5, /device:TPU:0, one launch (start us, length us, event | category | flops | bytes accessed | tf_op | source)
XLA Modules:
  0.0 77.2 jit_solution(2398137671234001849)
XLA Ops:
  0.0 0.0 copy-start
  0.0 0.7 copy-done
  0.7 0.1 fusion.19
  0.7 0.0 copy-start.2
  0.8 1.8 %bitcast_multiply_fusion = bf16[4,128,8,128]{3,2,0,1:T(8,128)(2,1)S(1)} fusion(bf16[1,128,4,8,128]{4,3,2,1,0:T(8,128)(2,1)} %param.4, bf16[4,128]{0,1:T(8,128)(2,1)S(1)} %fusion.13), kind=kLoop, calls=%fused_computation.28 | loop fusion | flops 524288 | bytes 2098176 | tf_op jit(solution)/shard_map/mul | solution.py:180
  2.7 2.4 %collective-permute-start = (bf16[1,1024,128]{2,1,0:T(8,128)(2,1)S(1)}, bf16[1,1024,128]{2,1,0:T(8,128)(2,1)S(1)}, u32[]{:S(2)}, u32[]{:S(2)}) collective-permute-start(bf16[1,1024,128]{2,1,0:T(8,128)(2,1)S(1)} %get-tuple-element.25), channel_id=1, source_target_pairs={{0,4},{4,8},{8,12},{1,5},{5,9},{9,13},{2,6},{6,10},{10,14},{3,7},{... | collective-permute-start | bytes 786440 | tf_op jit(solution)/shard_map/ppermute | solution.py:99
  5.1 1.3 %collective-permute-start.1 = (bf16[1,1024,128]{2,1,0:T(8,128)(2,1)S(1)}, bf16[1,1024,128]{2,1,0:T(8,128)(2,1)S(1)}, u32[]{:S(2)}, u32[]{:S(2)}) collective-permute-start(bf16[1,1024,128]{2,1,0:T(8,128)(2,1)S(1)} %get-tuple-element.26), channel_id=1, source_target_pairs={{4,0},{8,4},{12,8},{5,1},{9,5},{13,9},{6,2},{10,6},{14,10},{7,3},{... | collective-permute-start | bytes 786440 | tf_op jit(solution)/shard_map/ppermute | solution.py:100
  6.4 0.0 copy-done.2
  6.4 0.1 slice_bitcast_fusion.7
  6.5 0.1 pad_dynamic-update-slice_fusion.3
  6.6 0.0 copy-start.3
  6.6 0.2 maximum_dynamic-update-slice_fusion.3
  6.8 0.2 maximum_dynamic-update-slice_fusion.2
  6.9 0.2 maximum_dynamic-update-slice_fusion.1
  7.1 0.2 maximum_dynamic-update-slice_fusion
  7.3 0.2 pad_dynamic-update-slice_fusion.2
  7.5 0.1 pad_add_fusion.scalars_ref
  7.6 0.3 copy-done.3
  7.9 0.1 slice_bitcast_fusion.2
  8.0 0.0 copy-start.1
  8.0 0.1 pad_dynamic-update-slice_fusion.1
  8.0 0.2 maximum_dynamic-update-slice_fusion.7
  8.2 0.2 maximum_dynamic-update-slice_fusion.6
  8.4 0.8 %copy-done.1 = bf16[1,128,4,8,128]{4,3,2,1,0:T(8,128)(2,1)S(1)} copy-done((bf16[1,128,4,8,128]{4,3,2,1,0:T(8,128)(2,1)S(1)}, bf16[1,128,4,8,128]{4,3,2,1,0:T(8,128)(2,1)}, u32[]{:S(2)}) %copy-start.1) | copy-done | bytes 1048600
  9.2 0.7 copy_bitcast_fusion.res_ref
  9.9 0.0 collective-permute-done
  9.9 0.7 collective-permute-done.1
  10.6 0.2 pad_maximum_fusion
  10.8 0.7 fusion.24
  11.5 1.6 %pad_select_fusion.2 = (bf16[6,1024,128]{2,1,0:T(8,128)(2,1)S(1)}, bf16[6,1024,128]{2,1,0:T(8,128)(2,1)S(1)}) fusion(bf16[6,1023,128]{2,1,0:T(8,128)(2,1)S(1)} %get-tuple-element.8, pred[1024]{0:T(1024)(128)(4,1)S(1)} %fusion.16, bf16[6,1023,128]{2,1,0:T(8,128)(2,1)S(1)} %get-tuple-element.7, pred[1024]{0:T(1024)(128)(4,1)S(1)} %fusion.17), kind=kLoop, calls=%fused_computation.25 | loop fusion | flops 1572864 | bytes 6290432 | tf_op jit(solution)/shard_map/jit(_where)/select_n | solution.py:112
  13.1 3.8 %select_maximum_fusion.2.xs_ref = bf16[6,1056,384]{2,1,0:T(8,128)(2,1)} fusion(bf16[6,1024,128]{2,1,0:T(8,128)(2,1)S(1)} %get-tuple-element.27, bf16[6,1024,128]{2,1,0:T(8,128)(2,1)S(1)} %get-tuple-element.28, bf16[1,1024,128]{2,1,0:T(8,128)(2,1)S(1)} %collective-permute-done.1, bf16[4,1024,128]{2,1,0:T(8,128)(2,1)S(1)} %copy_bitcast_fusion.res_ref, ...), kind=kLoop, calls=%fused_computation.14 | loop fusion | flops 43794432 | bytes 9584640 | tf_op jit(solution)/shard_map/concatenate | solution.py:113
  16.9 12.0 %shard_map.46.res_ref = bf16[4,1024,128]{2,1,0:T(8,128)(2,1)S(1)} custom-call(s32[5]{0:T(128)S(1)} %pad_add_fusion.scalars_ref, bf16[6,1056,384]{2,1,0:T(8,128)(2,1)} %select_maximum_fusion.2.xs_ref, bf16[15,384,128]{2,1,0:T(8,128)(2,1)S(1)} %bitcast.63, bf16[4,1024,128]{2,1,0:T(8,128)(2,1)S(1)} %copy_bitcast_fusion.res_ref), custom_call_target="tpu_custom_call" | custom-call | flops 6228541440 | bytes 8437760 | tf_op jit(solution)/shard_map/pallas_call | solution.py:54
  28.9 0.8 %fusion.25 = (bf16[1,1024,128]{2,1,0:T(8,128)(2,1)}, bf16[1,1024,128]{2,1,0:T(8,128)(2,1)}) fusion(bf16[4,1024,128]{2,1,0:T(8,128)(2,1)S(1)} %shard_map.46.res_ref), kind=kLoop, calls=%fused_computation.85 | loop fusion | bytes 1048576 | tf_op jit(solution)/shard_map/slice | solution.py:99
  29.7 6.7 %collective-permute-start.2 = (bf16[1,1024,128]{2,1,0:T(8,128)(2,1)}, bf16[1,1024,128]{2,1,0:T(8,128)(2,1)S(1)}, u32[]{:S(2)}, u32[]{:S(2)}) collective-permute-start(bf16[1,1024,128]{2,1,0:T(8,128)(2,1)} %get-tuple-element.23), channel_id=1, source_target_pairs={{0,4},{4,8},{8,12},{1,5},{5,9},{9,13},{2,6},{6,10},{10,14},{3,7},{... | collective-permute-start | bytes 786440 | tf_op jit(solution)/shard_map/ppermute | solution.py:99
  36.4 1.5 %collective-permute-start.3 = (bf16[1,1024,128]{2,1,0:T(8,128)(2,1)}, bf16[1,1024,128]{2,1,0:T(8,128)(2,1)S(1)}, u32[]{:S(2)}, u32[]{:S(2)}) collective-permute-start(bf16[1,1024,128]{2,1,0:T(8,128)(2,1)} %get-tuple-element.24), channel_id=1, source_target_pairs={{4,0},{8,4},{12,8},{5,1},{9,5},{13,9},{6,2},{10,6},{14,10},{7,3},{... | collective-permute-start | bytes 786440 | tf_op jit(solution)/shard_map/ppermute | solution.py:100
  37.9 0.2 maximum_dynamic-update-slice_fusion.5
  38.1 0.2 maximum_dynamic-update-slice_fusion.4
  38.3 0.2 pad_dynamic-update-slice_fusion
  38.4 0.0 collective-permute-done.2
  38.5 1.6 %collective-permute-done.3 = bf16[1,1024,128]{2,1,0:T(8,128)(2,1)S(1)} collective-permute-done((bf16[1,1024,128]{2,1,0:T(8,128)(2,1)}, bf16[1,1024,128]{2,1,0:T(8,128)(2,1)S(1)}, u32[]{:S(2)}, u32[]{:S(2)}) %collective-permute-start.3) | collective-permute-done | bytes 262176 | tf_op jit(solution)/shard_map/ppermute | solution.py:100
  40.0 0.2 pad_maximum_fusion.1
  40.2 0.7 fusion.23
  41.0 0.6 pad_select_fusion.1
  41.5 0.4 pad_select_fusion
  41.9 4.3 %select_maximum_fusion.xs_ref = bf16[6,1152,384]{2,1,0:T(8,128)(2,1)} fusion(bf16[6,1024,128]{2,1,0:T(8,128)(2,1)S(1)} %pad_select_fusion, bf16[6,1024,128]{2,1,0:T(8,128)(2,1)S(1)} %pad_select_fusion.1, bf16[1,1024,128]{2,1,0:T(8,128)(2,1)S(1)} %collective-permute-done.3, bf16[4,1024,128]{2,1,0:T(8,128)(2,1)S(1)} %shard_map.46.res_ref, ...), kind=kLoop, calls=%fused_computation.7 | loop fusion | flops 47775744 | bytes 10027008 | tf_op jit(solution)/shard_map/concatenate | solution.py:113
  46.2 12.9 %shard_map.47 = bf16[4,1024,128]{2,1,0:T(8,128)(2,1)S(1)} custom-call(s32[5]{0:T(128)S(1)} %pad_add_fusion.scalars_ref, bf16[6,1152,384]{2,1,0:T(8,128)(2,1)} %select_maximum_fusion.xs_ref, bf16[15,384,128]{2,1,0:T(8,128)(2,1)S(1)} %bitcast.64, bf16[4,1024,128]{2,1,0:T(8,128)(2,1)S(1)} %shard_map.46.res_ref), custom_call_target="tpu_custom_call" | custom-call | flops 6794772480 | bytes 8880128 | tf_op jit(solution)/shard_map/pallas_call | solution.py:54
  59.0 0.1 dynamic-slice_bitcast_fusion
  59.1 4.3 %collective-permute-start.4 = (bf16[4,256,128]{2,1,0:T(8,128)(2,1)S(1)}, bf16[4,256,128]{2,1,0:T(8,128)(2,1)S(1)}, u32[]{:S(2)}, u32[]{:S(2)}) collective-permute-start(bf16[4,256,128]{2,1,0:T(8,128)(2,1)S(1)} %get-tuple-element.22), channel_id=1, source_target_pairs={{0,4},{4,8},{8,12},{12,0},{1,5},{5,9},{9,13},{13,1},{2,6},{6,10},{... | collective-permute-start | bytes 786440 | tf_op jit(solution)/shard_map/ppermute | solution.py:195
  63.4 0.0 collective-permute-start.5
  63.4 1.4 %collective-permute-start.6 = (bf16[4,256,128]{2,1,0:T(8,128)(2,1)S(1)}, bf16[4,256,128]{2,1,0:T(8,128)(2,1)S(1)}, u32[]{:S(2)}, u32[]{:S(2)}) collective-permute-start(bf16[4,256,128]{2,1,0:T(8,128)(2,1)S(1)} %get-tuple-element.20), channel_id=1, source_target_pairs={{0,12},{4,0},{8,4},{12,8},{1,13},{5,1},{9,5},{13,9},{2,14},{6,2},{... | collective-permute-start | bytes 786440 | tf_op jit(solution)/shard_map/ppermute | solution.py:195
  64.9 0.1 broadcast_in_dim.45
  65.0 0.1 broadcast_in_dim.46
  65.1 0.0 collective-permute-done.4
  65.1 6.6 %collective-permute-done.5 = bf16[4,256,128]{2,1,0:T(8,128)(2,1)S(1)} collective-permute-done((bf16[4,256,128]{2,1,0:T(8,128)(2,1)S(1)}, bf16[4,256,128]{2,1,0:T(8,128)(2,1)S(1)}, u32[]{:S(2)}, u32[]{:S(2)}) %collective-permute-start.5) | collective-permute-done | bytes 262176 | tf_op jit(solution)/shard_map/ppermute | solution.py:195
  71.7 3.3 %collective-permute-done.6 = bf16[4,256,128]{2,1,0:T(8,128)(2,1)S(1)} collective-permute-done((bf16[4,256,128]{2,1,0:T(8,128)(2,1)S(1)}, bf16[4,256,128]{2,1,0:T(8,128)(2,1)S(1)}, u32[]{:S(2)}, u32[]{:S(2)}) %collective-permute-start.6) | collective-permute-done | bytes 262176 | tf_op jit(solution)/shard_map/ppermute | solution.py:195
  75.1 0.1 pad_maximum_fusion.2
  75.2 0.7 gather_fusion
  76.0 1.3 %fusion.12 = bf16[1,32,16,8,128]{4,3,2,1,0:T(8,128)(2,1)} fusion(bf16[16,32,8,128]{3,2,1,0:T(8,128)(2,1)S(1)} %bitcast.65, pred[16]{0:T(512)(128)(4,1)S(1)} %broadcast_in_dim.46), kind=kLoop, calls=%fused_computation.30 | loop fusion | flops 524288 | bytes 2097168 | tf_op jit(solution)/shard_map/broadcast_in_dim | solution.py:201
  (7 shorter events, 0.1 us)
Async XLA Ops:
  0.0 0.7 copy-start
  0.7 5.7 %copy-start.2 = (bf16[5,3,5,64,64]{4,3,2,1,0:T(8,128)(2,1)S(1)}, bf16[5,3,5,64,64]{4,3,2,1,0:T(8,128)(2,1)}, u32[]{:S(2)}) copy-start(bf16[5,3,5,64,64]{4,3,2,1,0:T(8,128)(2,1)} %param.6) | copy-start | bytes 1843204
  2.7 7.2 %collective-permute-start = (bf16[1,1024,128]{2,1,0:T(8,128)(2,1)S(1)}, bf16[1,1024,128]{2,1,0:T(8,128)(2,1)S(1)}, u32[]{:S(2)}, u32[]{:S(2)}) collective-permute-start(bf16[1,1024,128]{2,1,0:T(8,128)(2,1)S(1)} %get-tuple-element.25), channel_id=1, source_target_pairs={{0,4},{4,8},{8,12},{1,5},{5,9},{9,13},{2,6},{6,10},{10,14},{3,7},{... | collective-permute-start | bytes 786440 | tf_op jit(solution)/shard_map/ppermute | solution.py:99
  5.1 5.5 %collective-permute-start.1 = (bf16[1,1024,128]{2,1,0:T(8,128)(2,1)S(1)}, bf16[1,1024,128]{2,1,0:T(8,128)(2,1)S(1)}, u32[]{:S(2)}, u32[]{:S(2)}) collective-permute-start(bf16[1,1024,128]{2,1,0:T(8,128)(2,1)S(1)} %get-tuple-element.26), channel_id=1, source_target_pairs={{4,0},{8,4},{12,8},{5,1},{9,5},{13,9},{6,2},{10,6},{14,10},{7,3},{... | collective-permute-start | bytes 786440 | tf_op jit(solution)/shard_map/ppermute | solution.py:100
  6.6 1.3 %copy-start.3 = (bf16[5,3,5,64,64]{4,3,2,1,0:T(8,128)(2,1)S(1)}, bf16[5,3,5,64,64]{4,3,2,1,0:T(8,128)(2,1)}, u32[]{:S(2)}) copy-start(bf16[5,3,5,64,64]{4,3,2,1,0:T(8,128)(2,1)} %param.7) | copy-start | bytes 1843204
  8.0 1.2 %copy-start.1 = (bf16[1,128,4,8,128]{4,3,2,1,0:T(8,128)(2,1)S(1)}, bf16[1,128,4,8,128]{4,3,2,1,0:T(8,128)(2,1)}, u32[]{:S(2)}) copy-start(bf16[1,128,4,8,128]{4,3,2,1,0:T(8,128)(2,1)} %param.4) | copy-start | bytes 3145732
  29.7 8.7 %collective-permute-start.2 = (bf16[1,1024,128]{2,1,0:T(8,128)(2,1)}, bf16[1,1024,128]{2,1,0:T(8,128)(2,1)S(1)}, u32[]{:S(2)}, u32[]{:S(2)}) collective-permute-start(bf16[1,1024,128]{2,1,0:T(8,128)(2,1)} %get-tuple-element.23), channel_id=1, source_target_pairs={{0,4},{4,8},{8,12},{1,5},{5,9},{9,13},{2,6},{6,10},{10,14},{3,7},{... | collective-permute-start | bytes 786440 | tf_op jit(solution)/shard_map/ppermute | solution.py:99
  36.4 3.6 %collective-permute-start.3 = (bf16[1,1024,128]{2,1,0:T(8,128)(2,1)}, bf16[1,1024,128]{2,1,0:T(8,128)(2,1)S(1)}, u32[]{:S(2)}, u32[]{:S(2)}) collective-permute-start(bf16[1,1024,128]{2,1,0:T(8,128)(2,1)} %get-tuple-element.24), channel_id=1, source_target_pairs={{4,0},{8,4},{12,8},{5,1},{9,5},{13,9},{6,2},{10,6},{14,10},{7,3},{... | collective-permute-start | bytes 786440 | tf_op jit(solution)/shard_map/ppermute | solution.py:100
  59.1 6.0 %collective-permute-start.4 = (bf16[4,256,128]{2,1,0:T(8,128)(2,1)S(1)}, bf16[4,256,128]{2,1,0:T(8,128)(2,1)S(1)}, u32[]{:S(2)}, u32[]{:S(2)}) collective-permute-start(bf16[4,256,128]{2,1,0:T(8,128)(2,1)S(1)} %get-tuple-element.22), channel_id=1, source_target_pairs={{0,4},{4,8},{8,12},{12,0},{1,5},{5,9},{9,13},{13,1},{2,6},{6,10},{... | collective-permute-start | bytes 786440 | tf_op jit(solution)/shard_map/ppermute | solution.py:195
  63.4 8.3 %collective-permute-start.5 = (bf16[4,256,128]{2,1,0:T(8,128)(2,1)S(1)}, bf16[4,256,128]{2,1,0:T(8,128)(2,1)S(1)}, u32[]{:S(2)}, u32[]{:S(2)}) collective-permute-start(bf16[4,256,128]{2,1,0:T(8,128)(2,1)S(1)} %get-tuple-element.21), channel_id=1, source_target_pairs={{0,8},{4,12},{8,0},{12,4},{1,9},{5,13},{9,1},{13,5},{2,10},{6,14},... | collective-permute-start | bytes 786440 | tf_op jit(solution)/shard_map/ppermute | solution.py:195
  63.4 11.6 %collective-permute-start.6 = (bf16[4,256,128]{2,1,0:T(8,128)(2,1)S(1)}, bf16[4,256,128]{2,1,0:T(8,128)(2,1)S(1)}, u32[]{:S(2)}, u32[]{:S(2)}) collective-permute-start(bf16[4,256,128]{2,1,0:T(8,128)(2,1)S(1)} %get-tuple-element.20), channel_id=1, source_target_pairs={{0,12},{4,0},{8,4},{12,8},{1,13},{5,1},{9,5},{13,9},{2,14},{6,2},{... | collective-permute-start | bytes 786440 | tf_op jit(solution)/shard_map/ppermute | solution.py:195

commit v6 on v5

--- a/solution.py
+++ b/solution.py
@@ -57,7 +57,9 @@
             num_scalar_prefetch=1,
             grid=(shots,),
             in_specs=[
-                pl.BlockSpec(xs.shape, lambda s, c: (0, 0, 0)),
+                pl.BlockSpec((1, xs.shape[1], xs.shape[2]), lambda s, c: (s, 0, 0)),
+                pl.BlockSpec((1, xs.shape[1], xs.shape[2]), lambda s, c: (s + 1, 0, 0)),
+                pl.BlockSpec((1, xs.shape[1], xs.shape[2]), lambda s, c: (s + 2, 0, 0)),
                 pl.BlockSpec(weights.shape, lambda s, c: (0, 0, 0)),
                 pl.BlockSpec((1, rows, lanes), lambda s, c: (s, 0, 0)),
             ],
@@ -70,13 +72,13 @@
             transcendentals=0,
             bytes_accessed=xs.size * 2 + weights.size * 2 + 4 * shots * rows * lanes,
         ),
-    )(scalars, xs, weights, flat)
-
-
-def spread_kernel(scalars_ref, xs_ref, w_ref, res_ref, out_ref, *, dilation, pairs):
+    )(scalars, xs, xs, xs, weights, flat)
+
+
+def spread_kernel(scalars_ref, x0_ref, x1_ref, x2_ref, w_ref, res_ref, out_ref, *, dilation, pairs):
     s = pl.program_id(0)
     rows, lanes = out_ref.shape[1:]
-    lhs = jnp.concatenate([xs_ref[s + b] for b in range(3)], axis=1)
+    lhs = jnp.concatenate([x0_ref[0], x1_ref[0], x2_ref[0]], axis=1)
     rhs = jnp.concatenate(
         [jnp.concatenate([w_ref[a * 3 + b] for a in range(5)], axis=1) for b in range(3)], axis=0
     )
@@ -194,9 +196,10 @@
             pairs_list = [(i, (i + shift) % count) for i in range(count)]
             piece = lax.ppermute(piece, "shot", pairs_list)
         arrived.append((shift, piece))
-    by_shift = jnp.stack([piece for _, piece in sorted(arrived, key=lambda t: t[0])])
-    order = lax.rem(me - jnp.arange(count, dtype=jnp.int32) + count, count)
-    ordered = jnp.take(by_shift, order, axis=0)
+    by_shift = [piece for _, piece in sorted(arrived, key=lambda t: t[0])]
+    ordered = jnp.concatenate(
+        [lax.select_n(lax.rem(me - q + count, count), *by_shift) for q in range(count)], axis=0
+    )
     ordered = ordered.reshape(count * shot_local, span, pairs, lanes)
     return jnp.transpose(ordered, (1, 0, 2, 3))[None]
 

time: 77.6 us -> 76.2 us (0.982)
  local copies, waits for them, and re-layouts: 5.79 us -> 4.85 us
  Pallas kernels: 24.9 us -> 24 us
    pallas_call x2, Pallas kernels: 24.9 us -> 24 us  [spread_call(): pl.pallas_call(functools.partial(spread_kernel, dilation=dilation, pairs=...]
    unnamed x10 -> x14, local copies, waits for them, and re-layouts: 1.88 us -> 1.89 us
  transfers between devices with their start and end apart: 7 -> 7, of which waited for: 4 -> 5; matrix products, arithmetic and copies ran while one was open for 4% -> 4% of each run, Pallas kernels for 0% -> 0%
where the time goes in v6:
time: 76.2 us; the launch traced here: 75.9 us
  Pallas kernels  24 us (31%)
  starting transfers between devices  17.6 us (23%)
  other arithmetic  16.6 us (22%)
  waiting for transfers between devices  12.5 us (16%)
  local copies, waits for them, and re-layouts  4.85 us (6%)
    pallas_call x2, Pallas kernels, spread_call(): pl.pallas_call(functools.partial(spread_kernel, dilation=dilation, pairs=...  24 us
    ppermute x3, waiting for transfers between devices, body(): piece = lax.ppermute(piece, 'shot', pairs_list)  10.2 us
    ppermute x2, starting transfers between devices, halos(): low = lax.ppermute(block[-1:], axis, forward)  9.07 us
    concatenate x2, other arithmetic, stack_flat(): stacked = jnp.concatenate([before, volume, after], axis=2)  8.03 us
    ppermute x3, starting transfers between devices, body(): piece = lax.ppermute(piece, 'shot', pairs_list)  5.74 us
    ppermute x2, starting transfers between devices, halos(): high = lax.ppermute(block[:1], axis, backward)  2.76 us
    ppermute x2, waiting for transfers between devices, halos(): high = lax.ppermute(block[:1], axis, backward)  2.25 us
    select_n x2, other arithmetic, stack_flat(): after = jnp.where(phase == pairs - 1, jnp.zeros_like(after), after)  1.97 us
  transfers between devices with their start and end apart: 7, of which 5 were waited for; matrix products, arithmetic and copies ran while one was open for 4% of the time, Pallas kernels for 0%

profile of v6, /device:TPU:0, one launch (start us, length us, event | category | flops | bytes accessed | tf_op | source)
XLA Modules:
  0.0 75.9 jit_solution(15901820995093021032)
XLA Ops:
  0.0 0.0 copy-start
  0.0 0.7 copy-done
  0.7 0.1 fusion.18
  0.7 0.0 copy-start.4
  0.8 1.8 %bitcast_multiply_fusion = bf16[4,128,8,128]{3,2,0,1:T(8,128)(2,1)S(1)} fusion(bf16[1,128,4,8,128]{4,3,2,1,0:T(8,128)(2,1)} %param.4, bf16[4,128]{0,1:T(8,128)(2,1)S(1)} %fusion.12), kind=kLoop, calls=%fused_computation.27 | loop fusion | flops 524288 | bytes 2098176 | tf_op jit(solution)/shard_map/mul | solution.py:182
  2.7 2.4 %collective-permute-start = (bf16[1,1024,128]{2,1,0:T(8,128)(2,1)S(1)}, bf16[1,1024,128]{2,1,0:T(8,128)(2,1)S(1)}, u32[]{:S(2)}, u32[]{:S(2)}) collective-permute-start(bf16[1,1024,128]{2,1,0:T(8,128)(2,1)S(1)} %get-tuple-element.28), channel_id=1, source_target_pairs={{0,4},{4,8},{8,12},{1,5},{5,9},{9,13},{2,6},{6,10},{10,14},{3,7},{... | collective-permute-start | bytes 786440 | tf_op jit(solution)/shard_map/ppermute | solution.py:101
  5.1 1.3 %collective-permute-start.1 = (bf16[1,1024,128]{2,1,0:T(8,128)(2,1)S(1)}, bf16[1,1024,128]{2,1,0:T(8,128)(2,1)S(1)}, u32[]{:S(2)}, u32[]{:S(2)}) collective-permute-start(bf16[1,1024,128]{2,1,0:T(8,128)(2,1)S(1)} %get-tuple-element.29), channel_id=1, source_target_pairs={{4,0},{8,4},{12,8},{5,1},{9,5},{13,9},{6,2},{10,6},{14,10},{7,3},{... | collective-permute-start | bytes 786440 | tf_op jit(solution)/shard_map/ppermute | solution.py:102
  6.4 0.0 copy-done.4
  6.4 0.1 slice_bitcast_fusion.7
  6.5 0.1 pad_dynamic-update-slice_fusion.3
  6.6 0.0 copy-start.5
  6.6 0.2 maximum_dynamic-update-slice_fusion.3
  6.8 0.2 maximum_dynamic-update-slice_fusion.2
  6.9 0.2 maximum_dynamic-update-slice_fusion.1
  7.1 0.2 maximum_dynamic-update-slice_fusion
  7.3 0.2 pad_dynamic-update-slice_fusion.2
  7.5 0.1 pad_add_fusion.scalars_ref
  7.6 0.3 copy-done.5
  7.9 0.1 slice_bitcast_fusion.2
  8.0 0.0 copy-start.3
  8.0 0.1 pad_dynamic-update-slice_fusion.1
  8.0 0.2 maximum_dynamic-update-slice_fusion.7
  8.2 0.2 maximum_dynamic-update-slice_fusion.6
  8.4 0.8 %copy-done.3 = bf16[1,128,4,8,128]{4,3,2,1,0:T(8,128)(2,1)S(1)} copy-done((bf16[1,128,4,8,128]{4,3,2,1,0:T(8,128)(2,1)S(1)}, bf16[1,128,4,8,128]{4,3,2,1,0:T(8,128)(2,1)}, u32[]{:S(2)}) %copy-start.3) | copy-done | bytes 1048600
  9.2 0.7 copy_bitcast_fusion.1.res_ref
  9.9 0.0 collective-permute-done
  9.9 0.7 collective-permute-done.1
  10.6 0.2 pad_maximum_fusion
  10.8 0.7 fusion.20
  11.5 1.6 %pad_select_fusion.2 = (bf16[6,1024,128]{2,1,0:T(8,128)(2,1)S(1)}, bf16[6,1024,128]{2,1,0:T(8,128)(2,1)S(1)}) fusion(bf16[6,1023,128]{2,1,0:T(8,128)(2,1)S(1)} %get-tuple-element.12, pred[1024]{0:T(1024)(128)(4,1)S(1)} %fusion.15, bf16[6,1023,128]{2,1,0:T(8,128)(2,1)S(1)} %get-tuple-element.11, pred[1024]{0:T(1024)(128)(4,1)S(1)} %fusion.16), kind=kLoop, calls=%fused_computation.24 | loop fusion | flops 1572864 | bytes 6290432 | tf_op jit(solution)/shard_map/jit(_where)/select_n | solution.py:114
  13.1 3.8 %select_maximum_fusion.2.x0_ref.x1_ref.x2_ref = bf16[6,1056,384]{2,1,0:T(8,128)(2,1)} fusion(bf16[6,1024,128]{2,1,0:T(8,128)(2,1)S(1)} %get-tuple-element.30, bf16[6,1024,128]{2,1,0:T(8,128)(2,1)S(1)} %get-tuple-element.31, bf16[1,1024,128]{2,1,0:T(8,128)(2,1)S(1)} %collective-permute-done.1, bf16[4,1024,128]{2,1,0:T(8,128)(2,1)S(1)} %copy_bitcast_fusion.1.res_ref, ...), kind=kLoop, calls=%fused_computation.13 | loop fusion | flops 43794432 | bytes 9584640 | tf_op jit(solution)/shard_map/concatenate | solution.py:115
  16.9 11.6 %shard_map.46.res_ref = bf16[4,1024,128]{2,1,0:T(8,128)(2,1)S(1)} custom-call(s32[5]{0:T(128)S(1)} %pad_add_fusion.scalars_ref, bf16[6,1056,384]{2,1,0:T(8,128)(2,1)} %select_maximum_fusion.2.x0_ref.x1_ref.x2_ref, bf16[6,1056,384]{2,1,0:T(8,128)(2,1)} %select_maximum_fusion.2.x0_ref.x1_ref.x2_ref, ...), custom_call_target="tpu_custom_call" | custom-call | flops 6228541440 | bytes 8437760 | tf_op jit(solution)/shard_map/pallas_call | solution.py:54
  28.4 0.8 %fusion.21 = (bf16[1,1024,128]{2,1,0:T(8,128)(2,1)}, bf16[1,1024,128]{2,1,0:T(8,128)(2,1)}) fusion(bf16[4,1024,128]{2,1,0:T(8,128)(2,1)S(1)} %shard_map.46.res_ref), kind=kLoop, calls=%fused_computation.75 | loop fusion | bytes 1048576 | tf_op jit(solution)/shard_map/slice | solution.py:101
  29.3 6.7 %collective-permute-start.2 = (bf16[1,1024,128]{2,1,0:T(8,128)(2,1)}, bf16[1,1024,128]{2,1,0:T(8,128)(2,1)S(1)}, u32[]{:S(2)}, u32[]{:S(2)}) collective-permute-start(bf16[1,1024,128]{2,1,0:T(8,128)(2,1)} %get-tuple-element.26), channel_id=1, source_target_pairs={{0,4},{4,8},{8,12},{1,5},{5,9},{9,13},{2,6},{6,10},{10,14},{3,7},{... | collective-permute-start | bytes 786440 | tf_op jit(solution)/shard_map/ppermute | solution.py:101
  35.9 1.5 %collective-permute-start.3 = (bf16[1,1024,128]{2,1,0:T(8,128)(2,1)}, bf16[1,1024,128]{2,1,0:T(8,128)(2,1)S(1)}, u32[]{:S(2)}, u32[]{:S(2)}) collective-permute-start(bf16[1,1024,128]{2,1,0:T(8,128)(2,1)} %get-tuple-element.27), channel_id=1, source_target_pairs={{4,0},{8,4},{12,8},{5,1},{9,5},{13,9},{6,2},{10,6},{14,10},{7,3},{... | collective-permute-start | bytes 786440 | tf_op jit(solution)/shard_map/ppermute | solution.py:102
  37.4 0.2 maximum_dynamic-update-slice_fusion.5
  37.6 0.2 maximum_dynamic-update-slice_fusion.4
  37.8 0.2 pad_dynamic-update-slice_fusion
  38.0 0.0 copy-start.1
  38.0 0.0 collective-permute-done.2
  38.0 1.6 %collective-permute-done.3 = bf16[1,1024,128]{2,1,0:T(8,128)(2,1)S(1)} collective-permute-done((bf16[1,1024,128]{2,1,0:T(8,128)(2,1)}, bf16[1,1024,128]{2,1,0:T(8,128)(2,1)S(1)}, u32[]{:S(2)}, u32[]{:S(2)}) %collective-permute-start.3) | collective-permute-done | bytes 262176 | tf_op jit(solution)/shard_map/ppermute | solution.py:102
  39.6 0.2 pad_maximum_fusion.1
  39.8 0.0 copy-done.1
  39.8 0.7 fusion.19
  40.5 0.6 pad_select_fusion.1
  41.1 0.4 pad_select_fusion
  41.5 0.0 copy-start.2
  41.5 4.3 %select_maximum_fusion.x0_ref.x1_ref.x2_ref = bf16[6,1152,384]{2,1,0:T(8,128)(2,1)} fusion(bf16[6,1024,128]{2,1,0:T(8,128)(2,1)S(1)} %pad_select_fusion, bf16[6,1024,128]{2,1,0:T(8,128)(2,1)S(1)} %pad_select_fusion.1, bf16[1,1024,128]{2,1,0:T(8,128)(2,1)S(1)} %collective-permute-done.3, bf16[4,1024,128]{2,1,0:T(8,128)(2,1)S(1)} %shard_map.46.res_ref, ...), kind=kLoop, calls=%fused_computation.6 | loop fusion | flops 47775744 | bytes 10027008 | tf_op jit(solution)/shard_map/concatenate | solution.py:115
  45.8 0.0 copy-done.2
  45.8 12.5 %shard_map.47 = bf16[4,1024,128]{2,1,0:T(8,128)(2,1)S(1)} custom-call(s32[5]{0:T(128)S(1)} %pad_add_fusion.scalars_ref, bf16[6,1152,384]{2,1,0:T(8,128)(2,1)} %select_maximum_fusion.x0_ref.x1_ref.x2_ref, bf16[6,1152,384]{2,1,0:T(8,128)(2,1)} %select_maximum_fusion.x0_ref.x1_ref.x2_ref, bf16[6,1152,384]{2,1,0:T(8,128)(2,1)} %select_maximum_fusion.x0_ref.x1_ref.x2_ref, ...), custom_call_target="tpu_custom_call" | custom-call | flops 6794772480 | bytes 8880128 | tf_op jit(solution)/shard_map/pallas_call | solution.py:54
  58.2 0.1 constant_dynamic-slice_fusion.2
  58.3 4.3 %collective-permute-start.4 = (bf16[4,256,128]{2,1,0:T(8,128)(2,1)S(1)}, bf16[4,256,128]{2,1,0:T(8,128)(2,1)S(1)}, u32[]{:S(2)}, u32[]{:S(2)}) collective-permute-start(bf16[4,256,128]{2,1,0:T(8,128)(2,1)S(1)} %get-tuple-element.23), channel_id=1, source_target_pairs={{0,4},{4,8},{8,12},{12,0},{1,5},{5,9},{9,13},{13,1},{2,6},{6,10},{... | collective-permute-start | bytes 786440 | tf_op jit(solution)/shard_map/ppermute | solution.py:197
  62.6 0.0 collective-permute-start.5
  62.6 1.4 %collective-permute-start.6 = (bf16[4,256,128]{2,1,0:T(8,128)(2,1)S(1)}, bf16[4,256,128]{2,1,0:T(8,128)(2,1)S(1)}, u32[]{:S(2)}, u32[]{:S(2)}) collective-permute-start(bf16[4,256,128]{2,1,0:T(8,128)(2,1)S(1)} %get-tuple-element.24), channel_id=1, source_target_pairs={{0,12},{4,0},{8,4},{12,8},{1,13},{5,1},{9,5},{13,9},{2,14},{6,2},{... | collective-permute-start | bytes 786440 | tf_op jit(solution)/shard_map/ppermute | solution.py:197
  64.1 0.1 collective-permute-done.4
  64.2 6.8 %collective-permute-done.5 = bf16[4,256,128]{2,1,0:T(8,128)(2,1)S(1)} collective-permute-done((bf16[4,256,128]{2,1,0:T(8,128)(2,1)S(1)}, bf16[4,256,128]{2,1,0:T(8,128)(2,1)S(1)}, u32[]{:S(2)}, u32[]{:S(2)}) %collective-permute-start.5) | collective-permute-done | bytes 262176 | tf_op jit(solution)/shard_map/ppermute | solution.py:197
  70.9 3.3 %collective-permute-done.6 = bf16[4,256,128]{2,1,0:T(8,128)(2,1)S(1)} collective-permute-done((bf16[4,256,128]{2,1,0:T(8,128)(2,1)S(1)}, bf16[4,256,128]{2,1,0:T(8,128)(2,1)S(1)}, u32[]{:S(2)}, u32[]{:S(2)}) %collective-permute-start.6) | collective-permute-done | bytes 262176 | tf_op jit(solution)/shard_map/ppermute | solution.py:197
  74.3 0.3 select_select_fusion.3
  74.6 1.3 %copy_bitcast_fusion = bf16[1,32,16,8,128]{4,3,2,1,0:T(8,128)(2,1)} fusion(bf16[4,256,128]{2,1,0:T(8,128)(2,1)S(1)} %get-tuple-element.6, bf16[4,256,128]{2,1,0:T(8,128)(2,1)S(1)} %get-tuple-element.7, bf16[4,256,128]{2,1,0:T(8,128)(2,1)S(1)} %get-tuple-element.8, bf16[4,256,128]{2,1,0:T(8,128)(2,1)S(1)} %get-tuple-element.5), kind=kLoop, calls=%fused_computation.28 | loop fusion | flops 1572864 | bytes 2097152 | tf_op jit(solution)/shard_map/broadcast_in_dim | solution.py:204
  (4 shorter events, 0.1 us)
Async XLA Ops:
  0.0 0.7 copy-start
  0.7 5.7 %copy-start.4 = (bf16[5,3,5,64,64]{4,3,2,1,0:T(8,128)(2,1)S(1)}, bf16[5,3,5,64,64]{4,3,2,1,0:T(8,128)(2,1)}, u32[]{:S(2)}) copy-start(bf16[5,3,5,64,64]{4,3,2,1,0:T(8,128)(2,1)} %param.6) | copy-start | bytes 1843204
  2.7 7.2 %collective-permute-start = (bf16[1,1024,128]{2,1,0:T(8,128)(2,1)S(1)}, bf16[1,1024,128]{2,1,0:T(8,128)(2,1)S(1)}, u32[]{:S(2)}, u32[]{:S(2)}) collective-permute-start(bf16[1,1024,128]{2,1,0:T(8,128)(2,1)S(1)} %get-tuple-element.28), channel_id=1, source_target_pairs={{0,4},{4,8},{8,12},{1,5},{5,9},{9,13},{2,6},{6,10},{10,14},{3,7},{... | collective-permute-start | bytes 786440 | tf_op jit(solution)/shard_map/ppermute | solution.py:101
  5.1 5.5 %collective-permute-start.1 = (bf16[1,1024,128]{2,1,0:T(8,128)(2,1)S(1)}, bf16[1,1024,128]{2,1,0:T(8,128)(2,1)S(1)}, u32[]{:S(2)}, u32[]{:S(2)}) collective-permute-start(bf16[1,1024,128]{2,1,0:T(8,128)(2,1)S(1)} %get-tuple-element.29), channel_id=1, source_target_pairs={{4,0},{8,4},{12,8},{5,1},{9,5},{13,9},{6,2},{10,6},{14,10},{7,3},{... | collective-permute-start | bytes 786440 | tf_op jit(solution)/shard_map/ppermute | solution.py:102
  6.6 1.3 %copy-start.5 = (bf16[5,3,5,64,64]{4,3,2,1,0:T(8,128)(2,1)S(1)}, bf16[5,3,5,64,64]{4,3,2,1,0:T(8,128)(2,1)}, u32[]{:S(2)}) copy-start(bf16[5,3,5,64,64]{4,3,2,1,0:T(8,128)(2,1)} %param.7) | copy-start | bytes 1843204
  8.0 1.2 %copy-start.3 = (bf16[1,128,4,8,128]{4,3,2,1,0:T(8,128)(2,1)S(1)}, bf16[1,128,4,8,128]{4,3,2,1,0:T(8,128)(2,1)}, u32[]{:S(2)}) copy-start(bf16[1,128,4,8,128]{4,3,2,1,0:T(8,128)(2,1)} %param.4) | copy-start | bytes 3145732
  29.3 8.7 %collective-permute-start.2 = (bf16[1,1024,128]{2,1,0:T(8,128)(2,1)}, bf16[1,1024,128]{2,1,0:T(8,128)(2,1)S(1)}, u32[]{:S(2)}, u32[]{:S(2)}) collective-permute-start(bf16[1,1024,128]{2,1,0:T(8,128)(2,1)} %get-tuple-element.26), channel_id=1, source_target_pairs={{0,4},{4,8},{8,12},{1,5},{5,9},{9,13},{2,6},{6,10},{10,14},{3,7},{... | collective-permute-start | bytes 786440 | tf_op jit(solution)/shard_map/ppermute | solution.py:101
  35.9 3.6 %collective-permute-start.3 = (bf16[1,1024,128]{2,1,0:T(8,128)(2,1)}, bf16[1,1024,128]{2,1,0:T(8,128)(2,1)S(1)}, u32[]{:S(2)}, u32[]{:S(2)}) collective-permute-start(bf16[1,1024,128]{2,1,0:T(8,128)(2,1)} %get-tuple-element.27), channel_id=1, source_target_pairs={{4,0},{8,4},{12,8},{5,1},{9,5},{13,9},{6,2},{10,6},{14,10},{7,3},{... | collective-permute-start | bytes 786440 | tf_op jit(solution)/shard_map/ppermute | solution.py:102
  38.0 1.8 %copy-start.1 = (bf16[5,3,384,128]{3,2,1,0:T(8,128)(2,1)}, bf16[5,3,384,128]{3,2,1,0:T(8,128)(2,1)S(1)}, u32[]{:S(2)}) copy-start(bf16[5,3,384,128]{3,2,1,0:T(8,128)(2,1)S(1)} %pad_dynamic-update-slice_fusion) | copy-start | bytes 4423684
  41.5 4.3 %copy-start.2 = (bf16[5,3,384,128]{3,2,1,0:T(8,128)(2,1)S(1)}, bf16[5,3,384,128]{3,2,1,0:T(8,128)(2,1)}, u32[]{:S(2)}) copy-start(bf16[5,3,384,128]{3,2,1,0:T(8,128)(2,1)} %copy-done.1) | copy-start | bytes 4423684
  58.3 5.8 %collective-permute-start.4 = (bf16[4,256,128]{2,1,0:T(8,128)(2,1)S(1)}, bf16[4,256,128]{2,1,0:T(8,128)(2,1)S(1)}, u32[]{:S(2)}, u32[]{:S(2)}) collective-permute-start(bf16[4,256,128]{2,1,0:T(8,128)(2,1)S(1)} %get-tuple-element.23), channel_id=1, source_target_pairs={{0,4},{4,8},{8,12},{12,0},{1,5},{5,9},{9,13},{13,1},{2,6},{6,10},{... | collective-permute-start | bytes 786440 | tf_op jit(solution)/shard_map/ppermute | solution.py:197
  62.6 8.3 %collective-permute-start.5 = (bf16[4,256,128]{2,1,0:T(8,128)(2,1)S(1)}, bf16[4,256,128]{2,1,0:T(8,128)(2,1)S(1)}, u32[]{:S(2)}, u32[]{:S(2)}) collective-permute-start(bf16[4,256,128]{2,1,0:T(8,128)(2,1)S(1)} %get-tuple-element.25), channel_id=1, source_target_pairs={{0,8},{4,12},{8,0},{12,4},{1,9},{5,13},{9,1},{13,5},{2,10},{6,14},... | collective-permute-start | bytes 786440 | tf_op jit(solution)/shard_map/ppermute | solution.py:197
  62.6 11.6 %collective-permute-start.6 = (bf16[4,256,128]{2,1,0:T(8,128)(2,1)S(1)}, bf16[4,256,128]{2,1,0:T(8,128)(2,1)S(1)}, u32[]{:S(2)}, u32[]{:S(2)}) collective-permute-start(bf16[4,256,128]{2,1,0:T(8,128)(2,1)S(1)} %get-tuple-element.24), channel_id=1, source_target_pairs={{0,12},{4,0},{8,4},{12,8},{1,13},{5,1},{9,5},{13,9},{2,14},{6,2},{... | collective-permute-start | bytes 786440 | tf_op jit(solution)/shard_map/ppermute | solution.py:197

commit v7 on v6

--- a/solution.py
+++ b/solution.py
@@ -47,7 +47,7 @@
     return stacked.reshape(stacked.shape[0], -1, stacked.shape[3])
 
 
-def spread_call(xs, weights, flat, counts, dilation, pairs):
+def spread_call(low, xs, high, weights, flat, counts, dilation, pairs):
     shots, rows, lanes = flat.shape
     scalars = jnp.concatenate([jnp.zeros((1,), jnp.int32), counts])
     flops = 2 * shots * 15 * xs.shape[1] * xs.shape[2] * weights.shape[2]
@@ -57,9 +57,13 @@
             num_scalar_prefetch=1,
             grid=(shots,),
             in_specs=[
+                pl.BlockSpec((1, xs.shape[1], xs.shape[2]), lambda s, c: (0, 0, 0)),
+                pl.BlockSpec((1, xs.shape[1], xs.shape[2]), lambda s, c: (jnp.maximum(s - 1, 0), 0, 0)),
                 pl.BlockSpec((1, xs.shape[1], xs.shape[2]), lambda s, c: (s, 0, 0)),
-                pl.BlockSpec((1, xs.shape[1], xs.shape[2]), lambda s, c: (s + 1, 0, 0)),
-                pl.BlockSpec((1, xs.shape[1], xs.shape[2]), lambda s, c: (s + 2, 0, 0)),
+                pl.BlockSpec(
+                    (1, xs.shape[1], xs.shape[2]), lambda s, c: (jnp.minimum(s + 1, shots - 1), 0, 0)
+                ),
+                pl.BlockSpec((1, xs.shape[1], xs.shape[2]), lambda s, c: (0, 0, 0)),
                 pl.BlockSpec(weights.shape, lambda s, c: (0, 0, 0)),
                 pl.BlockSpec((1, rows, lanes), lambda s, c: (s, 0, 0)),
             ],
@@ -70,15 +74,17 @@
         cost_estimate=pl.CostEstimate(
             flops=flops,
             transcendentals=0,
-            bytes_accessed=xs.size * 2 + weights.size * 2 + 4 * shots * rows * lanes,
-        ),
-    )(scalars, xs, xs, xs, weights, flat)
-
-
-def spread_kernel(scalars_ref, x0_ref, x1_ref, x2_ref, w_ref, res_ref, out_ref, *, dilation, pairs):
+            bytes_accessed=(xs.size + low.size + high.size) * 2 + weights.size * 2 + 4 * shots * rows * lanes,
+        ),
+    )(scalars, low, xs, xs, xs, high, weights, flat)
+
+
+def spread_kernel(scalars_ref, lo_ref, x0_ref, x1_ref, x2_ref, hi_ref, w_ref, res_ref, out_ref, *, dilation, pairs):
     s = pl.program_id(0)
     rows, lanes = out_ref.shape[1:]
-    lhs = jnp.concatenate([x0_ref[0], x1_ref[0], x2_ref[0]], axis=1)
+    first_shot = jnp.where(s == 0, lo_ref[0], x0_ref[0])
+    last_shot = jnp.where(s == pl.num_programs(0) - 1, hi_ref[0], x2_ref[0])
+    lhs = jnp.concatenate([first_shot, x1_ref[0], last_shot], axis=1)
     rhs = jnp.concatenate(
         [jnp.concatenate([w_ref[a * 3 + b] for a in range(5)], axis=1) for b in range(3)], axis=0
     )
@@ -103,8 +109,7 @@
     return low, high
 
 
-def stack_flat(inner, low, high, dilation, pairs):
-    volume = jnp.concatenate([low, inner, high], axis=0)
+def stack_rows(volume, dilation, pairs):
     rows = volume.shape[1]
     phase = (jnp.arange(rows, dtype=jnp.int32) % pairs)[None, :, None]
     blank = jnp.zeros_like(volume[:, :1])
@@ -177,17 +182,20 @@
     chosen = lax.dynamic_slice_in_dim(counts[:, 0], me * shot_local, shot_local)
     first_pairs = pair_weights(first_weight)
     second_pairs = pair_weights(second_weight)
-    volume = jnp.transpose(features[0], (1, 0, 2, 3))
-    alive = jnp.arange(receivers, dtype=jnp.int32)[None, :] < chosen[:, None]
-    inputs = volume * alive.astype(volume.dtype)[:, :, None, None]
-    flat1 = inputs.reshape(shot_local, receivers * pairs, lanes)
+    volume = jnp.transpose(features[0], (1, 0, 2, 3)).reshape(shot_local, receivers * pairs, lanes)
+    alive = jnp.arange(receivers * pairs, dtype=jnp.int32)[None, :] // pairs < chosen[:, None]
+    flat1 = volume * alive.astype(volume.dtype)[:, :, None]
     low1, high1 = halos(flat1, "shot")
-    xs1 = stack_flat(flat1, low1, high1, 1, pairs)
-    flat2 = spread_call(xs1, first_pairs, flat1, chosen, 1, pairs)
+    xs1 = stack_rows(flat1, 1, pairs)
+    flat2 = spread_call(
+        stack_rows(low1, 1, pairs), xs1, stack_rows(high1, 1, pairs), first_pairs, flat1, chosen, 1, pairs
+    )
     low2, high2 = halos(flat2, "shot")
-    xs2 = stack_flat(flat2, low2, high2, 4, pairs)
+    xs2 = stack_rows(flat2, 4, pairs)
     span = receivers // count
-    whole = spread_call(xs2, second_pairs, flat2, chosen, 4, pairs)
+    whole = spread_call(
+        stack_rows(low2, 4, pairs), xs2, stack_rows(high2, 4, pairs), second_pairs, flat2, chosen, 4, pairs
+    )
     arrived = []
     for shift in range(count):
         target = lax.rem(me + shift, count)

time: 76.2 us -> 72.9 us (0.957)
  other arithmetic: 16.6 us -> 12.5 us
  local copies, waits for them, and re-layouts: 4.85 us -> 8.53 us
  waiting for transfers between devices: 12.5 us -> 10.3 us
  starting transfers between devices: 17.6 us -> 16.8 us
    concatenate x4 -> x6, other arithmetic: 8.41 us -> 4.44 us  [stack_rows(): stacked = jnp.concatenate([before, volume, after], axis=2)]
    unnamed x14 -> x16, local copies, waits for them, and re-layouts: 1.89 us -> 5.85 us
    ppermute x2, waiting for transfers between devices: 2.25 us -> 0.01 us  [halos(): high = lax.ppermute(block[:1], axis, backward)]
    mul x1, other arithmetic: 1.85 us -> 0.69 us  [body(): flat1 = volume * alive.astype(volume.dtype)[:, :, None]]
    slice x4 -> x8, local copies, waits for them, and re-layouts: 2.31 us -> 1.29 us  [the longest x6 1.22 us: stack_rows(): before = jnp.concatenate([blank, volume[:, :-1]], axis=1)]
    select_n x1, other arithmetic: 0.34 us -> 1.3 us  [body(): lax.select_n(lax.rem(me - q + count, count), *by_shift)]
    ppermute x2, starting transfers between devices: 9.07 us -> 8.17 us  [halos(): low = lax.ppermute(block[-1:], axis, forward)]
    select_n x3 -> x7, other arithmetic: 2.53 us -> 3.25 us  [the longest x4 2.58 us: stack_rows(): after = jnp.where(phase == pairs - 1, jnp.zeros_like(after), after)]
  transfers between devices with their start and end apart: 7 -> 7, of which waited for: 5 -> 2; matrix products, arithmetic and copies ran while one was open for 4% -> 12% of each run, Pallas kernels for 0% -> 0%
where the time goes in v7:
time: 72.9 us; the launch traced here: 72.6 us
  Pallas kernels  24.1 us (33%)
  starting transfers between devices  16.8 us (23%)
  other arithmetic  12.5 us (17%)
  waiting for transfers between devices  10.3 us (14%)
  local copies, waits for them, and re-layouts  8.53 us (12%)
    pallas_call x2, Pallas kernels, spread_call(): pl.pallas_call(functools.partial(spread_kernel, dilation=dilation, pairs=...  24.1 us
    ppermute x3, waiting for transfers between devices, body(): piece = lax.ppermute(piece, 'shot', pairs_list)  10.3 us
    ppermute x2, starting transfers between devices, halos(): low = lax.ppermute(block[-1:], axis, forward)  8.17 us
    ppermute x3, starting transfers between devices, body(): piece = lax.ppermute(piece, 'shot', pairs_list)  6.04 us
    unnamed x16, local copies, waits for them, and re-layouts  5.85 us
    concatenate x6, other arithmetic, stack_rows(): stacked = jnp.concatenate([before, volume, after], axis=2)  4.44 us
    select_n x4, other arithmetic, stack_rows(): after = jnp.where(phase == pairs - 1, jnp.zeros_like(after), after)  2.58 us
    ppermute x2, starting transfers between devices, halos(): high = lax.ppermute(block[:1], axis, backward)  2.58 us
  transfers between devices with their start and end apart: 7, of which 2 were waited for; matrix products, arithmetic and copies ran while one was open for 12% of the time, Pallas kernels for 0%

profile of v7, /device:TPU:0, one launch (start us, length us, event | category | flops | bytes accessed | tf_op | source)
XLA Modules:
  0.0 72.6 jit_solution(1452972041082695985)
XLA Ops:
  0.0 0.8 %fusion.23 = s32[4]{0:T(128)S(1)} fusion(s32[16,1]{0,1:T(1,128)} %param.5, s32[]{:T(128)S(6)} %select_n.220), kind=kLoop, calls=%fused_computation.90 | loop fusion | bytes 36 | tf_op jit(solution)/shard_map/dynamic_slice | solution.py:182
  0.8 0.1 compare_convert_fusion
  0.9 0.3 copy-done
  1.2 0.7 bitcast_multiply_fusion.res_ref
  2.0 1.3 %collective-permute-start.1 = (bf16[1,1024,128]{2,1,0:T(8,128)(2,1)S(1)}, bf16[1,1024,128]{2,1,0:T(8,128)(2,1)S(1)}, u32[]{:S(2)}, u32[]{:S(2)}) collective-permute-start(bf16[1,1024,128]{2,1,0:T(8,128)(2,1)S(1)} %get-tuple-element.26), channel_id=1, source_target_pairs={{4,0},{8,4},{12,8},{5,1},{9,5},{13,9},{6,2},{10,6},{14,10},{7,3},{... | collective-permute-start | bytes 786440 | tf_op jit(solution)/shard_map/ppermute | solution.py:108
  3.3 3.0 %collective-permute-start = (bf16[1,1024,128]{2,1,0:T(8,128)(2,1)S(1)}, bf16[1,1024,128]{2,1,0:T(8,128)(2,1)S(1)}, u32[]{:S(2)}, u32[]{:S(2)}) collective-permute-start(bf16[1,1024,128]{2,1,0:T(8,128)(2,1)S(1)} %get-tuple-element.27), channel_id=1, source_target_pairs={{0,4},{4,8},{8,12},{1,5},{5,9},{9,13},{2,6},{6,10},{10,14},{3,7},{... | collective-permute-start | bytes 786440 | tf_op jit(solution)/shard_map/ppermute | solution.py:107
  6.4 0.0 copy-start.5
  6.4 0.4 fusion.27
  6.8 0.9 %copy-done.5 = bf16[5,3,5,64,64]{4,3,2,1,0:T(8,128)(2,1)S(1)} copy-done((bf16[5,3,5,64,64]{4,3,2,1,0:T(8,128)(2,1)S(1)}, bf16[5,3,5,64,64]{4,3,2,1,0:T(8,128)(2,1)}, u32[]{:S(2)}) %copy-start.5) | copy-done | bytes 614424
  7.7 0.1 slice_bitcast_fusion.5
  7.7 0.1 pad_dynamic-update-slice_fusion.3
  7.8 0.0 copy-start.6
  7.8 0.2 maximum_dynamic-update-slice_fusion.3
  8.0 0.2 maximum_dynamic-update-slice_fusion.2
  8.2 0.2 maximum_dynamic-update-slice_fusion.1
  8.4 0.2 maximum_dynamic-update-slice_fusion
  8.5 0.2 pad_dynamic-update-slice_fusion.2
  8.7 0.0 copy-start.3
  8.7 1.1 %copy-done.3 = bf16[5,3,384,128]{3,2,1,0:T(8,128)(2,1)} copy-done((bf16[5,3,384,128]{3,2,1,0:T(8,128)(2,1)}, bf16[5,3,384,128]{3,2,1,0:T(8,128)(2,1)S(1)}, u32[]{:S(2)}) %copy-start.3) | copy-done | bytes 1474584
  9.9 0.1 slice_bitcast_fusion
  10.0 0.1 pad_dynamic-update-slice_fusion.1
  10.0 1.2 %pad_select_fusion.2 = (bf16[4,1024,128]{2,1,0:T(8,128)(2,1)S(1)}, bf16[4,1024,128]{2,1,0:T(8,128)(2,1)S(1)}) fusion(bf16[4,1023,128]{2,1,0:T(8,128)(2,1)S(1)} %get-tuple-element.29, pred[1024]{0:T(1024)(128)(4,1)S(1)} %fusion.19, bf16[4,1023,128]{2,1,0:T(8,128)(2,1)S(1)} %get-tuple-element.28, pred[1024]{0:T(1024)(128)(4,1)S(1)} %fusion.20), kind=kLoop, calls=%fused_computation.27 | loop fusion | flops 1048576 | bytes 4194304 | tf_op jit(solution)/shard_map/jit(_where)/select_n | solution.py:119
  11.2 1.9 %fusion.11.x0_ref.x1_ref.x2_ref = bf16[4,1056,384]{2,1,0:T(8,128)(2,1)} fusion(bf16[4,1024,128]{2,1,0:T(8,128)(2,1)S(1)} %get-tuple-element.48, bf16[4,1024,128]{2,1,0:T(8,128)(2,1)S(1)} %bitcast_multiply_fusion.res_ref, bf16[4,1024,128]{2,1,0:T(8,128)(2,1)S(1)} %get-tuple-element.49), kind=kLoop, calls=%fused_computation.15 | loop fusion | flops 19464192 | bytes 6389760 | tf_op jit(solution)/shard_map/concatenate | solution.py:120
  13.2 0.2 maximum_dynamic-update-slice_fusion.7
  13.4 0.2 maximum_dynamic-update-slice_fusion.6
  13.5 0.2 maximum_dynamic-update-slice_fusion.5
  13.7 0.2 maximum_dynamic-update-slice_fusion.4
  13.9 0.2 pad_dynamic-update-slice_fusion
  14.1 1.1 %copy-done.1 = bf16[5,3,384,128]{3,2,1,0:T(8,128)(2,1)} copy-done((bf16[5,3,384,128]{3,2,1,0:T(8,128)(2,1)}, bf16[5,3,384,128]{3,2,1,0:T(8,128)(2,1)S(1)}, u32[]{:S(2)}) %copy-start.1) | copy-done | bytes 1474584
  15.2 0.1 pad_add_fusion.scalars_ref
  15.3 0.0 collective-permute-done.1
  15.3 0.1 fusion.30
  15.4 0.0 collective-permute-done
  15.4 0.1 fusion.31
  15.5 0.9 %pad_select_fusion.8 = (bf16[1,1024,128]{2,1,0:T(8,128)(2,1)S(1)}, bf16[1,1024,128]{2,1,0:T(8,128)(2,1)S(1)}, bf16[1,1024,128]{2,1,0:T(8,128)(2,1)S(1)}, bf16[1,1024,128]{2,1,0:T(8,128)(2,1)S(1)}) fusion(bf16[1,1023,128]{2,1,0:T(8,128)(2,1)S(1)} %get-tuple-element.35, pred[1024]{0:T(1024)(128)(4,1)S(1)} %fusion.19, ...), kind=kLoop, calls=%fused_computation.47 | loop fusion | flops 524288 | bytes 2098176 | tf_op jit(solution)/shard_map/jit(_where)/select_n | solution.py:119
  16.4 0.1 select_maximum_fusion.4.hi_ref
  16.5 0.1 select_maximum_fusion.6.lo_ref
  16.7 1.1 %copy-done.4 = bf16[5,3,384,128]{3,2,1,0:T(8,128)(2,1)S(1)} copy-done((bf16[5,3,384,128]{3,2,1,0:T(8,128)(2,1)S(1)}, bf16[5,3,384,128]{3,2,1,0:T(8,128)(2,1)}, u32[]{:S(2)}) %copy-start.4) | copy-done | bytes 1474584
  17.8 11.6 %shard_map.46.res_ref = bf16[4,1024,128]{2,1,0:T(8,128)(2,1)S(1)} custom-call(s32[5]{0:T(128)S(1)} %pad_add_fusion.scalars_ref, bf16[1,1056,384]{2,1,0:T(8,128)(2,1)S(1)} %select_maximum_fusion.6.lo_ref, bf16[4,1056,384]{2,1,0:T(8,128)(2,1)} %fusion.11.x0_ref.x1_ref.x2_ref, bf16[4,1056,384]{2,1,0:T(8,128)(2,1)} %fusion.11.x0_ref.x1_ref.x2_ref, ...), custom_call_target="tpu_custom_call" | custom-call | flops 6228541440 | bytes 8437760 | tf_op jit(solution)/shard_map/pallas_call | solution.py:54
  29.4 0.4 fusion.25
  29.8 1.3 %collective-permute-start.3 = (bf16[1,1024,128]{2,1,0:T(8,128)(2,1)S(1)}, bf16[1,1024,128]{2,1,0:T(8,128)(2,1)S(1)}, u32[]{:S(2)}, u32[]{:S(2)}) collective-permute-start(bf16[1,1024,128]{2,1,0:T(8,128)(2,1)S(1)} %get-tuple-element.22), channel_id=1, source_target_pairs={{4,0},{8,4},{12,8},{5,1},{9,5},{13,9},{6,2},{10,6},{14,10},{7,3},{... | collective-permute-start | bytes 786440 | tf_op jit(solution)/shard_map/ppermute | solution.py:108
  31.1 5.1 %collective-permute-start.2 = (bf16[1,1024,128]{2,1,0:T(8,128)(2,1)S(1)}, bf16[1,1024,128]{2,1,0:T(8,128)(2,1)S(1)}, u32[]{:S(2)}, u32[]{:S(2)}) collective-permute-start(bf16[1,1024,128]{2,1,0:T(8,128)(2,1)S(1)} %get-tuple-element.23), channel_id=1, source_target_pairs={{0,4},{4,8},{8,12},{1,5},{5,9},{9,13},{2,6},{6,10},{10,14},{3,7},{... | collective-permute-start | bytes 786440 | tf_op jit(solution)/shard_map/ppermute | solution.py:107
  36.3 0.3 pad_select_fusion
  36.6 0.4 pad_select_fusion.1
  37.0 2.1 %fusion.9.x0_ref.x1_ref.x2_ref = bf16[4,1152,384]{2,1,0:T(8,128)(2,1)} fusion(bf16[4,1024,128]{2,1,0:T(8,128)(2,1)S(1)} %pad_select_fusion, bf16[4,1024,128]{2,1,0:T(8,128)(2,1)S(1)} %shard_map.46.res_ref, bf16[4,1024,128]{2,1,0:T(8,128)(2,1)S(1)} %pad_select_fusion.1), kind=kLoop, calls=%fused_computation.13 | loop fusion | flops 21233664 | bytes 6684672 | tf_op jit(solution)/shard_map/concatenate | solution.py:120
  39.0 0.0 collective-permute-done.3
  39.0 0.1 fusion.28
  39.1 0.0 collective-permute-done.2
  39.1 0.1 fusion.29
  39.2 0.3 pad_select_fusion.5
  39.5 0.2 pad_select_fusion.4
  39.7 0.1 select_maximum_fusion.hi_ref
  39.9 0.1 select_maximum_fusion.2.lo_ref
  40.0 1.1 %copy-done.2 = bf16[5,3,384,128]{3,2,1,0:T(8,128)(2,1)S(1)} copy-done((bf16[5,3,384,128]{3,2,1,0:T(8,128)(2,1)S(1)}, bf16[5,3,384,128]{3,2,1,0:T(8,128)(2,1)}, u32[]{:S(2)}) %copy-start.2) | copy-done | bytes 1474584
  41.1 12.5 %shard_map.47 = bf16[4,1024,128]{2,1,0:T(8,128)(2,1)S(1)} custom-call(s32[5]{0:T(128)S(1)} %pad_add_fusion.scalars_ref, bf16[1,1152,384]{2,1,0:T(8,128)(2,1)S(1)} %select_maximum_fusion.2.lo_ref, bf16[4,1152,384]{2,1,0:T(8,128)(2,1)} %fusion.9.x0_ref.x1_ref.x2_ref, bf16[4,1152,384]{2,1,0:T(8,128)(2,1)} %fusion.9.x0_ref.x1_ref.x2_ref, ...), custom_call_target="tpu_custom_call" | custom-call | flops 6794772480 | bytes 8880128 | tf_op jit(solution)/shard_map/pallas_call | solution.py:54
  53.6 0.1 constant_dynamic-slice_fusion.2
  53.7 2.2 %collective-permute-start.4 = (bf16[4,256,128]{2,1,0:T(8,128)(2,1)S(1)}, bf16[4,256,128]{2,1,0:T(8,128)(2,1)S(1)}, u32[]{:S(2)}, u32[]{:S(2)}) collective-permute-start(bf16[4,256,128]{2,1,0:T(8,128)(2,1)S(1)} %get-tuple-element.19), channel_id=1, source_target_pairs={{0,4},{4,8},{8,12},{12,0},{1,5},{5,9},{9,13},{13,1},{2,6},{6,10},{... | collective-permute-start | bytes 786440 | tf_op jit(solution)/shard_map/ppermute | solution.py:205
  55.9 2.4 %collective-permute-start.5 = (bf16[4,256,128]{2,1,0:T(8,128)(2,1)S(1)}, bf16[4,256,128]{2,1,0:T(8,128)(2,1)S(1)}, u32[]{:S(2)}, u32[]{:S(2)}) collective-permute-start(bf16[4,256,128]{2,1,0:T(8,128)(2,1)S(1)} %get-tuple-element.21), channel_id=1, source_target_pairs={{0,8},{4,12},{8,0},{12,4},{1,9},{5,13},{9,1},{13,5},{2,10},{6,14},... | collective-permute-start | bytes 786440 | tf_op jit(solution)/shard_map/ppermute | solution.py:205
  58.3 1.4 %collective-permute-start.6 = (bf16[4,256,128]{2,1,0:T(8,128)(2,1)S(1)}, bf16[4,256,128]{2,1,0:T(8,128)(2,1)}, u32[]{:S(2)}, u32[]{:S(2)}) collective-permute-start(bf16[4,256,128]{2,1,0:T(8,128)(2,1)S(1)} %get-tuple-element.20), channel_id=1, source_target_pairs={{0,12},{4,0},{8,4},{12,8},{1,13},{5,1},{9,5},{13,9},{2,14},{6,2},{... | collective-permute-start | bytes 786440 | tf_op jit(solution)/shard_map/ppermute | solution.py:205
  59.7 0.0 collective-permute-done.4
  59.7 5.3 %collective-permute-done.5 = bf16[4,256,128]{2,1,0:T(8,128)(2,1)S(1)} collective-permute-done((bf16[4,256,128]{2,1,0:T(8,128)(2,1)S(1)}, bf16[4,256,128]{2,1,0:T(8,128)(2,1)S(1)}, u32[]{:S(2)}, u32[]{:S(2)}) %collective-permute-start.5) | collective-permute-done | bytes 262176 | tf_op jit(solution)/shard_map/ppermute | solution.py:205
  65.0 5.0 %collective-permute-done.6 = bf16[4,256,128]{2,1,0:T(8,128)(2,1)} collective-permute-done((bf16[4,256,128]{2,1,0:T(8,128)(2,1)S(1)}, bf16[4,256,128]{2,1,0:T(8,128)(2,1)}, u32[]{:S(2)}, u32[]{:S(2)}) %collective-permute-start.6) | collective-permute-done | bytes 262176 | tf_op jit(solution)/shard_map/ppermute | solution.py:205
  70.0 1.3 %select_select_fusion.3 = (bf16[4,256,128]{2,1,0:T(8,128)(2,1)S(1)}, bf16[4,256,128]{2,1,0:T(8,128)(2,1)S(1)}, bf16[4,256,128]{2,1,0:T(8,128)(2,1)S(1)}, bf16[4,256,128]{2,1,0:T(8,128)(2,1)S(1)}) fusion(bf16[4,256,128]{2,1,0:T(8,128)(2,1)S(1)} %collective-permute-done.5, bf16[4,256,128]{2,1,0:T(8,128)(2,1)} %collective-permute-done.6, ...), kind=kLoop, calls=%fused_computation.42 | loop fusion | flops 1572864 | bytes 2097168 | tf_op jit(solution)/shard_map/select_n | solution.py:209
  71.3 1.3 %copy_bitcast_fusion = bf16[1,32,16,8,128]{4,3,2,1,0:T(8,128)(2,1)} fusion(bf16[4,256,128]{2,1,0:T(8,128)(2,1)S(1)} %get-tuple-element.6, bf16[4,256,128]{2,1,0:T(8,128)(2,1)S(1)} %get-tuple-element.7, bf16[4,256,128]{2,1,0:T(8,128)(2,1)S(1)} %get-tuple-element.8, bf16[4,256,128]{2,1,0:T(8,128)(2,1)S(1)} %get-tuple-element.5), kind=kLoop, calls=%fused_computation.24 | loop fusion | flops 1572864 | bytes 2097152 | tf_op jit(solution)/shard_map/broadcast_in_dim | solution.py:212
  (10 shorter events, 0.1 us)
Async XLA Ops:
  0.0 1.2 %copy-start = (bf16[1,128,4,8,128]{4,3,2,1,0:T(8,128)(2,1)S(1)}, bf16[1,128,4,8,128]{4,3,2,1,0:T(8,128)(2,1)}, u32[]{:S(2)}) copy-start(bf16[1,128,4,8,128]{4,3,2,1,0:T(8,128)(2,1)} %param.4) | copy-start | bytes 3145732
  2.0 13.3 %collective-permute-start.1 = (bf16[1,1024,128]{2,1,0:T(8,128)(2,1)S(1)}, bf16[1,1024,128]{2,1,0:T(8,128)(2,1)S(1)}, u32[]{:S(2)}, u32[]{:S(2)}) collective-permute-start(bf16[1,1024,128]{2,1,0:T(8,128)(2,1)S(1)} %get-tuple-element.26), channel_id=1, source_target_pairs={{4,0},{8,4},{12,8},{5,1},{9,5},{13,9},{6,2},{10,6},{14,10},{7,3},{... | collective-permute-start | bytes 786440 | tf_op jit(solution)/shard_map/ppermute | solution.py:108
  3.3 12.1 %collective-permute-start = (bf16[1,1024,128]{2,1,0:T(8,128)(2,1)S(1)}, bf16[1,1024,128]{2,1,0:T(8,128)(2,1)S(1)}, u32[]{:S(2)}, u32[]{:S(2)}) collective-permute-start(bf16[1,1024,128]{2,1,0:T(8,128)(2,1)S(1)} %get-tuple-element.27), channel_id=1, source_target_pairs={{0,4},{4,8},{8,12},{1,5},{5,9},{9,13},{2,6},{6,10},{10,14},{3,7},{... | collective-permute-start | bytes 786440 | tf_op jit(solution)/shard_map/ppermute | solution.py:107
  6.4 1.3 %copy-start.5 = (bf16[5,3,5,64,64]{4,3,2,1,0:T(8,128)(2,1)S(1)}, bf16[5,3,5,64,64]{4,3,2,1,0:T(8,128)(2,1)}, u32[]{:S(2)}) copy-start(bf16[5,3,5,64,64]{4,3,2,1,0:T(8,128)(2,1)} %param.6) | copy-start | bytes 1843204
  7.8 2.1 %copy-start.6 = (bf16[5,3,5,64,64]{4,3,2,1,0:T(8,128)(2,1)S(1)}, bf16[5,3,5,64,64]{4,3,2,1,0:T(8,128)(2,1)}, u32[]{:S(2)}) copy-start(bf16[5,3,5,64,64]{4,3,2,1,0:T(8,128)(2,1)} %param.7) | copy-start | bytes 1843204
  8.7 1.2 %copy-start.3 = (bf16[5,3,384,128]{3,2,1,0:T(8,128)(2,1)}, bf16[5,3,384,128]{3,2,1,0:T(8,128)(2,1)S(1)}, u32[]{:S(2)}) copy-start(bf16[5,3,384,128]{3,2,1,0:T(8,128)(2,1)S(1)} %pad_dynamic-update-slice_fusion.2) | copy-start | bytes 4423684
  14.1 1.1 %copy-start.1 = (bf16[5,3,384,128]{3,2,1,0:T(8,128)(2,1)}, bf16[5,3,384,128]{3,2,1,0:T(8,128)(2,1)S(1)}, u32[]{:S(2)}) copy-start(bf16[5,3,384,128]{3,2,1,0:T(8,128)(2,1)S(1)} %pad_dynamic-update-slice_fusion) | copy-start | bytes 4423684
  16.4 1.4 %copy-start.4 = (bf16[5,3,384,128]{3,2,1,0:T(8,128)(2,1)S(1)}, bf16[5,3,384,128]{3,2,1,0:T(8,128)(2,1)}, u32[]{:S(2)}) copy-start(bf16[5,3,384,128]{3,2,1,0:T(8,128)(2,1)} %copy-done.3) | copy-start | bytes 4423684
  29.8 9.2 %collective-permute-start.3 = (bf16[1,1024,128]{2,1,0:T(8,128)(2,1)S(1)}, bf16[1,1024,128]{2,1,0:T(8,128)(2,1)S(1)}, u32[]{:S(2)}, u32[]{:S(2)}) collective-permute-start(bf16[1,1024,128]{2,1,0:T(8,128)(2,1)S(1)} %get-tuple-element.22), channel_id=1, source_target_pairs={{4,0},{8,4},{12,8},{5,1},{9,5},{13,9},{6,2},{10,6},{14,10},{7,3},{... | collective-permute-start | bytes 786440 | tf_op jit(solution)/shard_map/ppermute | solution.py:108
  31.1 8.0 %collective-permute-start.2 = (bf16[1,1024,128]{2,1,0:T(8,128)(2,1)S(1)}, bf16[1,1024,128]{2,1,0:T(8,128)(2,1)S(1)}, u32[]{:S(2)}, u32[]{:S(2)}) collective-permute-start(bf16[1,1024,128]{2,1,0:T(8,128)(2,1)S(1)} %get-tuple-element.23), channel_id=1, source_target_pairs={{0,4},{4,8},{8,12},{1,5},{5,9},{9,13},{2,6},{6,10},{10,14},{3,7},{... | collective-permute-start | bytes 786440 | tf_op jit(solution)/shard_map/ppermute | solution.py:107
  39.7 1.4 %copy-start.2 = (bf16[5,3,384,128]{3,2,1,0:T(8,128)(2,1)S(1)}, bf16[5,3,384,128]{3,2,1,0:T(8,128)(2,1)}, u32[]{:S(2)}) copy-start(bf16[5,3,384,128]{3,2,1,0:T(8,128)(2,1)} %copy-done.1) | copy-start | bytes 4423684
  53.7 6.0 %collective-permute-start.4 = (bf16[4,256,128]{2,1,0:T(8,128)(2,1)S(1)}, bf16[4,256,128]{2,1,0:T(8,128)(2,1)S(1)}, u32[]{:S(2)}, u32[]{:S(2)}) collective-permute-start(bf16[4,256,128]{2,1,0:T(8,128)(2,1)S(1)} %get-tuple-element.19), channel_id=1, source_target_pairs={{0,4},{4,8},{8,12},{12,0},{1,5},{5,9},{9,13},{13,1},{2,6},{6,10},{... | collective-permute-start | bytes 786440 | tf_op jit(solution)/shard_map/ppermute | solution.py:205
  55.9 9.1 %collective-permute-start.5 = (bf16[4,256,128]{2,1,0:T(8,128)(2,1)S(1)}, bf16[4,256,128]{2,1,0:T(8,128)(2,1)S(1)}, u32[]{:S(2)}, u32[]{:S(2)}) collective-permute-start(bf16[4,256,128]{2,1,0:T(8,128)(2,1)S(1)} %get-tuple-element.21), channel_id=1, source_target_pairs={{0,8},{4,12},{8,0},{12,4},{1,9},{5,13},{9,1},{13,5},{2,10},{6,14},... | collective-permute-start | bytes 786440 | tf_op jit(solution)/shard_map/ppermute | solution.py:205
  58.3 11.7 %collective-permute-start.6 = (bf16[4,256,128]{2,1,0:T(8,128)(2,1)S(1)}, bf16[4,256,128]{2,1,0:T(8,128)(2,1)}, u32[]{:S(2)}, u32[]{:S(2)}) collective-permute-start(bf16[4,256,128]{2,1,0:T(8,128)(2,1)S(1)} %get-tuple-element.20), channel_id=1, source_target_pairs={{0,12},{4,0},{8,4},{12,8},{1,13},{5,1},{9,5},{13,9},{2,14},{6,2},{... | collective-permute-start | bytes 786440 | tf_op jit(solution)/shard_map/ppermute | solution.py:205

commit v8 on v7

--- a/solution.py
+++ b/solution.py
@@ -102,10 +102,13 @@
 
 def halos(block, axis):
     count = lax.axis_size(axis)
-    forward = [(i, i + 1) for i in range(count - 1)]
-    backward = [(target, source) for source, target in forward]
+    me = lax.axis_index(axis)
+    forward = [(i, (i + 1) % count) for i in range(count)]
+    backward = [((i + 1) % count, i) for i in range(count)]
     low = lax.ppermute(block[-1:], axis, forward)
     high = lax.ppermute(block[:1], axis, backward)
+    low = jnp.where(me == 0, jnp.zeros_like(low), low)
+    high = jnp.where(me == count - 1, jnp.zeros_like(high), high)
     return low, high
 
 

time: 72.9 us -> 70.5 us (0.967)
  starting transfers between devices: 16.8 us -> 8.32 us
  waiting for transfers between devices: 10.3 us -> 14.2 us
  other arithmetic: 12.5 us -> 15.2 us
  local copies, waits for them, and re-layouts: 8.53 us -> 7.49 us
    ppermute x2, starting transfers between devices: 8.17 us -> 2.05 us  [halos(): low = lax.ppermute(block[-1:], axis, forward)]
    unnamed x8, other arithmetic: 1.43 us -> 4.14 us
    unnamed x16 -> x12, local copies, waits for them, and re-layouts: 5.85 us -> 3.44 us
    ppermute x2, waiting for transfers between devices: 0.01 us -> 2.31 us  [halos(): high = lax.ppermute(block[:1], axis, backward)]
    ppermute x3, starting transfers between devices: 6.04 us -> 4.12 us  [body(): piece = lax.ppermute(piece, 'shot', pairs_list)]
    ppermute x2, waiting for transfers between devices: 0.01 us -> 1.58 us  [halos(): low = lax.ppermute(block[-1:], axis, forward)]
  transfers between devices with their start and end apart: 7 -> 7, of which waited for: 2 -> 5; matrix products, arithmetic and copies ran while one was open for 12% -> 18% of each run, Pallas kernels for 0% -> 0%
where the time goes in v8:
time: 70.5 us; the launch traced here: 70.3 us
  Pallas kernels  24.8 us (35%)
  other arithmetic  15.2 us (22%)
  waiting for transfers between devices  14.2 us (20%)
  starting transfers between devices  8.32 us (12%)
  local copies, waits for them, and re-layouts  7.49 us (11%)
    pallas_call x2, Pallas kernels, spread_call(): pl.pallas_call(functools.partial(spread_kernel, dilation=dilation, pairs=...  24.8 us
    ppermute x3, waiting for transfers between devices, body(): piece = lax.ppermute(piece, 'shot', pairs_list)  10.3 us
    concatenate x6, other arithmetic, stack_rows(): stacked = jnp.concatenate([before, volume, after], axis=2)  4.37 us
    unnamed x8, other arithmetic  4.14 us
    ppermute x3, starting transfers between devices, body(): piece = lax.ppermute(piece, 'shot', pairs_list)  4.12 us
    unnamed x12, local copies, waits for them, and re-layouts  3.44 us
    select_n x4, other arithmetic, stack_rows(): after = jnp.where(phase == pairs - 1, jnp.zeros_like(after), after)  2.55 us
    ppermute x2, waiting for transfers between devices, halos(): high = lax.ppermute(block[:1], axis, backward)  2.31 us
  transfers between devices with their start and end apart: 7, of which 5 were waited for; matrix products, arithmetic and copies ran while one was open for 18% of the time, Pallas kernels for 0%

profile of v8, /device:TPU:0, one launch (start us, length us, event | category | flops | bytes accessed | tf_op | source)
XLA Modules:
  0.0 70.3 jit_solution(5906965255942945942)
XLA Ops:
  0.0 0.0 copy-start
  0.0 0.8 %fusion.23 = s32[4]{0:T(128)S(1)} fusion(s32[16,1]{0,1:T(1,128)} %param.5, s32[]{:T(128)S(6)} %select_n.242), kind=kLoop, calls=%fused_computation.94 | loop fusion | bytes 36 | tf_op jit(solution)/shard_map/dynamic_slice | solution.py:185
  0.8 0.1 compare_convert_fusion
  0.9 0.3 copy-done
  1.2 0.7 bitcast_multiply_fusion.res_ref
  1.9 0.7 %fusion.26 = (bf16[1,1024,128]{2,1,0:T(8,128)(2,1)S(1)}, bf16[1,1024,128]{2,1,0:T(8,128)(2,1)}) fusion(bf16[4,1024,128]{2,1,0:T(8,128)(2,1)S(1)} %bitcast_multiply_fusion.res_ref), kind=kLoop, calls=%fused_computation.98 | loop fusion | bytes 1048576 | tf_op jit(solution)/shard_map/slice | solution.py:109
  2.7 0.5 collective-permute-start
  3.2 1.9 %collective-permute-start.1 = (bf16[1,1024,128]{2,1,0:T(8,128)(2,1)S(1)}, bf16[1,1024,128]{2,1,0:T(8,128)(2,1)S(1)}, u32[]{:S(2)}, u32[]{:S(2)}) collective-permute-start(bf16[1,1024,128]{2,1,0:T(8,128)(2,1)S(1)} %get-tuple-element.26), channel_id=1, source_target_pairs={{4,0},{8,4},{12,8},{0,12},{5,1},{9,5},{13,9},{1,13},{6,2},{10,6},{... | collective-permute-start | bytes 786440 | tf_op jit(solution)/shard_map/ppermute | solution.py:109
  5.1 0.4 fusion.27
  5.5 0.0 copy-done.3
  5.5 0.1 slice_bitcast_fusion.5
  5.6 0.1 pad_dynamic-update-slice_fusion.3
  5.7 0.0 copy-start.4
  5.7 0.2 maximum_dynamic-update-slice_fusion.3
  5.9 0.2 maximum_dynamic-update-slice_fusion.2
  6.1 0.2 maximum_dynamic-update-slice_fusion.1
  6.3 0.2 maximum_dynamic-update-slice_fusion
  6.4 0.2 pad_dynamic-update-slice_fusion.2
  6.6 0.0 copy-start.1
  6.6 1.1 %copy-done.1 = bf16[5,3,384,128]{3,2,1,0:T(8,128)(2,1)} copy-done((bf16[5,3,384,128]{3,2,1,0:T(8,128)(2,1)}, bf16[5,3,384,128]{3,2,1,0:T(8,128)(2,1)S(1)}, u32[]{:S(2)}) %copy-start.1) | copy-done | bytes 1474584
  7.7 0.0 copy-done.4
  7.7 0.1 slice_bitcast_fusion
  7.9 0.8 %pad_dynamic-update-slice_fusion.1 = bf16[5,3,384,128]{3,2,1,0:T(8,128)(2,1)} fusion(bf16[5,3,64,64]{3,2,1,0:T(8,128)(2,1)S(1)} %get-tuple-element.12), kind=kLoop, calls=%fused_computation.68 | loop fusion | bytes 368640
  8.6 1.2 %pad_select_fusion.2 = (bf16[4,1024,128]{2,1,0:T(8,128)(2,1)S(1)}, bf16[4,1024,128]{2,1,0:T(8,128)(2,1)S(1)}) fusion(bf16[4,1023,128]{2,1,0:T(8,128)(2,1)S(1)} %get-tuple-element.29, pred[1024]{0:T(1024)(128)(4,1)S(1)} %fusion.19, bf16[4,1023,128]{2,1,0:T(8,128)(2,1)S(1)} %get-tuple-element.28, pred[1024]{0:T(1024)(128)(4,1)S(1)} %fusion.20), kind=kLoop, calls=%fused_computation.27 | loop fusion | flops 1048576 | bytes 4194304 | tf_op jit(solution)/shard_map/jit(_where)/select_n | solution.py:122
  9.8 1.9 %fusion.11.x0_ref.x1_ref.x2_ref = bf16[4,1056,384]{2,1,0:T(8,128)(2,1)} fusion(bf16[4,1024,128]{2,1,0:T(8,128)(2,1)S(1)} %get-tuple-element.48, bf16[4,1024,128]{2,1,0:T(8,128)(2,1)S(1)} %bitcast_multiply_fusion.res_ref, bf16[4,1024,128]{2,1,0:T(8,128)(2,1)S(1)} %get-tuple-element.49), kind=kLoop, calls=%fused_computation.15 | loop fusion | flops 19464192 | bytes 6389760 | tf_op jit(solution)/shard_map/concatenate | solution.py:123
  11.7 0.9 %maximum_dynamic-update-slice_fusion.7 = bf16[5,3,384,128]{3,2,1,0:T(8,128)(2,1)} fusion(bf16[5,3,384,128]{3,2,1,0:T(8,128)(2,1)} %pad_dynamic-update-slice_fusion.1, bf16[5,3,64,64]{3,2,1,0:T(8,128)(2,1)S(1)} %get-tuple-element.12, bf16[5,3,64,64]{3,2,1,0:T(8,128)(2,1)S(1)} %get-tuple-element.11), kind=kLoop, calls=%fused_computation.62 | loop fusion | flops 491520 | bytes 491520
  12.6 0.9 %maximum_dynamic-update-slice_fusion.6 = bf16[5,3,384,128]{3,2,1,0:T(8,128)(2,1)} fusion(bf16[5,3,384,128]{3,2,1,0:T(8,128)(2,1)} %maximum_dynamic-update-slice_fusion.7, bf16[5,3,64,64]{3,2,1,0:T(8,128)(2,1)S(1)} %get-tuple-element.11, bf16[5,3,64,64]{3,2,1,0:T(8,128)(2,1)S(1)} %get-tuple-element.13), kind=kLoop, calls=%fused_computation.61 | loop fusion | flops 491520 | bytes 491520
  13.4 0.9 %maximum_dynamic-update-slice_fusion.5 = bf16[5,3,384,128]{3,2,1,0:T(8,128)(2,1)} fusion(bf16[5,3,384,128]{3,2,1,0:T(8,128)(2,1)} %maximum_dynamic-update-slice_fusion.6, bf16[5,3,64,64]{3,2,1,0:T(8,128)(2,1)S(1)} %get-tuple-element.13, bf16[5,3,64,64]{3,2,1,0:T(8,128)(2,1)S(1)} %get-tuple-element.10), kind=kLoop, calls=%fused_computation.60 | loop fusion | flops 491520 | bytes 491520
  14.3 0.1 pad_add_fusion.scalars_ref
  14.4 0.8 %maximum_dynamic-update-slice_fusion.4 = bf16[5,3,384,128]{3,2,1,0:T(8,128)(2,1)} fusion(bf16[5,3,384,128]{3,2,1,0:T(8,128)(2,1)} %maximum_dynamic-update-slice_fusion.5, bf16[5,3,64,64]{3,2,1,0:T(8,128)(2,1)S(1)} %get-tuple-element.10, bf16[5,3,64,64]{3,2,1,0:T(8,128)(2,1)S(1)} %get-tuple-element.9), kind=kLoop, calls=%fused_computation.59 | loop fusion | flops 491520 | bytes 491520
  15.2 0.8 %pad_dynamic-update-slice_fusion = bf16[5,3,384,128]{3,2,1,0:T(8,128)(2,1)} fusion(bf16[5,3,384,128]{3,2,1,0:T(8,128)(2,1)} %maximum_dynamic-update-slice_fusion.4, bf16[5,3,64,64]{3,2,1,0:T(8,128)(2,1)S(1)} %get-tuple-element.9), kind=kLoop, calls=%fused_computation.63 | loop fusion | bytes 368640 | tf_op jit(solution)/shard_map/concatenate | solution.py:36
  16.0 0.0 collective-permute-done
  16.1 0.1 fusion.31
  16.2 0.0 collective-permute-done.1
  16.2 0.1 fusion.30
  16.3 0.9 %pad_select_fusion.8 = (bf16[1,1024,128]{2,1,0:T(8,128)(2,1)S(1)}, bf16[1,1024,128]{2,1,0:T(8,128)(2,1)S(1)}, bf16[1,1024,128]{2,1,0:T(8,128)(2,1)S(1)}, bf16[1,1024,128]{2,1,0:T(8,128)(2,1)S(1)}) fusion(bf16[1,1023,128]{2,1,0:T(8,128)(2,1)S(1)} %get-tuple-element.35, pred[1024]{0:T(1024)(128)(4,1)S(1)} %fusion.19, ...), kind=kLoop, calls=%fused_computation.47 | loop fusion | flops 524288 | bytes 2098176 | tf_op jit(solution)/shard_map/jit(_where)/select_n | solution.py:122
  17.2 0.1 select_maximum_fusion.4.hi_ref
  17.3 0.1 select_maximum_fusion.6.lo_ref
  17.5 1.1 %copy-done.2 = bf16[5,3,384,128]{3,2,1,0:T(8,128)(2,1)S(1)} copy-done((bf16[5,3,384,128]{3,2,1,0:T(8,128)(2,1)S(1)}, bf16[5,3,384,128]{3,2,1,0:T(8,128)(2,1)}, u32[]{:S(2)}) %copy-start.2) | copy-done | bytes 1474584
  18.6 11.8 %shard_map.46.res_ref = bf16[4,1024,128]{2,1,0:T(8,128)(2,1)S(1)} custom-call(s32[5]{0:T(128)S(1)} %pad_add_fusion.scalars_ref, bf16[1,1056,384]{2,1,0:T(8,128)(2,1)S(1)} %select_maximum_fusion.6.lo_ref, bf16[4,1056,384]{2,1,0:T(8,128)(2,1)} %fusion.11.x0_ref.x1_ref.x2_ref, bf16[4,1056,384]{2,1,0:T(8,128)(2,1)} %fusion.11.x0_ref.x1_ref.x2_ref, ...), custom_call_target="tpu_custom_call" | custom-call | flops 6228541440 | bytes 8437760 | tf_op jit(solution)/shard_map/pallas_call | solution.py:54
  30.4 0.4 fusion.25
  30.8 1.6 %collective-permute-start.2 = (bf16[1,1024,128]{2,1,0:T(8,128)(2,1)S(1)}, bf16[1,1024,128]{2,1,0:T(8,128)(2,1)S(1)}, u32[]{:S(2)}, u32[]{:S(2)}) collective-permute-start(bf16[1,1024,128]{2,1,0:T(8,128)(2,1)S(1)} %get-tuple-element.23), channel_id=1, source_target_pairs={{0,4},{4,8},{8,12},{12,0},{1,5},{5,9},{9,13},{13,1},{2,6},{6,10},{... | collective-permute-start | bytes 786440 | tf_op jit(solution)/shard_map/ppermute | solution.py:108
  32.4 0.2 collective-permute-start.3
  32.6 0.3 pad_select_fusion
  32.9 0.4 pad_select_fusion.1
  33.3 2.0 %fusion.9.x0_ref.x1_ref.x2_ref = bf16[4,1152,384]{2,1,0:T(8,128)(2,1)} fusion(bf16[4,1024,128]{2,1,0:T(8,128)(2,1)S(1)} %pad_select_fusion, bf16[4,1024,128]{2,1,0:T(8,128)(2,1)S(1)} %shard_map.46.res_ref, bf16[4,1024,128]{2,1,0:T(8,128)(2,1)S(1)} %pad_select_fusion.1), kind=kLoop, calls=%fused_computation.13 | loop fusion | flops 21233664 | bytes 6684672 | tf_op jit(solution)/shard_map/concatenate | solution.py:123
  35.3 1.6 %collective-permute-done.2 = bf16[1,1024,128]{2,1,0:T(8,128)(2,1)S(1)} collective-permute-done((bf16[1,1024,128]{2,1,0:T(8,128)(2,1)S(1)}, bf16[1,1024,128]{2,1,0:T(8,128)(2,1)S(1)}, u32[]{:S(2)}, u32[]{:S(2)}) %collective-permute-start.2) | collective-permute-done | bytes 262176 | tf_op jit(solution)/shard_map/ppermute | solution.py:108
  36.9 0.1 fusion.29
  37.0 2.3 %collective-permute-done.3 = bf16[1,1024,128]{2,1,0:T(8,128)(2,1)S(1)} collective-permute-done((bf16[1,1024,128]{2,1,0:T(8,128)(2,1)S(1)}, bf16[1,1024,128]{2,1,0:T(8,128)(2,1)S(1)}, u32[]{:S(2)}, u32[]{:S(2)}) %collective-permute-start.3) | collective-permute-done | bytes 262176 | tf_op jit(solution)/shard_map/ppermute | solution.py:109
  39.3 0.1 fusion.28
  39.4 0.3 pad_select_fusion.5
  39.7 0.2 pad_select_fusion.4
  39.9 0.1 select_maximum_fusion.hi_ref
  40.1 0.1 select_maximum_fusion.2.lo_ref
  40.2 13.0 %shard_map.47 = bf16[4,1024,128]{2,1,0:T(8,128)(2,1)S(1)} custom-call(s32[5]{0:T(128)S(1)} %pad_add_fusion.scalars_ref, bf16[1,1152,384]{2,1,0:T(8,128)(2,1)S(1)} %select_maximum_fusion.2.lo_ref, bf16[4,1152,384]{2,1,0:T(8,128)(2,1)} %fusion.9.x0_ref.x1_ref.x2_ref, bf16[4,1152,384]{2,1,0:T(8,128)(2,1)} %fusion.9.x0_ref.x1_ref.x2_ref, ...), custom_call_target="tpu_custom_call" | custom-call | flops 6794772480 | bytes 8880128 | tf_op jit(solution)/shard_map/pallas_call | solution.py:54
  53.2 0.1 constant_dynamic-slice_fusion.2
  53.3 0.3 collective-permute-start.4
  53.6 2.4 %collective-permute-start.5 = (bf16[4,256,128]{2,1,0:T(8,128)(2,1)S(1)}, bf16[4,256,128]{2,1,0:T(8,128)(2,1)S(1)}, u32[]{:S(2)}, u32[]{:S(2)}) collective-permute-start(bf16[4,256,128]{2,1,0:T(8,128)(2,1)S(1)} %get-tuple-element.21), channel_id=1, source_target_pairs={{0,8},{4,12},{8,0},{12,4},{1,9},{5,13},{9,1},{13,5},{2,10},{6,14},... | collective-permute-start | bytes 786440 | tf_op jit(solution)/shard_map/ppermute | solution.py:208
  56.0 1.4 %collective-permute-start.6 = (bf16[4,256,128]{2,1,0:T(8,128)(2,1)S(1)}, bf16[4,256,128]{2,1,0:T(8,128)(2,1)}, u32[]{:S(2)}, u32[]{:S(2)}) collective-permute-start(bf16[4,256,128]{2,1,0:T(8,128)(2,1)S(1)} %get-tuple-element.20), channel_id=1, source_target_pairs={{0,12},{4,0},{8,4},{12,8},{1,13},{5,1},{9,5},{13,9},{2,14},{6,2},{... | collective-permute-start | bytes 786440 | tf_op jit(solution)/shard_map/ppermute | solution.py:208
  57.4 4.2 %collective-permute-done.4 = bf16[4,256,128]{2,1,0:T(8,128)(2,1)S(1)} collective-permute-done((bf16[4,256,128]{2,1,0:T(8,128)(2,1)S(1)}, bf16[4,256,128]{2,1,0:T(8,128)(2,1)S(1)}, u32[]{:S(2)}, u32[]{:S(2)}) %collective-permute-start.4) | collective-permute-done | bytes 262176 | tf_op jit(solution)/shard_map/ppermute | solution.py:208
  61.6 1.6 %collective-permute-done.5 = bf16[4,256,128]{2,1,0:T(8,128)(2,1)S(1)} collective-permute-done((bf16[4,256,128]{2,1,0:T(8,128)(2,1)S(1)}, bf16[4,256,128]{2,1,0:T(8,128)(2,1)S(1)}, u32[]{:S(2)}, u32[]{:S(2)}) %collective-permute-start.5) | collective-permute-done | bytes 262176 | tf_op jit(solution)/shard_map/ppermute | solution.py:208
  63.2 4.5 %collective-permute-done.6 = bf16[4,256,128]{2,1,0:T(8,128)(2,1)} collective-permute-done((bf16[4,256,128]{2,1,0:T(8,128)(2,1)S(1)}, bf16[4,256,128]{2,1,0:T(8,128)(2,1)}, u32[]{:S(2)}, u32[]{:S(2)}) %collective-permute-start.6) | collective-permute-done | bytes 262176 | tf_op jit(solution)/shard_map/ppermute | solution.py:208
  67.7 1.3 %select_select_fusion.3 = (bf16[4,256,128]{2,1,0:T(8,128)(2,1)S(1)}, bf16[4,256,128]{2,1,0:T(8,128)(2,1)S(1)}, bf16[4,256,128]{2,1,0:T(8,128)(2,1)S(1)}, bf16[4,256,128]{2,1,0:T(8,128)(2,1)S(1)}) fusion(bf16[4,256,128]{2,1,0:T(8,128)(2,1)S(1)} %collective-permute-done.5, bf16[4,256,128]{2,1,0:T(8,128)(2,1)} %collective-permute-done.6, ...), kind=kLoop, calls=%fused_computation.42 | loop fusion | flops 1572864 | bytes 2097168 | tf_op jit(solution)/shard_map/select_n | solution.py:212
  69.0 1.3 %copy_bitcast_fusion = bf16[1,32,16,8,128]{4,3,2,1,0:T(8,128)(2,1)} fusion(bf16[4,256,128]{2,1,0:T(8,128)(2,1)S(1)} %get-tuple-element.6, bf16[4,256,128]{2,1,0:T(8,128)(2,1)S(1)} %get-tuple-element.7, bf16[4,256,128]{2,1,0:T(8,128)(2,1)S(1)} %get-tuple-element.8, bf16[4,256,128]{2,1,0:T(8,128)(2,1)S(1)} %get-tuple-element.5), kind=kLoop, calls=%fused_computation.24 | loop fusion | flops 1572864 | bytes 2097152 | tf_op jit(solution)/shard_map/broadcast_in_dim | solution.py:215
  (10 shorter events, 0.1 us)
Async XLA Ops:
  0.0 1.2 %copy-start = (bf16[1,128,4,8,128]{4,3,2,1,0:T(8,128)(2,1)S(1)}, bf16[1,128,4,8,128]{4,3,2,1,0:T(8,128)(2,1)}, u32[]{:S(2)}) copy-start(bf16[1,128,4,8,128]{4,3,2,1,0:T(8,128)(2,1)} %param.4) | copy-start | bytes 3145732
  2.7 13.4 %collective-permute-start = (bf16[1,1024,128]{2,1,0:T(8,128)(2,1)}, bf16[1,1024,128]{2,1,0:T(8,128)(2,1)S(1)}, u32[]{:S(2)}, u32[]{:S(2)}) collective-permute-start(bf16[1,1024,128]{2,1,0:T(8,128)(2,1)} %get-tuple-element.27), channel_id=1, source_target_pairs={{0,4},{4,8},{8,12},{12,0},{1,5},{5,9},{9,13},{13,1},{2,6},{6,10},{... | collective-permute-start | bytes 786440 | tf_op jit(solution)/shard_map/ppermute | solution.py:108
  3.2 2.4 %copy-start.3 = (bf16[5,3,5,64,64]{4,3,2,1,0:T(8,128)(2,1)S(1)}, bf16[5,3,5,64,64]{4,3,2,1,0:T(8,128)(2,1)}, u32[]{:S(2)}) copy-start(bf16[5,3,5,64,64]{4,3,2,1,0:T(8,128)(2,1)} %param.6) | copy-start | bytes 1843204
  3.2 13.0 %collective-permute-start.1 = (bf16[1,1024,128]{2,1,0:T(8,128)(2,1)S(1)}, bf16[1,1024,128]{2,1,0:T(8,128)(2,1)S(1)}, u32[]{:S(2)}, u32[]{:S(2)}) collective-permute-start(bf16[1,1024,128]{2,1,0:T(8,128)(2,1)S(1)} %get-tuple-element.26), channel_id=1, source_target_pairs={{4,0},{8,4},{12,8},{0,12},{5,1},{9,5},{13,9},{1,13},{6,2},{10,6},{... | collective-permute-start | bytes 786440 | tf_op jit(solution)/shard_map/ppermute | solution.py:109
  5.7 2.0 %copy-start.4 = (bf16[5,3,5,64,64]{4,3,2,1,0:T(8,128)(2,1)S(1)}, bf16[5,3,5,64,64]{4,3,2,1,0:T(8,128)(2,1)}, u32[]{:S(2)}) copy-start(bf16[5,3,5,64,64]{4,3,2,1,0:T(8,128)(2,1)} %param.7) | copy-start | bytes 1843204
  6.6 1.1 %copy-start.1 = (bf16[5,3,384,128]{3,2,1,0:T(8,128)(2,1)}, bf16[5,3,384,128]{3,2,1,0:T(8,128)(2,1)S(1)}, u32[]{:S(2)}) copy-start(bf16[5,3,384,128]{3,2,1,0:T(8,128)(2,1)S(1)} %pad_dynamic-update-slice_fusion.2) | copy-start | bytes 4423684
  17.2 1.4 %copy-start.2 = (bf16[5,3,384,128]{3,2,1,0:T(8,128)(2,1)S(1)}, bf16[5,3,384,128]{3,2,1,0:T(8,128)(2,1)}, u32[]{:S(2)}) copy-start(bf16[5,3,384,128]{3,2,1,0:T(8,128)(2,1)} %copy-done.1) | copy-start | bytes 4423684
  30.8 6.1 %collective-permute-start.2 = (bf16[1,1024,128]{2,1,0:T(8,128)(2,1)S(1)}, bf16[1,1024,128]{2,1,0:T(8,128)(2,1)S(1)}, u32[]{:S(2)}, u32[]{:S(2)}) collective-permute-start(bf16[1,1024,128]{2,1,0:T(8,128)(2,1)S(1)} %get-tuple-element.23), channel_id=1, source_target_pairs={{0,4},{4,8},{8,12},{12,0},{1,5},{5,9},{9,13},{13,1},{2,6},{6,10},{... | collective-permute-start | bytes 786440 | tf_op jit(solution)/shard_map/ppermute | solution.py:108
  32.4 6.9 %collective-permute-start.3 = (bf16[1,1024,128]{2,1,0:T(8,128)(2,1)S(1)}, bf16[1,1024,128]{2,1,0:T(8,128)(2,1)S(1)}, u32[]{:S(2)}, u32[]{:S(2)}) collective-permute-start(bf16[1,1024,128]{2,1,0:T(8,128)(2,1)S(1)} %get-tuple-element.22), channel_id=1, source_target_pairs={{4,0},{8,4},{12,8},{0,12},{5,1},{9,5},{13,9},{1,13},{6,2},{10,6},{... | collective-permute-start | bytes 786440 | tf_op jit(solution)/shard_map/ppermute | solution.py:109
  53.3 8.3 %collective-permute-start.4 = (bf16[4,256,128]{2,1,0:T(8,128)(2,1)S(1)}, bf16[4,256,128]{2,1,0:T(8,128)(2,1)S(1)}, u32[]{:S(2)}, u32[]{:S(2)}) collective-permute-start(bf16[4,256,128]{2,1,0:T(8,128)(2,1)S(1)} %get-tuple-element.19), channel_id=1, source_target_pairs={{0,4},{4,8},{8,12},{12,0},{1,5},{5,9},{9,13},{13,1},{2,6},{6,10},{... | collective-permute-start | bytes 786440 | tf_op jit(solution)/shard_map/ppermute | solution.py:208
  53.6 9.6 %collective-permute-start.5 = (bf16[4,256,128]{2,1,0:T(8,128)(2,1)S(1)}, bf16[4,256,128]{2,1,0:T(8,128)(2,1)S(1)}, u32[]{:S(2)}, u32[]{:S(2)}) collective-permute-start(bf16[4,256,128]{2,1,0:T(8,128)(2,1)S(1)} %get-tuple-element.21), channel_id=1, source_target_pairs={{0,8},{4,12},{8,0},{12,4},{1,9},{5,13},{9,1},{13,5},{2,10},{6,14},... | collective-permute-start | bytes 786440 | tf_op jit(solution)/shard_map/ppermute | solution.py:208
  56.0 11.7 %collective-permute-start.6 = (bf16[4,256,128]{2,1,0:T(8,128)(2,1)S(1)}, bf16[4,256,128]{2,1,0:T(8,128)(2,1)}, u32[]{:S(2)}, u32[]{:S(2)}) collective-permute-start(bf16[4,256,128]{2,1,0:T(8,128)(2,1)S(1)} %get-tuple-element.20), channel_id=1, source_target_pairs={{0,12},{4,0},{8,4},{12,8},{1,13},{5,1},{9,5},{13,9},{2,14},{6,2},{... | collective-permute-start | bytes 786440 | tf_op jit(solution)/shard_map/ppermute | solution.py:208

commit v9 on v8

--- a/solution.py
+++ b/solution.py
@@ -20,22 +20,10 @@
 
 
 def pair_weights(weight):
-    channels = weight.shape[3]
-    zeroed = jnp.zeros(weight.shape[:2] + (channels, channels), weight.dtype)
-    row_blocks = []
-    for time_step in range(3):
-        for in_phase in range(2):
-            column_blocks = []
-            for out_phase in range(2):
-                tap_time = 2 * time_step + in_phase - out_phase
-                if 0 <= tap_time <= 4:
-                    column_blocks.append(weight[:, :, tap_time])
-                else:
-                    column_blocks.append(zeroed)
-            row_blocks.append(jnp.concatenate(column_blocks, axis=3))
-    stacked = jnp.concatenate(row_blocks, axis=2)
-    return stacked.reshape((-1,) + stacked.shape[2:])
-
+    ahead = jnp.pad(weight, ((0, 0), (0, 0), (0, 1), (0, 0), (0, 0)))
+    behind = jnp.pad(weight, ((0, 0), (0, 0), (1, 0), (0, 0), (0, 0)))
+    joined = jnp.concatenate([ahead, behind], axis=4)
+    return joined.reshape(weight.shape[0] * weight.shape[1], -1, joined.shape[4])
 
 def stack_time(block, dilation):
     pairs = block.shape[2]

time: 70.5 us -> 69.8 us (0.990)
  local copies, waits for them, and re-layouts: 7.49 us -> 5.44 us
  other arithmetic: 15.2 us -> 16.6 us
  waiting for transfers between devices: 14.2 us -> 13.2 us
  starting transfers between devices: 8.32 us -> 9.28 us
    concatenate x0 -> x2, other arithmetic: none -> 4.61 us  [pair_weights(): joined = jnp.concatenate([ahead, behind], axis=4)]
    unnamed x8 -> x0, other arithmetic: 4.14 us -> none
    unnamed x12 -> x8, local copies, waits for them, and re-layouts: 3.44 us -> 1.49 us
    concatenate x2 -> x0, local copies, waits for them, and re-layouts: 0.99 us -> none  [pair_weights(): stacked = jnp.concatenate(row_blocks, axis=2)]
    slice x6, local copies, waits for them, and re-layouts: 1.22 us -> 2.19 us  [stack_rows(): before = jnp.concatenate([blank, volume[:, :-1]], axis=1)]
    select_n x2, other arithmetic: 0.05 us -> 1 us  [halos(): high = jnp.where(me == count - 1, jnp.zeros_like(high), high)]
    ppermute x3, starting transfers between devices: 4.12 us -> 5.07 us  [body(): piece = lax.ppermute(piece, 'shot', pairs_list)]
    ppermute x2, waiting for transfers between devices: 2.31 us -> 1.6 us  [halos(): high = lax.ppermute(block[:1], axis, backward)]
  transfers between devices with their start and end apart: 7 -> 7, of which waited for: 5 -> 5; matrix products, arithmetic and copies ran while one was open for 18% -> 17% of each run, Pallas kernels for 0% -> 0%
where the time goes in v9:
time: 69.8 us; the launch traced here: 69.1 us
  Pallas kernels  24.3 us (35%)
  other arithmetic  16.6 us (24%)
  waiting for transfers between devices  13.2 us (19%)
  starting transfers between devices  9.28 us (13%)
  local copies, waits for them, and re-layouts  5.44 us (8%)
    pallas_call x2, Pallas kernels, spread_call(): pl.pallas_call(functools.partial(spread_kernel, dilation=dilation, pairs=...  24.3 us
    ppermute x3, waiting for transfers between devices, body(): piece = lax.ppermute(piece, 'shot', pairs_list)  10.3 us
    ppermute x3, starting transfers between devices, body(): piece = lax.ppermute(piece, 'shot', pairs_list)  5.07 us
    concatenate x2, other arithmetic, pair_weights(): joined = jnp.concatenate([ahead, behind], axis=4)  4.61 us
    concatenate x6, other arithmetic, stack_rows(): stacked = jnp.concatenate([before, volume, after], axis=2)  4.34 us
    select_n x4, other arithmetic, stack_rows(): after = jnp.where(phase == pairs - 1, jnp.zeros_like(after), after)  2.54 us
    slice x6, local copies, waits for them, and re-layouts, stack_rows(): before = jnp.concatenate([blank, volume[:, :-1]], axis=1)  2.19 us
    ppermute x2, starting transfers between devices, halos(): low = lax.ppermute(block[-1:], axis, forward)  2.15 us
  transfers between devices with their start and end apart: 7, of which 5 were waited for; matrix products, arithmetic and copies ran while one was open for 17% of the time, Pallas kernels for 0%

profile of v9, /device:TPU:0, one launch (start us, length us, event | category | flops | bytes accessed | tf_op | source)
XLA Modules:
  0.0 69.1 jit_solution(11647481873188309454)
XLA Ops:
  0.0 0.0 copy-start
  0.0 0.8 %fusion.29 = s32[4]{0:T(128)S(1)} fusion(s32[16,1]{0,1:T(1,128)} %param.5, s32[]{:T(128)S(6)} %select_n.242), kind=kLoop, calls=%fused_computation.80 | loop fusion | bytes 36 | tf_op jit(solution)/shard_map/dynamic_slice | solution.py:173
  0.8 0.1 compare_convert_fusion
  0.9 0.3 copy-done
  1.2 0.7 %bitcast_multiply_fusion.res_ref = bf16[4,1024,128]{2,1,0:T(8,128)(2,1)S(1)} fusion(bf16[4,1024]{1,0:T(4,128)(2,1)S(1)} %compare_convert_fusion, bf16[1,128,4,8,128]{4,3,2,1,0:T(8,128)(2,1)S(1)} %copy-done), kind=kLoop, calls=%fused_computation.31 | loop fusion | flops 2097152 | bytes 2105344 | tf_op jit(solution)/shard_map/mul | solution.py:178
  1.9 0.8 %fusion.32 = (bf16[1,1024,128]{2,1,0:T(8,128)(2,1)}, bf16[1,1024,128]{2,1,0:T(8,128)(2,1)}) fusion(bf16[4,1024,128]{2,1,0:T(8,128)(2,1)S(1)} %bitcast_multiply_fusion.res_ref), kind=kLoop, calls=%fused_computation.84 | loop fusion | bytes 1048576 | tf_op jit(solution)/shard_map/slice | solution.py:97
  2.8 0.5 collective-permute-start
  3.3 1.9 %collective-permute-start.1 = (bf16[1,1024,128]{2,1,0:T(8,128)(2,1)}, bf16[1,1024,128]{2,1,0:T(8,128)(2,1)}, u32[]{:S(2)}, u32[]{:S(2)}) collective-permute-start(bf16[1,1024,128]{2,1,0:T(8,128)(2,1)} %get-tuple-element.16), channel_id=1, source_target_pairs={{4,0},{8,4},{12,8},{0,12},{5,1},{9,5},{13,9},{1,13},{6,2},{10,6},{... | collective-permute-start | bytes 786440 | tf_op jit(solution)/shard_map/ppermute | solution.py:97
  5.2 1.4 %fusion.33 = (bf16[4,1023,128]{2,1,0:T(8,128)(2,1)S(1)}, bf16[4,1023,128]{2,1,0:T(8,128)(2,1)}) fusion(bf16[4,1024,128]{2,1,0:T(8,128)(2,1)S(1)} %bitcast_multiply_fusion.res_ref), kind=kLoop, calls=%fused_computation.85 | loop fusion | bytes 4190208 | tf_op jit(solution)/shard_map/slice | solution.py:107
  6.6 0.0 copy-start.2
  6.6 3.7 %fusion.18 = bf16[5,3,6,64,128]{4,3,2,1,0:T(8,128)(2,1)} fusion(bf16[5,3,5,64,64]{4,3,2,1,0:T(8,128)(2,1)} %param.6), kind=kLoop, calls=%fused_computation.28 | loop fusion | flops 5898240 | bytes 2088960 | tf_op jit(solution)/shard_map/concatenate | solution.py:25
  10.4 0.0 copy-done.2
  10.4 1.2 %pad_select_fusion.2 = (bf16[4,1024,128]{2,1,0:T(8,128)(2,1)S(1)}, bf16[4,1024,128]{2,1,0:T(8,128)(2,1)S(1)}) fusion(bf16[4,1023,128]{2,1,0:T(8,128)(2,1)S(1)} %copy-done.2, pred[1024]{0:T(1024)(128)(4,1)S(1)} %fusion.25, bf16[4,1023,128]{2,1,0:T(8,128)(2,1)S(1)} %get-tuple-element.18, pred[1024]{0:T(1024)(128)(4,1)S(1)} %fusion.26), kind=kLoop, calls=%fused_computation.35 | loop fusion | flops 1048576 | bytes 4194304 | tf_op jit(solution)/shard_map/jit(_where)/select_n | solution.py:110
  11.5 0.0 copy-start.3
  11.6 1.9 %fusion.11.x0_ref.x1_ref.x2_ref = bf16[4,1056,384]{2,1,0:T(8,128)(2,1)} fusion(bf16[4,1024,128]{2,1,0:T(8,128)(2,1)S(1)} %get-tuple-element.38, bf16[4,1024,128]{2,1,0:T(8,128)(2,1)S(1)} %bitcast_multiply_fusion.res_ref, bf16[4,1024,128]{2,1,0:T(8,128)(2,1)S(1)} %get-tuple-element.39), kind=kLoop, calls=%fused_computation.15 | loop fusion | flops 19464192 | bytes 6389760 | tf_op jit(solution)/shard_map/concatenate | solution.py:111
  13.5 0.1 pad_add_fusion.scalars_ref
  13.5 0.0 copy-done.3
  13.5 0.9 %fusion.19 = bf16[5,3,6,64,128]{4,3,2,1,0:T(8,128)(2,1)S(1)} fusion(bf16[5,3,5,64,64]{4,3,2,1,0:T(8,128)(2,1)S(1)} %copy-done.3), kind=kLoop, calls=%fused_computation.29 | loop fusion | flops 5898240 | bytes 2088960 | tf_op jit(solution)/shard_map/concatenate | solution.py:25
  14.4 0.0 collective-permute-done
  14.5 0.1 fusion.37
  14.6 0.0 collective-permute-done.1
  14.6 1.0 %broadcast_select_fusion.1 = bf16[1,1024,128]{2,1,0:T(8,128)(2,1)S(1)} fusion(bf16[1,1024,128]{2,1,0:T(8,128)(2,1)} %collective-permute-done.1, pred[]{:T(512)S(6)} %eq.62), kind=kLoop, calls=%fused_computation.60 | loop fusion | flops 131072 | bytes 524289 | tf_op jit(solution)/shard_map/jit(_where)/select_n | solution.py:99
  15.6 0.1 fusion.36
  15.7 0.9 %pad_select_fusion.8 = (bf16[1,1024,128]{2,1,0:T(8,128)(2,1)S(1)}, bf16[1,1024,128]{2,1,0:T(8,128)(2,1)S(1)}, bf16[1,1024,128]{2,1,0:T(8,128)(2,1)S(1)}, bf16[1,1024,128]{2,1,0:T(8,128)(2,1)S(1)}) fusion(bf16[1,1023,128]{2,1,0:T(8,128)(2,1)S(1)} %get-tuple-element.25, pred[1024]{0:T(1024)(128)(4,1)S(1)} %fusion.25, ...), kind=kLoop, calls=%fused_computation.55 | loop fusion | flops 524288 | bytes 2098176 | tf_op jit(solution)/shard_map/jit(_where)/select_n | solution.py:110
  16.6 0.0 copy-start.1
  16.6 0.1 select_maximum_fusion.4.hi_ref
  16.7 0.1 select_maximum_fusion.6.lo_ref
  16.8 1.1 %copy-done.1 = bf16[5,3,6,64,128]{4,3,2,1,0:T(8,128)(2,1)S(1)} copy-done((bf16[5,3,6,64,128]{4,3,2,1,0:T(8,128)(2,1)S(1)}, bf16[5,3,6,64,128]{4,3,2,1,0:T(8,128)(2,1)}, u32[]{:S(2)}) %copy-start.1) | copy-done | bytes 1474584
  17.9 11.7 %shard_map.46.res_ref = bf16[4,1024,128]{2,1,0:T(8,128)(2,1)S(1)} custom-call(s32[5]{0:T(128)S(1)} %pad_add_fusion.scalars_ref, bf16[1,1056,384]{2,1,0:T(8,128)(2,1)S(1)} %select_maximum_fusion.6.lo_ref, bf16[4,1056,384]{2,1,0:T(8,128)(2,1)} %fusion.11.x0_ref.x1_ref.x2_ref, bf16[4,1056,384]{2,1,0:T(8,128)(2,1)} %fusion.11.x0_ref.x1_ref.x2_ref, ...), custom_call_target="tpu_custom_call" | custom-call | flops 6228541440 | bytes 8437760 | tf_op jit(solution)/shard_map/pallas_call | solution.py:42
  29.7 0.4 fusion.31
  30.1 1.7 %collective-permute-start.2 = (bf16[1,1024,128]{2,1,0:T(8,128)(2,1)S(1)}, bf16[1,1024,128]{2,1,0:T(8,128)(2,1)S(1)}, u32[]{:S(2)}, u32[]{:S(2)}) collective-permute-start(bf16[1,1024,128]{2,1,0:T(8,128)(2,1)S(1)} %get-tuple-element.13), channel_id=1, source_target_pairs={{0,4},{4,8},{8,12},{12,0},{1,5},{5,9},{9,13},{13,1},{2,6},{6,10},{... | collective-permute-start | bytes 786440 | tf_op jit(solution)/shard_map/ppermute | solution.py:96
  31.8 0.1 collective-permute-start.3
  31.9 0.3 pad_select_fusion
  32.2 0.4 pad_select_fusion.1
  32.6 2.0 %fusion.9.x0_ref.x1_ref.x2_ref = bf16[4,1152,384]{2,1,0:T(8,128)(2,1)} fusion(bf16[4,1024,128]{2,1,0:T(8,128)(2,1)S(1)} %pad_select_fusion, bf16[4,1024,128]{2,1,0:T(8,128)(2,1)S(1)} %shard_map.46.res_ref, bf16[4,1024,128]{2,1,0:T(8,128)(2,1)S(1)} %pad_select_fusion.1), kind=kLoop, calls=%fused_computation.13 | loop fusion | flops 21233664 | bytes 6684672 | tf_op jit(solution)/shard_map/concatenate | solution.py:111
  34.6 1.4 %collective-permute-done.2 = bf16[1,1024,128]{2,1,0:T(8,128)(2,1)S(1)} collective-permute-done((bf16[1,1024,128]{2,1,0:T(8,128)(2,1)S(1)}, bf16[1,1024,128]{2,1,0:T(8,128)(2,1)S(1)}, u32[]{:S(2)}, u32[]{:S(2)}) %collective-permute-start.2) | collective-permute-done | bytes 262176 | tf_op jit(solution)/shard_map/ppermute | solution.py:96
  36.0 0.1 fusion.35
  36.1 1.6 %collective-permute-done.3 = bf16[1,1024,128]{2,1,0:T(8,128)(2,1)S(1)} collective-permute-done((bf16[1,1024,128]{2,1,0:T(8,128)(2,1)S(1)}, bf16[1,1024,128]{2,1,0:T(8,128)(2,1)S(1)}, u32[]{:S(2)}, u32[]{:S(2)}) %collective-permute-start.3) | collective-permute-done | bytes 262176 | tf_op jit(solution)/shard_map/ppermute | solution.py:97
  37.7 0.1 fusion.34
  37.8 0.3 pad_select_fusion.5
  38.1 0.2 pad_select_fusion.4
  38.3 0.1 select_maximum_fusion.hi_ref
  38.4 0.1 select_maximum_fusion.2.lo_ref
  38.5 12.6 %shard_map.47 = bf16[4,1024,128]{2,1,0:T(8,128)(2,1)S(1)} custom-call(s32[5]{0:T(128)S(1)} %pad_add_fusion.scalars_ref, bf16[1,1152,384]{2,1,0:T(8,128)(2,1)S(1)} %select_maximum_fusion.2.lo_ref, bf16[4,1152,384]{2,1,0:T(8,128)(2,1)} %fusion.9.x0_ref.x1_ref.x2_ref, bf16[4,1152,384]{2,1,0:T(8,128)(2,1)} %fusion.9.x0_ref.x1_ref.x2_ref, ...), custom_call_target="tpu_custom_call" | custom-call | flops 6794772480 | bytes 8880128 | tf_op jit(solution)/shard_map/pallas_call | solution.py:42
  51.1 0.1 constant_dynamic-slice_fusion.2
  51.2 1.7 %collective-permute-start.4 = (bf16[4,256,128]{2,1,0:T(8,128)(2,1)S(1)}, bf16[4,256,128]{2,1,0:T(8,128)(2,1)S(1)}, u32[]{:S(2)}, u32[]{:S(2)}) collective-permute-start(bf16[4,256,128]{2,1,0:T(8,128)(2,1)S(1)} %get-tuple-element.9), channel_id=1, source_target_pairs={{0,4},{4,8},{8,12},{12,0},{1,5},{5,9},{9,13},{13,1},{2,6},{6,10},{... | collective-permute-start | bytes 786440 | tf_op jit(solution)/shard_map/ppermute | solution.py:196
  52.9 2.0 %collective-permute-start.5 = (bf16[4,256,128]{2,1,0:T(8,128)(2,1)S(1)}, bf16[4,256,128]{2,1,0:T(8,128)(2,1)S(1)}, u32[]{:S(2)}, u32[]{:S(2)}) collective-permute-start(bf16[4,256,128]{2,1,0:T(8,128)(2,1)S(1)} %get-tuple-element.11), channel_id=1, source_target_pairs={{0,8},{4,12},{8,0},{12,4},{1,9},{5,13},{9,1},{13,5},{2,10},{6,14},... | collective-permute-start | bytes 786440 | tf_op jit(solution)/shard_map/ppermute | solution.py:196
  54.9 1.4 %collective-permute-start.6 = (bf16[4,256,128]{2,1,0:T(8,128)(2,1)S(1)}, bf16[4,256,128]{2,1,0:T(8,128)(2,1)}, u32[]{:S(2)}, u32[]{:S(2)}) collective-permute-start(bf16[4,256,128]{2,1,0:T(8,128)(2,1)S(1)} %get-tuple-element.10), channel_id=1, source_target_pairs={{0,12},{4,0},{8,4},{12,8},{1,13},{5,1},{9,5},{13,9},{2,14},{6,2},{... | collective-permute-start | bytes 786440 | tf_op jit(solution)/shard_map/ppermute | solution.py:196
  56.3 2.3 %collective-permute-done.4 = bf16[4,256,128]{2,1,0:T(8,128)(2,1)S(1)} collective-permute-done((bf16[4,256,128]{2,1,0:T(8,128)(2,1)S(1)}, bf16[4,256,128]{2,1,0:T(8,128)(2,1)S(1)}, u32[]{:S(2)}, u32[]{:S(2)}) %collective-permute-start.4) | collective-permute-done | bytes 262176 | tf_op jit(solution)/shard_map/ppermute | solution.py:196
  58.6 3.5 %collective-permute-done.5 = bf16[4,256,128]{2,1,0:T(8,128)(2,1)S(1)} collective-permute-done((bf16[4,256,128]{2,1,0:T(8,128)(2,1)S(1)}, bf16[4,256,128]{2,1,0:T(8,128)(2,1)S(1)}, u32[]{:S(2)}, u32[]{:S(2)}) %collective-permute-start.5) | collective-permute-done | bytes 262176 | tf_op jit(solution)/shard_map/ppermute | solution.py:196
  62.1 4.5 %collective-permute-done.6 = bf16[4,256,128]{2,1,0:T(8,128)(2,1)} collective-permute-done((bf16[4,256,128]{2,1,0:T(8,128)(2,1)S(1)}, bf16[4,256,128]{2,1,0:T(8,128)(2,1)}, u32[]{:S(2)}, u32[]{:S(2)}) %collective-permute-start.6) | collective-permute-done | bytes 262176 | tf_op jit(solution)/shard_map/ppermute | solution.py:196
  66.6 1.3 %select_select_fusion.3 = (bf16[4,256,128]{2,1,0:T(8,128)(2,1)S(1)}, bf16[4,256,128]{2,1,0:T(8,128)(2,1)S(1)}, bf16[4,256,128]{2,1,0:T(8,128)(2,1)S(1)}, bf16[4,256,128]{2,1,0:T(8,128)(2,1)S(1)}) fusion(bf16[4,256,128]{2,1,0:T(8,128)(2,1)S(1)} %collective-permute-done.5, bf16[4,256,128]{2,1,0:T(8,128)(2,1)} %collective-permute-done.6, ...), kind=kLoop, calls=%fused_computation.50 | loop fusion | flops 1572864 | bytes 2097168 | tf_op jit(solution)/shard_map/select_n | solution.py:200
  67.9 1.3 %copy_bitcast_fusion = bf16[1,32,16,8,128]{4,3,2,1,0:T(8,128)(2,1)} fusion(bf16[4,256,128]{2,1,0:T(8,128)(2,1)S(1)} %get-tuple-element.6, bf16[4,256,128]{2,1,0:T(8,128)(2,1)S(1)} %get-tuple-element.7, bf16[4,256,128]{2,1,0:T(8,128)(2,1)S(1)} %get-tuple-element.8, bf16[4,256,128]{2,1,0:T(8,128)(2,1)S(1)} %get-tuple-element.5), kind=kLoop, calls=%fused_computation.32 | loop fusion | flops 1572864 | bytes 2097152 | tf_op jit(solution)/shard_map/broadcast_in_dim | solution.py:203
  (7 shorter events, 0.1 us)
Async XLA Ops:
  0.0 1.2 %copy-start = (bf16[1,128,4,8,128]{4,3,2,1,0:T(8,128)(2,1)S(1)}, bf16[1,128,4,8,128]{4,3,2,1,0:T(8,128)(2,1)}, u32[]{:S(2)}) copy-start(bf16[1,128,4,8,128]{4,3,2,1,0:T(8,128)(2,1)} %param.4) | copy-start | bytes 3145732
  2.8 11.6 %collective-permute-start = (bf16[1,1024,128]{2,1,0:T(8,128)(2,1)}, bf16[1,1024,128]{2,1,0:T(8,128)(2,1)}, u32[]{:S(2)}, u32[]{:S(2)}) collective-permute-start(bf16[1,1024,128]{2,1,0:T(8,128)(2,1)} %get-tuple-element.17), channel_id=1, source_target_pairs={{0,4},{4,8},{8,12},{12,0},{1,5},{5,9},{9,13},{13,1},{2,6},{6,10},{... | collective-permute-start | bytes 786440 | tf_op jit(solution)/shard_map/ppermute | solution.py:96
  3.3 11.3 %collective-permute-start.1 = (bf16[1,1024,128]{2,1,0:T(8,128)(2,1)}, bf16[1,1024,128]{2,1,0:T(8,128)(2,1)}, u32[]{:S(2)}, u32[]{:S(2)}) collective-permute-start(bf16[1,1024,128]{2,1,0:T(8,128)(2,1)} %get-tuple-element.16), channel_id=1, source_target_pairs={{4,0},{8,4},{12,8},{0,12},{5,1},{9,5},{13,9},{1,13},{6,2},{10,6},{... | collective-permute-start | bytes 786440 | tf_op jit(solution)/shard_map/ppermute | solution.py:97
  6.6 3.8 %copy-start.2 = (bf16[4,1023,128]{2,1,0:T(8,128)(2,1)S(1)}, bf16[4,1023,128]{2,1,0:T(8,128)(2,1)}, u32[]{:S(2)}) copy-start(bf16[4,1023,128]{2,1,0:T(8,128)(2,1)} %get-tuple-element.19) | copy-start | bytes 3142660
  11.5 2.0 %copy-start.3 = (bf16[5,3,5,64,64]{4,3,2,1,0:T(8,128)(2,1)S(1)}, bf16[5,3,5,64,64]{4,3,2,1,0:T(8,128)(2,1)}, u32[]{:S(2)}) copy-start(bf16[5,3,5,64,64]{4,3,2,1,0:T(8,128)(2,1)} %param.7) | copy-start | bytes 1843204
  16.6 1.4 %copy-start.1 = (bf16[5,3,6,64,128]{4,3,2,1,0:T(8,128)(2,1)S(1)}, bf16[5,3,6,64,128]{4,3,2,1,0:T(8,128)(2,1)}, u32[]{:S(2)}) copy-start(bf16[5,3,6,64,128]{4,3,2,1,0:T(8,128)(2,1)} %fusion.18) | copy-start | bytes 4423684
  30.1 5.8 %collective-permute-start.2 = (bf16[1,1024,128]{2,1,0:T(8,128)(2,1)S(1)}, bf16[1,1024,128]{2,1,0:T(8,128)(2,1)S(1)}, u32[]{:S(2)}, u32[]{:S(2)}) collective-permute-start(bf16[1,1024,128]{2,1,0:T(8,128)(2,1)S(1)} %get-tuple-element.13), channel_id=1, source_target_pairs={{0,4},{4,8},{8,12},{12,0},{1,5},{5,9},{9,13},{13,1},{2,6},{6,10},{... | collective-permute-start | bytes 786440 | tf_op jit(solution)/shard_map/ppermute | solution.py:96
  31.8 5.9 %collective-permute-start.3 = (bf16[1,1024,128]{2,1,0:T(8,128)(2,1)S(1)}, bf16[1,1024,128]{2,1,0:T(8,128)(2,1)S(1)}, u32[]{:S(2)}, u32[]{:S(2)}) collective-permute-start(bf16[1,1024,128]{2,1,0:T(8,128)(2,1)S(1)} %get-tuple-element.12), channel_id=1, source_target_pairs={{4,0},{8,4},{12,8},{0,12},{5,1},{9,5},{13,9},{1,13},{6,2},{10,6},{... | collective-permute-start | bytes 786440 | tf_op jit(solution)/shard_map/ppermute | solution.py:97
  51.2 7.4 %collective-permute-start.4 = (bf16[4,256,128]{2,1,0:T(8,128)(2,1)S(1)}, bf16[4,256,128]{2,1,0:T(8,128)(2,1)S(1)}, u32[]{:S(2)}, u32[]{:S(2)}) collective-permute-start(bf16[4,256,128]{2,1,0:T(8,128)(2,1)S(1)} %get-tuple-element.9), channel_id=1, source_target_pairs={{0,4},{4,8},{8,12},{12,0},{1,5},{5,9},{9,13},{13,1},{2,6},{6,10},{... | collective-permute-start | bytes 786440 | tf_op jit(solution)/shard_map/ppermute | solution.py:196
  52.9 9.2 %collective-permute-start.5 = (bf16[4,256,128]{2,1,0:T(8,128)(2,1)S(1)}, bf16[4,256,128]{2,1,0:T(8,128)(2,1)S(1)}, u32[]{:S(2)}, u32[]{:S(2)}) collective-permute-start(bf16[4,256,128]{2,1,0:T(8,128)(2,1)S(1)} %get-tuple-element.11), channel_id=1, source_target_pairs={{0,8},{4,12},{8,0},{12,4},{1,9},{5,13},{9,1},{13,5},{2,10},{6,14},... | collective-permute-start | bytes 786440 | tf_op jit(solution)/shard_map/ppermute | solution.py:196
  54.9 11.7 %collective-permute-start.6 = (bf16[4,256,128]{2,1,0:T(8,128)(2,1)S(1)}, bf16[4,256,128]{2,1,0:T(8,128)(2,1)}, u32[]{:S(2)}, u32[]{:S(2)}) collective-permute-start(bf16[4,256,128]{2,1,0:T(8,128)(2,1)S(1)} %get-tuple-element.10), channel_id=1, source_target_pairs={{0,12},{4,0},{8,4},{12,8},{1,13},{5,1},{9,5},{13,9},{2,14},{6,2},{... | collective-permute-start | bytes 786440 | tf_op jit(solution)/shard_map/ppermute | solution.py:196

commit v10 on v9

--- a/solution.py
+++ b/solution.py
@@ -38,7 +38,7 @@
 def spread_call(low, xs, high, weights, flat, counts, dilation, pairs):
     shots, rows, lanes = flat.shape
     scalars = jnp.concatenate([jnp.zeros((1,), jnp.int32), counts])
-    flops = 2 * shots * 15 * xs.shape[1] * xs.shape[2] * weights.shape[2]
+    flops = 2 * shots * 3 * xs.shape[1] * xs.shape[2] * 5 * lanes
     return pl.pallas_call(
         functools.partial(spread_kernel, dilation=dilation, pairs=pairs),
         grid_spec=pltpu.PrefetchScalarGridSpec(
@@ -52,10 +52,11 @@
                     (1, xs.shape[1], xs.shape[2]), lambda s, c: (jnp.minimum(s + 1, shots - 1), 0, 0)
                 ),
                 pl.BlockSpec((1, xs.shape[1], xs.shape[2]), lambda s, c: (0, 0, 0)),
-                pl.BlockSpec(weights.shape, lambda s, c: (0, 0, 0)),
+                pl.BlockSpec(weights.shape, lambda s, c: (0, 0, 0, 0, 0)),
                 pl.BlockSpec((1, rows, lanes), lambda s, c: (s, 0, 0)),
             ],
             out_specs=pl.BlockSpec((1, rows, lanes), lambda s, c: (s, 0, 0)),
+            scratch_shapes=[pltpu.VMEM((3 * xs.shape[2], 5 * lanes), weights.dtype)],
         ),
         out_shape=jax.ShapeDtypeStruct((shots, rows, lanes), jnp.bfloat16),
         compiler_params=pltpu.CompilerParams(vmem_limit_bytes=48 * 1024 * 1024),
@@ -67,16 +68,30 @@
     )(scalars, low, xs, xs, xs, high, weights, flat)
 
 
-def spread_kernel(scalars_ref, lo_ref, x0_ref, x1_ref, x2_ref, hi_ref, w_ref, res_ref, out_ref, *, dilation, pairs):
+def spread_kernel(
+    scalars_ref, lo_ref, x0_ref, x1_ref, x2_ref, hi_ref, w_ref, res_ref, out_ref, rhs_ref, *, dilation, pairs
+):
     s = pl.program_id(0)
+    receiver_taps, shot_taps, time_taps, channels, _ = w_ref.shape
+
+    @pl.when(s == 0)
+    def _():
+        zero = jnp.zeros((channels, channels), rhs_ref.dtype)
+        for b in range(shot_taps):
+            for e in range(time_taps + 1):
+                row = (b * (time_taps + 1) + e) * channels
+                for a in range(receiver_taps):
+                    ahead = w_ref[a, b, e] if e < time_taps else zero
+                    behind = w_ref[a, b, e - 1] if e >= 1 else zero
+                    rhs_ref[pl.ds(row, channels), pl.ds(a * 2 * channels, 2 * channels)] = jnp.concatenate(
+                        [ahead, behind], axis=1
+                    )
+
     rows, lanes = out_ref.shape[1:]
     first_shot = jnp.where(s == 0, lo_ref[0], x0_ref[0])
     last_shot = jnp.where(s == pl.num_programs(0) - 1, hi_ref[0], x2_ref[0])
     lhs = jnp.concatenate([first_shot, x1_ref[0], last_shot], axis=1)
-    rhs = jnp.concatenate(
-        [jnp.concatenate([w_ref[a * 3 + b] for a in range(5)], axis=1) for b in range(3)], axis=0
-    )
-    spread = jnp.dot(lhs, rhs, preferred_element_type=jnp.float32)
+    spread = jnp.dot(lhs, rhs_ref[...], preferred_element_type=jnp.float32)
     total = None
     for a in range(5):
         part = spread[a * dilation * pairs : a * dilation * pairs + rows, a * lanes : (a + 1) * lanes]
@@ -171,21 +186,19 @@
     count = lax.axis_size("shot")
     me = lax.axis_index("shot")
     chosen = lax.dynamic_slice_in_dim(counts[:, 0], me * shot_local, shot_local)
-    first_pairs = pair_weights(first_weight)
-    second_pairs = pair_weights(second_weight)
     volume = jnp.transpose(features[0], (1, 0, 2, 3)).reshape(shot_local, receivers * pairs, lanes)
     alive = jnp.arange(receivers * pairs, dtype=jnp.int32)[None, :] // pairs < chosen[:, None]
     flat1 = volume * alive.astype(volume.dtype)[:, :, None]
     low1, high1 = halos(flat1, "shot")
     xs1 = stack_rows(flat1, 1, pairs)
     flat2 = spread_call(
-        stack_rows(low1, 1, pairs), xs1, stack_rows(high1, 1, pairs), first_pairs, flat1, chosen, 1, pairs
+        stack_rows(low1, 1, pairs), xs1, stack_rows(high1, 1, pairs), first_weight, flat1, chosen, 1, pairs
     )
     low2, high2 = halos(flat2, "shot")
     xs2 = stack_rows(flat2, 4, pairs)
     span = receivers // count
     whole = spread_call(
-        stack_rows(low2, 4, pairs), xs2, stack_rows(high2, 4, pairs), second_pairs, flat2, chosen, 4, pairs
+        stack_rows(low2, 4, pairs), xs2, stack_rows(high2, 4, pairs), second_weight, flat2, chosen, 4, pairs
     )
     arrived = []
     for shift in range(count):

time: 69.8 us -> 66.5 us (0.953)
  other arithmetic: 16.6 us -> 11.1 us
  waiting for transfers between devices: 13.2 us -> 16.8 us
  local copies, waits for them, and re-layouts: 5.44 us -> 4.6 us
    concatenate x2 -> x0, other arithmetic: 4.61 us -> none  [pair_weights(): joined = jnp.concatenate([ahead, behind], axis=4)]
    ppermute x2, waiting for transfers between devices: 1.6 us -> 4.31 us  [halos(): high = lax.ppermute(block[:1], axis, backward)]
    ppermute x2, starting transfers between devices: 2.05 us -> 3.97 us  [halos(): high = lax.ppermute(block[:1], axis, backward)]
    ppermute x2, starting transfers between devices: 2.15 us -> 0.79 us  [halos(): low = lax.ppermute(block[-1:], axis, forward)]
    ppermute x3, starting transfers between devices: 5.07 us -> 3.93 us  [body(): piece = lax.ppermute(piece, 'shot', pairs_list)]
    slice x6, local copies, waits for them, and re-layouts: 2.19 us -> 1.22 us  [stack_rows(): before = jnp.concatenate([blank, volume[:, :-1]], axis=1)]
    select_n x2, other arithmetic: 1 us -> 0.04 us  [halos(): high = jnp.where(me == count - 1, jnp.zeros_like(high), high)]
    unnamed x8 -> x6, local copies, waits for them, and re-layouts: 1.49 us -> 2.43 us
  transfers between devices with their start and end apart: 7 -> 7, of which waited for: 5 -> 7; matrix products, arithmetic and copies ran while one was open for 17% -> 10% of each run, Pallas kernels for 0% -> 0%
where the time goes in v10:
time: 66.5 us; the launch traced here: 66.2 us
  Pallas kernels  24.8 us (37%)
  waiting for transfers between devices  16.8 us (25%)
  other arithmetic  11.1 us (17%)
  starting transfers between devices  8.69 us (13%)
  local copies, waits for them, and re-layouts  4.6 us (7%)
    pallas_call x2, Pallas kernels, spread_call(): pl.pallas_call(functools.partial(spread_kernel, dilation=dilation, pairs=...  24.8 us
    ppermute x3, waiting for transfers between devices, body(): piece = lax.ppermute(piece, 'shot', pairs_list)  10.3 us
    concatenate x6, other arithmetic, stack_rows(): stacked = jnp.concatenate([before, volume, after], axis=2)  4.35 us
    ppermute x2, waiting for transfers between devices, halos(): high = lax.ppermute(block[:1], axis, backward)  4.31 us
    ppermute x2, starting transfers between devices, halos(): high = lax.ppermute(block[:1], axis, backward)  3.97 us
    ppermute x3, starting transfers between devices, body(): piece = lax.ppermute(piece, 'shot', pairs_list)  3.93 us
    select_n x4, other arithmetic, stack_rows(): after = jnp.where(phase == pairs - 1, jnp.zeros_like(after), after)  2.58 us
    unnamed x6, local copies, waits for them, and re-layouts  2.43 us
  transfers between devices with their start and end apart: 7, of which 7 were waited for; matrix products, arithmetic and copies ran while one was open for 10% of the time, Pallas kernels for 0%

profile of v10, /device:TPU:0, one launch (start us, length us, event | category | flops | bytes accessed | tf_op | source)
XLA Modules:
  0.0 66.2 jit_solution(3945158425079917401)
XLA Ops:
  0.0 0.0 copy-start
  0.0 0.8 %fusion.23 = s32[4]{0:T(128)S(1)} fusion(s32[16,1]{0,1:T(1,128)} %param.5, s32[]{:T(128)S(6)} %select_n.242), kind=kLoop, calls=%fused_computation.72 | loop fusion | bytes 36 | tf_op jit(solution)/shard_map/dynamic_slice | solution.py:188
  0.8 0.1 compare_convert_fusion
  0.9 0.3 copy-done
  1.2 0.7 %bitcast_multiply_fusion.res_ref = bf16[4,1024,128]{2,1,0:T(8,128)(2,1)S(1)} fusion(bf16[4,1024]{1,0:T(4,128)(2,1)S(1)} %compare_convert_fusion, bf16[1,128,4,8,128]{4,3,2,1,0:T(8,128)(2,1)S(1)} %copy-done), kind=kLoop, calls=%fused_computation.23 | loop fusion | flops 2097152 | bytes 2105344 | tf_op jit(solution)/shard_map/mul | solution.py:191
  2.0 0.5 collective-permute-start
  2.5 2.0 %collective-permute-start.1 = (bf16[1,1024,128]{2,1,0:T(8,128)(2,1)S(1)}, bf16[1,1024,128]{2,1,0:T(8,128)(2,1)S(1)}, u32[]{:S(2)}, u32[]{:S(2)}) collective-permute-start(bf16[1,1024,128]{2,1,0:T(8,128)(2,1)S(1)} %get-tuple-element.16), channel_id=1, source_target_pairs={{4,0},{8,4},{12,8},{0,12},{5,1},{9,5},{13,9},{1,13},{6,2},{10,6},{... | collective-permute-start | bytes 786440 | tf_op jit(solution)/shard_map/ppermute | solution.py:112
  4.5 0.4 fusion.27
  5.0 1.2 %pad_select_fusion.2 = (bf16[4,1024,128]{2,1,0:T(8,128)(2,1)S(1)}, bf16[4,1024,128]{2,1,0:T(8,128)(2,1)S(1)}) fusion(bf16[4,1023,128]{2,1,0:T(8,128)(2,1)S(1)} %get-tuple-element.19, pred[1024]{0:T(1024)(128)(4,1)S(1)} %fusion.19, bf16[4,1023,128]{2,1,0:T(8,128)(2,1)S(1)} %get-tuple-element.18, pred[1024]{0:T(1024)(128)(4,1)S(1)} %fusion.20), kind=kLoop, calls=%fused_computation.27 | loop fusion | flops 1048576 | bytes 4194304 | tf_op jit(solution)/shard_map/jit(_where)/select_n | solution.py:125
  6.2 1.9 %fusion.11.x0_ref.x1_ref.x2_ref = bf16[4,1056,384]{2,1,0:T(8,128)(2,1)} fusion(bf16[4,1024,128]{2,1,0:T(8,128)(2,1)S(1)} %get-tuple-element.38, bf16[4,1024,128]{2,1,0:T(8,128)(2,1)S(1)} %bitcast_multiply_fusion.res_ref, bf16[4,1024,128]{2,1,0:T(8,128)(2,1)S(1)} %get-tuple-element.39), kind=kLoop, calls=%fused_computation.15 | loop fusion | flops 19464192 | bytes 6389760 | tf_op jit(solution)/shard_map/concatenate | solution.py:126
  8.1 0.1 pad_add_fusion.scalars_ref
  8.1 0.6 collective-permute-done
  8.7 0.1 fusion.31
  8.8 2.3 %collective-permute-done.1 = bf16[1,1024,128]{2,1,0:T(8,128)(2,1)S(1)} collective-permute-done((bf16[1,1024,128]{2,1,0:T(8,128)(2,1)S(1)}, bf16[1,1024,128]{2,1,0:T(8,128)(2,1)S(1)}, u32[]{:S(2)}, u32[]{:S(2)}) %collective-permute-start.1) | collective-permute-done | bytes 262176 | tf_op jit(solution)/shard_map/ppermute | solution.py:112
  11.2 0.1 fusion.30
  11.3 0.9 %pad_select_fusion.8 = (bf16[1,1024,128]{2,1,0:T(8,128)(2,1)S(1)}, bf16[1,1024,128]{2,1,0:T(8,128)(2,1)S(1)}, bf16[1,1024,128]{2,1,0:T(8,128)(2,1)S(1)}, bf16[1,1024,128]{2,1,0:T(8,128)(2,1)S(1)}) fusion(bf16[1,1023,128]{2,1,0:T(8,128)(2,1)S(1)} %get-tuple-element.25, pred[1024]{0:T(1024)(128)(4,1)S(1)} %fusion.19, ...), kind=kLoop, calls=%fused_computation.47 | loop fusion | flops 524288 | bytes 2098176 | tf_op jit(solution)/shard_map/jit(_where)/select_n | solution.py:125
  12.2 0.0 copy-start.1
  12.2 0.1 select_maximum_fusion.4.hi_ref
  12.3 0.1 select_maximum_fusion.6.lo_ref
  12.4 1.0 %copy-done.1 = bf16[5,3,5,64,64]{4,3,2,1,0:T(8,128)(2,1)S(1)} copy-done((bf16[5,3,5,64,64]{4,3,2,1,0:T(8,128)(2,1)S(1)}, bf16[5,3,5,64,64]{4,3,2,1,0:T(8,128)(2,1)}, u32[]{:S(2)}) %copy-start.1) | copy-done | bytes 614424
  13.5 11.9 %shard_map.46.res_ref = bf16[4,1024,128]{2,1,0:T(8,128)(2,1)S(1)} custom-call(s32[5]{0:T(128)S(1)} %pad_add_fusion.scalars_ref, bf16[1,1056,384]{2,1,0:T(8,128)(2,1)S(1)} %select_maximum_fusion.6.lo_ref, bf16[4,1056,384]{2,1,0:T(8,128)(2,1)} %fusion.11.x0_ref.x1_ref.x2_ref, bf16[4,1056,384]{2,1,0:T(8,128)(2,1)} %fusion.11.x0_ref.x1_ref.x2_ref, ...), custom_call_target="tpu_custom_call" | custom-call | flops 6228541440 | bytes 7577600 | tf_op jit(solution)/shard_map/pallas_call | solution.py:42
  25.4 0.4 fusion.25
  25.9 0.2 collective-permute-start.2
  26.1 2.0 %collective-permute-start.3 = (bf16[1,1024,128]{2,1,0:T(8,128)(2,1)S(1)}, bf16[1,1024,128]{2,1,0:T(8,128)(2,1)S(1)}, u32[]{:S(2)}, u32[]{:S(2)}) collective-permute-start(bf16[1,1024,128]{2,1,0:T(8,128)(2,1)S(1)} %get-tuple-element.12), channel_id=1, source_target_pairs={{4,0},{8,4},{12,8},{0,12},{5,1},{9,5},{13,9},{1,13},{6,2},{10,6},{... | collective-permute-start | bytes 786440 | tf_op jit(solution)/shard_map/ppermute | solution.py:112
  28.1 0.3 pad_select_fusion
  28.4 0.4 pad_select_fusion.1
  28.8 2.0 %fusion.9.x0_ref.x1_ref.x2_ref = bf16[4,1152,384]{2,1,0:T(8,128)(2,1)} fusion(bf16[4,1024,128]{2,1,0:T(8,128)(2,1)S(1)} %pad_select_fusion, bf16[4,1024,128]{2,1,0:T(8,128)(2,1)S(1)} %shard_map.46.res_ref, bf16[4,1024,128]{2,1,0:T(8,128)(2,1)S(1)} %pad_select_fusion.1), kind=kLoop, calls=%fused_computation.13 | loop fusion | flops 21233664 | bytes 6684672 | tf_op jit(solution)/shard_map/concatenate | solution.py:126
  30.8 1.6 %collective-permute-done.2 = bf16[1,1024,128]{2,1,0:T(8,128)(2,1)S(1)} collective-permute-done((bf16[1,1024,128]{2,1,0:T(8,128)(2,1)S(1)}, bf16[1,1024,128]{2,1,0:T(8,128)(2,1)S(1)}, u32[]{:S(2)}, u32[]{:S(2)}) %collective-permute-start.2) | collective-permute-done | bytes 262176 | tf_op jit(solution)/shard_map/ppermute | solution.py:111
  32.5 0.1 fusion.29
  32.6 2.0 %collective-permute-done.3 = bf16[1,1024,128]{2,1,0:T(8,128)(2,1)S(1)} collective-permute-done((bf16[1,1024,128]{2,1,0:T(8,128)(2,1)S(1)}, bf16[1,1024,128]{2,1,0:T(8,128)(2,1)S(1)}, u32[]{:S(2)}, u32[]{:S(2)}) %collective-permute-start.3) | collective-permute-done | bytes 262176 | tf_op jit(solution)/shard_map/ppermute | solution.py:112
  34.6 0.1 fusion.28
  34.7 0.3 pad_select_fusion.5
  35.0 0.2 pad_select_fusion.4
  35.2 0.0 copy-start.2
  35.2 0.1 select_maximum_fusion.hi_ref
  35.3 0.1 select_maximum_fusion.2.lo_ref
  35.5 1.0 %copy-done.2 = bf16[5,3,5,64,64]{4,3,2,1,0:T(8,128)(2,1)S(1)} copy-done((bf16[5,3,5,64,64]{4,3,2,1,0:T(8,128)(2,1)S(1)}, bf16[5,3,5,64,64]{4,3,2,1,0:T(8,128)(2,1)}, u32[]{:S(2)}) %copy-start.2) | copy-done | bytes 614424
  36.5 12.9 %shard_map.47 = bf16[4,1024,128]{2,1,0:T(8,128)(2,1)S(1)} custom-call(s32[5]{0:T(128)S(1)} %pad_add_fusion.scalars_ref, bf16[1,1152,384]{2,1,0:T(8,128)(2,1)S(1)} %select_maximum_fusion.2.lo_ref, bf16[4,1152,384]{2,1,0:T(8,128)(2,1)} %fusion.9.x0_ref.x1_ref.x2_ref, bf16[4,1152,384]{2,1,0:T(8,128)(2,1)} %fusion.9.x0_ref.x1_ref.x2_ref, ...), custom_call_target="tpu_custom_call" | custom-call | flops 6794772480 | bytes 8019968 | tf_op jit(solution)/shard_map/pallas_call | solution.py:42
  49.4 0.1 constant_dynamic-slice_fusion.2
  49.4 0.2 collective-permute-start.4
  49.6 2.3 %collective-permute-start.5 = (bf16[4,256,128]{2,1,0:T(8,128)(2,1)S(1)}, bf16[4,256,128]{2,1,0:T(8,128)(2,1)S(1)}, u32[]{:S(2)}, u32[]{:S(2)}) collective-permute-start(bf16[4,256,128]{2,1,0:T(8,128)(2,1)S(1)} %get-tuple-element.11), channel_id=1, source_target_pairs={{0,8},{4,12},{8,0},{12,4},{1,9},{5,13},{9,1},{13,5},{2,10},{6,14},... | collective-permute-start | bytes 786440 | tf_op jit(solution)/shard_map/ppermute | solution.py:209
  52.0 1.4 %collective-permute-start.6 = (bf16[4,256,128]{2,1,0:T(8,128)(2,1)S(1)}, bf16[4,256,128]{2,1,0:T(8,128)(2,1)}, u32[]{:S(2)}, u32[]{:S(2)}) collective-permute-start(bf16[4,256,128]{2,1,0:T(8,128)(2,1)S(1)} %get-tuple-element.10), channel_id=1, source_target_pairs={{0,12},{4,0},{8,4},{12,8},{1,13},{5,1},{9,5},{13,9},{2,14},{6,2},{... | collective-permute-start | bytes 786440 | tf_op jit(solution)/shard_map/ppermute | solution.py:209
  53.4 4.2 %collective-permute-done.4 = bf16[4,256,128]{2,1,0:T(8,128)(2,1)S(1)} collective-permute-done((bf16[4,256,128]{2,1,0:T(8,128)(2,1)S(1)}, bf16[4,256,128]{2,1,0:T(8,128)(2,1)S(1)}, u32[]{:S(2)}, u32[]{:S(2)}) %collective-permute-start.4) | collective-permute-done | bytes 262176 | tf_op jit(solution)/shard_map/ppermute | solution.py:209
  57.5 1.6 %collective-permute-done.5 = bf16[4,256,128]{2,1,0:T(8,128)(2,1)S(1)} collective-permute-done((bf16[4,256,128]{2,1,0:T(8,128)(2,1)S(1)}, bf16[4,256,128]{2,1,0:T(8,128)(2,1)S(1)}, u32[]{:S(2)}, u32[]{:S(2)}) %collective-permute-start.5) | collective-permute-done | bytes 262176 | tf_op jit(solution)/shard_map/ppermute | solution.py:209
  59.1 4.5 %collective-permute-done.6 = bf16[4,256,128]{2,1,0:T(8,128)(2,1)} collective-permute-done((bf16[4,256,128]{2,1,0:T(8,128)(2,1)S(1)}, bf16[4,256,128]{2,1,0:T(8,128)(2,1)}, u32[]{:S(2)}, u32[]{:S(2)}) %collective-permute-start.6) | collective-permute-done | bytes 262176 | tf_op jit(solution)/shard_map/ppermute | solution.py:209
  63.7 1.3 %select_select_fusion.3 = (bf16[4,256,128]{2,1,0:T(8,128)(2,1)S(1)}, bf16[4,256,128]{2,1,0:T(8,128)(2,1)S(1)}, bf16[4,256,128]{2,1,0:T(8,128)(2,1)S(1)}, bf16[4,256,128]{2,1,0:T(8,128)(2,1)S(1)}) fusion(bf16[4,256,128]{2,1,0:T(8,128)(2,1)S(1)} %collective-permute-done.5, bf16[4,256,128]{2,1,0:T(8,128)(2,1)} %collective-permute-done.6, ...), kind=kLoop, calls=%fused_computation.42 | loop fusion | flops 1572864 | bytes 2097168 | tf_op jit(solution)/shard_map/select_n | solution.py:213
  65.0 1.3 %copy_bitcast_fusion = bf16[1,32,16,8,128]{4,3,2,1,0:T(8,128)(2,1)} fusion(bf16[4,256,128]{2,1,0:T(8,128)(2,1)S(1)} %get-tuple-element.6, bf16[4,256,128]{2,1,0:T(8,128)(2,1)S(1)} %get-tuple-element.7, bf16[4,256,128]{2,1,0:T(8,128)(2,1)S(1)} %get-tuple-element.8, bf16[4,256,128]{2,1,0:T(8,128)(2,1)S(1)} %get-tuple-element.5), kind=kLoop, calls=%fused_computation.24 | loop fusion | flops 1572864 | bytes 2097152 | tf_op jit(solution)/shard_map/broadcast_in_dim | solution.py:216
  (9 shorter events, 0.2 us)
Async XLA Ops:
  0.0 1.2 %copy-start = (bf16[1,128,4,8,128]{4,3,2,1,0:T(8,128)(2,1)S(1)}, bf16[1,128,4,8,128]{4,3,2,1,0:T(8,128)(2,1)}, u32[]{:S(2)}) copy-start(bf16[1,128,4,8,128]{4,3,2,1,0:T(8,128)(2,1)} %param.4) | copy-start | bytes 3145732
  2.0 6.7 %collective-permute-start = (bf16[1,1024,128]{2,1,0:T(8,128)(2,1)S(1)}, bf16[1,1024,128]{2,1,0:T(8,128)(2,1)S(1)}, u32[]{:S(2)}, u32[]{:S(2)}) collective-permute-start(bf16[1,1024,128]{2,1,0:T(8,128)(2,1)S(1)} %get-tuple-element.17), channel_id=1, source_target_pairs={{0,4},{4,8},{8,12},{12,0},{1,5},{5,9},{9,13},{13,1},{2,6},{6,10},{... | collective-permute-start | bytes 786440 | tf_op jit(solution)/shard_map/ppermute | solution.py:111
  2.5 8.6 %collective-permute-start.1 = (bf16[1,1024,128]{2,1,0:T(8,128)(2,1)S(1)}, bf16[1,1024,128]{2,1,0:T(8,128)(2,1)S(1)}, u32[]{:S(2)}, u32[]{:S(2)}) collective-permute-start(bf16[1,1024,128]{2,1,0:T(8,128)(2,1)S(1)} %get-tuple-element.16), channel_id=1, source_target_pairs={{4,0},{8,4},{12,8},{0,12},{5,1},{9,5},{13,9},{1,13},{6,2},{10,6},{... | collective-permute-start | bytes 786440 | tf_op jit(solution)/shard_map/ppermute | solution.py:112
  12.2 1.3 %copy-start.1 = (bf16[5,3,5,64,64]{4,3,2,1,0:T(8,128)(2,1)S(1)}, bf16[5,3,5,64,64]{4,3,2,1,0:T(8,128)(2,1)}, u32[]{:S(2)}) copy-start(bf16[5,3,5,64,64]{4,3,2,1,0:T(8,128)(2,1)} %w_ref.2) | copy-start | bytes 1843204
  25.9 6.6 %collective-permute-start.2 = (bf16[1,1024,128]{2,1,0:T(8,128)(2,1)S(1)}, bf16[1,1024,128]{2,1,0:T(8,128)(2,1)S(1)}, u32[]{:S(2)}, u32[]{:S(2)}) collective-permute-start(bf16[1,1024,128]{2,1,0:T(8,128)(2,1)S(1)} %get-tuple-element.13), channel_id=1, source_target_pairs={{0,4},{4,8},{8,12},{12,0},{1,5},{5,9},{9,13},{13,1},{2,6},{6,10},{... | collective-permute-start | bytes 786440 | tf_op jit(solution)/shard_map/ppermute | solution.py:111
  26.1 8.5 %collective-permute-start.3 = (bf16[1,1024,128]{2,1,0:T(8,128)(2,1)S(1)}, bf16[1,1024,128]{2,1,0:T(8,128)(2,1)S(1)}, u32[]{:S(2)}, u32[]{:S(2)}) collective-permute-start(bf16[1,1024,128]{2,1,0:T(8,128)(2,1)S(1)} %get-tuple-element.12), channel_id=1, source_target_pairs={{4,0},{8,4},{12,8},{0,12},{5,1},{9,5},{13,9},{1,13},{6,2},{10,6},{... | collective-permute-start | bytes 786440 | tf_op jit(solution)/shard_map/ppermute | solution.py:112
  35.2 1.3 %copy-start.2 = (bf16[5,3,5,64,64]{4,3,2,1,0:T(8,128)(2,1)S(1)}, bf16[5,3,5,64,64]{4,3,2,1,0:T(8,128)(2,1)}, u32[]{:S(2)}) copy-start(bf16[5,3,5,64,64]{4,3,2,1,0:T(8,128)(2,1)} %w_ref.3) | copy-start | bytes 1843204
  49.4 8.1 %collective-permute-start.4 = (bf16[4,256,128]{2,1,0:T(8,128)(2,1)S(1)}, bf16[4,256,128]{2,1,0:T(8,128)(2,1)S(1)}, u32[]{:S(2)}, u32[]{:S(2)}) collective-permute-start(bf16[4,256,128]{2,1,0:T(8,128)(2,1)S(1)} %get-tuple-element.9), channel_id=1, source_target_pairs={{0,4},{4,8},{8,12},{12,0},{1,5},{5,9},{9,13},{13,1},{2,6},{6,10},{... | collective-permute-start | bytes 786440 | tf_op jit(solution)/shard_map/ppermute | solution.py:209
  49.6 9.5 %collective-permute-start.5 = (bf16[4,256,128]{2,1,0:T(8,128)(2,1)S(1)}, bf16[4,256,128]{2,1,0:T(8,128)(2,1)S(1)}, u32[]{:S(2)}, u32[]{:S(2)}) collective-permute-start(bf16[4,256,128]{2,1,0:T(8,128)(2,1)S(1)} %get-tuple-element.11), channel_id=1, source_target_pairs={{0,8},{4,12},{8,0},{12,4},{1,9},{5,13},{9,1},{13,5},{2,10},{6,14},... | collective-permute-start | bytes 786440 | tf_op jit(solution)/shard_map/ppermute | solution.py:209
  52.0 11.7 %collective-permute-start.6 = (bf16[4,256,128]{2,1,0:T(8,128)(2,1)S(1)}, bf16[4,256,128]{2,1,0:T(8,128)(2,1)}, u32[]{:S(2)}, u32[]{:S(2)}) collective-permute-start(bf16[4,256,128]{2,1,0:T(8,128)(2,1)S(1)} %get-tuple-element.10), channel_id=1, source_target_pairs={{0,12},{4,0},{8,4},{12,8},{1,13},{5,1},{9,5},{13,9},{2,14},{6,2},{... | collective-permute-start | bytes 786440 | tf_op jit(solution)/shard_map/ppermute | solution.py:209

commit v11 on v10

--- a/solution.py
+++ b/solution.py
@@ -6,33 +6,6 @@
 from jax.experimental import pallas as pl
 from jax.experimental.pallas import tpu as pltpu
 from jax.sharding import PartitionSpec as P
-
-
-def extended(block, axis, dim, width):
-    count = lax.axis_size(axis)
-    forward = [(i, i + 1) for i in range(count - 1)]
-    backward = [(target, source) for source, target in forward]
-    low = lax.ppermute(
-        lax.slice_in_dim(block, block.shape[dim] - width, None, axis=dim), axis, forward
-    )
-    high = lax.ppermute(lax.slice_in_dim(block, 0, width, axis=dim), axis, backward)
-    return jnp.concatenate([low, block, high], axis=dim)
-
-
-def pair_weights(weight):
-    ahead = jnp.pad(weight, ((0, 0), (0, 0), (0, 1), (0, 0), (0, 0)))
-    behind = jnp.pad(weight, ((0, 0), (0, 0), (1, 0), (0, 0), (0, 0)))
-    joined = jnp.concatenate([ahead, behind], axis=4)
-    return joined.reshape(weight.shape[0] * weight.shape[1], -1, joined.shape[4])
-
-def stack_time(block, dilation):
-    pairs = block.shape[2]
-    padded = jnp.pad(block, ((0, 0), (2 * dilation, 2 * dilation), (1, 1), (0, 0)))
-    stacked = jnp.concatenate(
-        [padded[:, :, 0:pairs], padded[:, :, 1 : pairs + 1], padded[:, :, 2 : pairs + 2]],
-        axis=3,
-    )
-    return stacked.reshape(stacked.shape[0], -1, stacked.shape[3])
 
 
 def spread_call(low, xs, high, weights, flat, counts, dilation, pairs):
@@ -128,56 +101,6 @@
     return jnp.pad(stacked, ((0, 0), (margin, margin), (0, 0)))
 
 
-def conv_kernel(scalars_ref, xs_ref, w_ref, res_ref, out_ref, acc_ref, *, dilation, pairs):
-    s = pl.program_id(0)
-    rows = acc_ref.shape[0]
-    for a in range(5):
-        for b in range(3):
-            lhs = xs_ref[s + b, pl.ds(a * dilation * pairs, rows), :]
-            contrib = jnp.dot(lhs, w_ref[a * 3 + b], preferred_element_type=jnp.float32)
-            if a == 0 and b == 0:
-                acc_ref[...] = contrib
-            else:
-                acc_ref[...] += contrib
-    first = scalars_ref[0] * (rows // pairs)
-    receiver = first + lax.broadcasted_iota(jnp.int32, acc_ref.shape, 0) // pairs
-    live = receiver < scalars_ref[1 + s]
-    value = res_ref[0].astype(jnp.float32) + jnp.maximum(acc_ref[...], 0.0)
-    out_ref[0] = jnp.where(live, value, 0.0).astype(out_ref.dtype)
-
-
-def conv_call(xs, weights, flat, counts, dilation, pairs, block, block_rows):
-    shots, _, lanes = flat.shape
-    window = block_rows + 4 * dilation * pairs
-    scalars = jnp.concatenate([jnp.reshape(block, (1,)).astype(jnp.int32), counts])
-    flops = 2 * shots * 15 * block_rows * xs.shape[2] * lanes
-    return pl.pallas_call(
-        functools.partial(conv_kernel, dilation=dilation, pairs=pairs),
-        grid_spec=pltpu.PrefetchScalarGridSpec(
-            num_scalar_prefetch=1,
-            grid=(shots,),
-            in_specs=[
-                pl.BlockSpec(
-                    (pl.Element(xs.shape[0]), pl.Element(window), pl.Element(xs.shape[2])),
-                    lambda s, c: (0, c[0] * block_rows, 0),
-                ),
-                pl.BlockSpec(weights.shape, lambda s, c: (0, 0, 0)),
-                pl.BlockSpec((1, block_rows, lanes), lambda s, c: (s, c[0], 0)),
-            ],
-            out_specs=pl.BlockSpec((1, block_rows, lanes), lambda s, c: (s, 0, 0)),
-            scratch_shapes=[pltpu.VMEM((block_rows, lanes), jnp.float32)],
-        ),
-        out_shape=jax.ShapeDtypeStruct((shots, block_rows, lanes), jnp.bfloat16),
-        compiler_params=pltpu.CompilerParams(vmem_limit_bytes=48 * 1024 * 1024),
-        cost_estimate=pl.CostEstimate(
-            flops=flops,
-            transcendentals=0,
-            bytes_accessed=xs.shape[0] * window * xs.shape[2] * 2 + weights.size * 2
-            + 4 * shots * block_rows * lanes,
-        ),
-    )(scalars, xs, weights, flat)
-
-
 def body(features, counts, first_weight, second_weight):
     receivers = features.shape[1]
     shot_local = features.shape[2]

time: 66.5 us -> 66.5 us (level)
  no operation moved by 1% of the time
where the time goes in v11:
time: 66.5 us; the launch traced here: 66.2 us
  Pallas kernels  24.8 us (37%)
  waiting for transfers between devices  16.8 us (25%)
  other arithmetic  11.1 us (17%)
  starting transfers between devices  8.69 us (13%)
  local copies, waits for them, and re-layouts  4.6 us (7%)
    pallas_call x2, Pallas kernels, spread_call(): pl.pallas_call(functools.partial(spread_kernel, dilation=dilation, pairs=...  24.8 us
    ppermute x3, waiting for transfers between devices, body(): piece = lax.ppermute(piece, 'shot', pairs_list)  10.3 us
    concatenate x6, other arithmetic, stack_rows(): stacked = jnp.concatenate([before, volume, after], axis=2)  4.35 us
    ppermute x2, waiting for transfers between devices, halos(): high = lax.ppermute(block[:1], axis, backward)  4.31 us
    ppermute x2, starting transfers between devices, halos(): high = lax.ppermute(block[:1], axis, backward)  3.97 us
    ppermute x3, starting transfers between devices, body(): piece = lax.ppermute(piece, 'shot', pairs_list)  3.93 us
    select_n x4, other arithmetic, stack_rows(): after = jnp.where(phase == pairs - 1, jnp.zeros_like(after), after)  2.58 us
    unnamed x6, local copies, waits for them, and re-layouts  2.43 us
  transfers between devices with their start and end apart: 7, of which 7 were waited for; matrix products, arithmetic and copies ran while one was open for 10% of the time, Pallas kernels for 0%

profile of v11, /device:TPU:0, one launch (start us, length us, event | category | flops | bytes accessed | tf_op | source)
XLA Modules:
  0.0 66.2 jit_solution(3945158425079917401)
XLA Ops:
  0.0 0.0 copy-start
  0.0 0.8 %fusion.23 = s32[4]{0:T(128)S(1)} fusion(s32[16,1]{0,1:T(1,128)} %param.5, s32[]{:T(128)S(6)} %select_n.242), kind=kLoop, calls=%fused_computation.72 | loop fusion | bytes 36 | tf_op jit(solution)/shard_map/dynamic_slice | solution.py:111
  0.8 0.1 compare_convert_fusion
  0.9 0.3 copy-done
  1.2 0.7 %bitcast_multiply_fusion.res_ref = bf16[4,1024,128]{2,1,0:T(8,128)(2,1)S(1)} fusion(bf16[4,1024]{1,0:T(4,128)(2,1)S(1)} %compare_convert_fusion, bf16[1,128,4,8,128]{4,3,2,1,0:T(8,128)(2,1)S(1)} %copy-done), kind=kLoop, calls=%fused_computation.23 | loop fusion | flops 2097152 | bytes 2105344 | tf_op jit(solution)/shard_map/mul | solution.py:114
  2.0 0.5 collective-permute-start
  2.5 2.0 %collective-permute-start.1 = (bf16[1,1024,128]{2,1,0:T(8,128)(2,1)S(1)}, bf16[1,1024,128]{2,1,0:T(8,128)(2,1)S(1)}, u32[]{:S(2)}, u32[]{:S(2)}) collective-permute-start(bf16[1,1024,128]{2,1,0:T(8,128)(2,1)S(1)} %get-tuple-element.16), channel_id=1, source_target_pairs={{4,0},{8,4},{12,8},{0,12},{5,1},{9,5},{13,9},{1,13},{6,2},{10,6},{... | collective-permute-start | bytes 786440 | tf_op jit(solution)/shard_map/ppermute | solution.py:85
  4.5 0.4 fusion.27
  5.0 1.2 %pad_select_fusion.2 = (bf16[4,1024,128]{2,1,0:T(8,128)(2,1)S(1)}, bf16[4,1024,128]{2,1,0:T(8,128)(2,1)S(1)}) fusion(bf16[4,1023,128]{2,1,0:T(8,128)(2,1)S(1)} %get-tuple-element.19, pred[1024]{0:T(1024)(128)(4,1)S(1)} %fusion.19, bf16[4,1023,128]{2,1,0:T(8,128)(2,1)S(1)} %get-tuple-element.18, pred[1024]{0:T(1024)(128)(4,1)S(1)} %fusion.20), kind=kLoop, calls=%fused_computation.27 | loop fusion | flops 1048576 | bytes 4194304 | tf_op jit(solution)/shard_map/jit(_where)/select_n | solution.py:98
  6.2 1.9 %fusion.11.x0_ref.x1_ref.x2_ref = bf16[4,1056,384]{2,1,0:T(8,128)(2,1)} fusion(bf16[4,1024,128]{2,1,0:T(8,128)(2,1)S(1)} %get-tuple-element.38, bf16[4,1024,128]{2,1,0:T(8,128)(2,1)S(1)} %bitcast_multiply_fusion.res_ref, bf16[4,1024,128]{2,1,0:T(8,128)(2,1)S(1)} %get-tuple-element.39), kind=kLoop, calls=%fused_computation.15 | loop fusion | flops 19464192 | bytes 6389760 | tf_op jit(solution)/shard_map/concatenate | solution.py:99
  8.1 0.1 pad_add_fusion.scalars_ref
  8.1 0.6 collective-permute-done
  8.7 0.1 fusion.31
  8.8 2.3 %collective-permute-done.1 = bf16[1,1024,128]{2,1,0:T(8,128)(2,1)S(1)} collective-permute-done((bf16[1,1024,128]{2,1,0:T(8,128)(2,1)S(1)}, bf16[1,1024,128]{2,1,0:T(8,128)(2,1)S(1)}, u32[]{:S(2)}, u32[]{:S(2)}) %collective-permute-start.1) | collective-permute-done | bytes 262176 | tf_op jit(solution)/shard_map/ppermute | solution.py:85
  11.2 0.1 fusion.30
  11.3 0.9 %pad_select_fusion.8 = (bf16[1,1024,128]{2,1,0:T(8,128)(2,1)S(1)}, bf16[1,1024,128]{2,1,0:T(8,128)(2,1)S(1)}, bf16[1,1024,128]{2,1,0:T(8,128)(2,1)S(1)}, bf16[1,1024,128]{2,1,0:T(8,128)(2,1)S(1)}) fusion(bf16[1,1023,128]{2,1,0:T(8,128)(2,1)S(1)} %get-tuple-element.25, pred[1024]{0:T(1024)(128)(4,1)S(1)} %fusion.19, ...), kind=kLoop, calls=%fused_computation.47 | loop fusion | flops 524288 | bytes 2098176 | tf_op jit(solution)/shard_map/jit(_where)/select_n | solution.py:98
  12.2 0.0 copy-start.1
  12.2 0.1 select_maximum_fusion.4.hi_ref
  12.3 0.1 select_maximum_fusion.6.lo_ref
  12.4 1.0 %copy-done.1 = bf16[5,3,5,64,64]{4,3,2,1,0:T(8,128)(2,1)S(1)} copy-done((bf16[5,3,5,64,64]{4,3,2,1,0:T(8,128)(2,1)S(1)}, bf16[5,3,5,64,64]{4,3,2,1,0:T(8,128)(2,1)}, u32[]{:S(2)}) %copy-start.1) | copy-done | bytes 614424
  13.5 11.9 %shard_map.46.res_ref = bf16[4,1024,128]{2,1,0:T(8,128)(2,1)S(1)} custom-call(s32[5]{0:T(128)S(1)} %pad_add_fusion.scalars_ref, bf16[1,1056,384]{2,1,0:T(8,128)(2,1)S(1)} %select_maximum_fusion.6.lo_ref, bf16[4,1056,384]{2,1,0:T(8,128)(2,1)} %fusion.11.x0_ref.x1_ref.x2_ref, bf16[4,1056,384]{2,1,0:T(8,128)(2,1)} %fusion.11.x0_ref.x1_ref.x2_ref, ...), custom_call_target="tpu_custom_call" | custom-call | flops 6228541440 | bytes 7577600 | tf_op jit(solution)/shard_map/pallas_call | solution.py:15
  25.4 0.4 fusion.25
  25.9 0.2 collective-permute-start.2
  26.1 2.0 %collective-permute-start.3 = (bf16[1,1024,128]{2,1,0:T(8,128)(2,1)S(1)}, bf16[1,1024,128]{2,1,0:T(8,128)(2,1)S(1)}, u32[]{:S(2)}, u32[]{:S(2)}) collective-permute-start(bf16[1,1024,128]{2,1,0:T(8,128)(2,1)S(1)} %get-tuple-element.12), channel_id=1, source_target_pairs={{4,0},{8,4},{12,8},{0,12},{5,1},{9,5},{13,9},{1,13},{6,2},{10,6},{... | collective-permute-start | bytes 786440 | tf_op jit(solution)/shard_map/ppermute | solution.py:85
  28.1 0.3 pad_select_fusion
  28.4 0.4 pad_select_fusion.1
  28.8 2.0 %fusion.9.x0_ref.x1_ref.x2_ref = bf16[4,1152,384]{2,1,0:T(8,128)(2,1)} fusion(bf16[4,1024,128]{2,1,0:T(8,128)(2,1)S(1)} %pad_select_fusion, bf16[4,1024,128]{2,1,0:T(8,128)(2,1)S(1)} %shard_map.46.res_ref, bf16[4,1024,128]{2,1,0:T(8,128)(2,1)S(1)} %pad_select_fusion.1), kind=kLoop, calls=%fused_computation.13 | loop fusion | flops 21233664 | bytes 6684672 | tf_op jit(solution)/shard_map/concatenate | solution.py:99
  30.8 1.6 %collective-permute-done.2 = bf16[1,1024,128]{2,1,0:T(8,128)(2,1)S(1)} collective-permute-done((bf16[1,1024,128]{2,1,0:T(8,128)(2,1)S(1)}, bf16[1,1024,128]{2,1,0:T(8,128)(2,1)S(1)}, u32[]{:S(2)}, u32[]{:S(2)}) %collective-permute-start.2) | collective-permute-done | bytes 262176 | tf_op jit(solution)/shard_map/ppermute | solution.py:84
  32.5 0.1 fusion.29
  32.6 2.0 %collective-permute-done.3 = bf16[1,1024,128]{2,1,0:T(8,128)(2,1)S(1)} collective-permute-done((bf16[1,1024,128]{2,1,0:T(8,128)(2,1)S(1)}, bf16[1,1024,128]{2,1,0:T(8,128)(2,1)S(1)}, u32[]{:S(2)}, u32[]{:S(2)}) %collective-permute-start.3) | collective-permute-done | bytes 262176 | tf_op jit(solution)/shard_map/ppermute | solution.py:85
  34.6 0.1 fusion.28
  34.7 0.3 pad_select_fusion.5
  35.0 0.2 pad_select_fusion.4
  35.2 0.0 copy-start.2
  35.2 0.1 select_maximum_fusion.hi_ref
  35.3 0.1 select_maximum_fusion.2.lo_ref
  35.5 1.0 %copy-done.2 = bf16[5,3,5,64,64]{4,3,2,1,0:T(8,128)(2,1)S(1)} copy-done((bf16[5,3,5,64,64]{4,3,2,1,0:T(8,128)(2,1)S(1)}, bf16[5,3,5,64,64]{4,3,2,1,0:T(8,128)(2,1)}, u32[]{:S(2)}) %copy-start.2) | copy-done | bytes 614424
  36.5 12.9 %shard_map.47 = bf16[4,1024,128]{2,1,0:T(8,128)(2,1)S(1)} custom-call(s32[5]{0:T(128)S(1)} %pad_add_fusion.scalars_ref, bf16[1,1152,384]{2,1,0:T(8,128)(2,1)S(1)} %select_maximum_fusion.2.lo_ref, bf16[4,1152,384]{2,1,0:T(8,128)(2,1)} %fusion.9.x0_ref.x1_ref.x2_ref, bf16[4,1152,384]{2,1,0:T(8,128)(2,1)} %fusion.9.x0_ref.x1_ref.x2_ref, ...), custom_call_target="tpu_custom_call" | custom-call | flops 6794772480 | bytes 8019968 | tf_op jit(solution)/shard_map/pallas_call | solution.py:15
  49.4 0.1 constant_dynamic-slice_fusion.2
  49.4 0.2 collective-permute-start.4
  49.6 2.3 %collective-permute-start.5 = (bf16[4,256,128]{2,1,0:T(8,128)(2,1)S(1)}, bf16[4,256,128]{2,1,0:T(8,128)(2,1)S(1)}, u32[]{:S(2)}, u32[]{:S(2)}) collective-permute-start(bf16[4,256,128]{2,1,0:T(8,128)(2,1)S(1)} %get-tuple-element.11), channel_id=1, source_target_pairs={{0,8},{4,12},{8,0},{12,4},{1,9},{5,13},{9,1},{13,5},{2,10},{6,14},... | collective-permute-start | bytes 786440 | tf_op jit(solution)/shard_map/ppermute | solution.py:132
  52.0 1.4 %collective-permute-start.6 = (bf16[4,256,128]{2,1,0:T(8,128)(2,1)S(1)}, bf16[4,256,128]{2,1,0:T(8,128)(2,1)}, u32[]{:S(2)}, u32[]{:S(2)}) collective-permute-start(bf16[4,256,128]{2,1,0:T(8,128)(2,1)S(1)} %get-tuple-element.10), channel_id=1, source_target_pairs={{0,12},{4,0},{8,4},{12,8},{1,13},{5,1},{9,5},{13,9},{2,14},{6,2},{... | collective-permute-start | bytes 786440 | tf_op jit(solution)/shard_map/ppermute | solution.py:132
  53.4 4.2 %collective-permute-done.4 = bf16[4,256,128]{2,1,0:T(8,128)(2,1)S(1)} collective-permute-done((bf16[4,256,128]{2,1,0:T(8,128)(2,1)S(1)}, bf16[4,256,128]{2,1,0:T(8,128)(2,1)S(1)}, u32[]{:S(2)}, u32[]{:S(2)}) %collective-permute-start.4) | collective-permute-done | bytes 262176 | tf_op jit(solution)/shard_map/ppermute | solution.py:132
  57.5 1.6 %collective-permute-done.5 = bf16[4,256,128]{2,1,0:T(8,128)(2,1)S(1)} collective-permute-done((bf16[4,256,128]{2,1,0:T(8,128)(2,1)S(1)}, bf16[4,256,128]{2,1,0:T(8,128)(2,1)S(1)}, u32[]{:S(2)}, u32[]{:S(2)}) %collective-permute-start.5) | collective-permute-done | bytes 262176 | tf_op jit(solution)/shard_map/ppermute | solution.py:132
  59.1 4.5 %collective-permute-done.6 = bf16[4,256,128]{2,1,0:T(8,128)(2,1)} collective-permute-done((bf16[4,256,128]{2,1,0:T(8,128)(2,1)S(1)}, bf16[4,256,128]{2,1,0:T(8,128)(2,1)}, u32[]{:S(2)}, u32[]{:S(2)}) %collective-permute-start.6) | collective-permute-done | bytes 262176 | tf_op jit(solution)/shard_map/ppermute | solution.py:132
  63.7 1.3 %select_select_fusion.3 = (bf16[4,256,128]{2,1,0:T(8,128)(2,1)S(1)}, bf16[4,256,128]{2,1,0:T(8,128)(2,1)S(1)}, bf16[4,256,128]{2,1,0:T(8,128)(2,1)S(1)}, bf16[4,256,128]{2,1,0:T(8,128)(2,1)S(1)}) fusion(bf16[4,256,128]{2,1,0:T(8,128)(2,1)S(1)} %collective-permute-done.5, bf16[4,256,128]{2,1,0:T(8,128)(2,1)} %collective-permute-done.6, ...), kind=kLoop, calls=%fused_computation.42 | loop fusion | flops 1572864 | bytes 2097168 | tf_op jit(solution)/shard_map/select_n | solution.py:136
  65.0 1.3 %copy_bitcast_fusion = bf16[1,32,16,8,128]{4,3,2,1,0:T(8,128)(2,1)} fusion(bf16[4,256,128]{2,1,0:T(8,128)(2,1)S(1)} %get-tuple-element.6, bf16[4,256,128]{2,1,0:T(8,128)(2,1)S(1)} %get-tuple-element.7, bf16[4,256,128]{2,1,0:T(8,128)(2,1)S(1)} %get-tuple-element.8, bf16[4,256,128]{2,1,0:T(8,128)(2,1)S(1)} %get-tuple-element.5), kind=kLoop, calls=%fused_computation.24 | loop fusion | flops 1572864 | bytes 2097152 | tf_op jit(solution)/shard_map/broadcast_in_dim | solution.py:139
  (9 shorter events, 0.2 us)
Async XLA Ops:
  0.0 1.2 %copy-start = (bf16[1,128,4,8,128]{4,3,2,1,0:T(8,128)(2,1)S(1)}, bf16[1,128,4,8,128]{4,3,2,1,0:T(8,128)(2,1)}, u32[]{:S(2)}) copy-start(bf16[1,128,4,8,128]{4,3,2,1,0:T(8,128)(2,1)} %param.4) | copy-start | bytes 3145732
  2.0 6.7 %collective-permute-start = (bf16[1,1024,128]{2,1,0:T(8,128)(2,1)S(1)}, bf16[1,1024,128]{2,1,0:T(8,128)(2,1)S(1)}, u32[]{:S(2)}, u32[]{:S(2)}) collective-permute-start(bf16[1,1024,128]{2,1,0:T(8,128)(2,1)S(1)} %get-tuple-element.17), channel_id=1, source_target_pairs={{0,4},{4,8},{8,12},{12,0},{1,5},{5,9},{9,13},{13,1},{2,6},{6,10},{... | collective-permute-start | bytes 786440 | tf_op jit(solution)/shard_map/ppermute | solution.py:84
  2.5 8.6 %collective-permute-start.1 = (bf16[1,1024,128]{2,1,0:T(8,128)(2,1)S(1)}, bf16[1,1024,128]{2,1,0:T(8,128)(2,1)S(1)}, u32[]{:S(2)}, u32[]{:S(2)}) collective-permute-start(bf16[1,1024,128]{2,1,0:T(8,128)(2,1)S(1)} %get-tuple-element.16), channel_id=1, source_target_pairs={{4,0},{8,4},{12,8},{0,12},{5,1},{9,5},{13,9},{1,13},{6,2},{10,6},{... | collective-permute-start | bytes 786440 | tf_op jit(solution)/shard_map/ppermute | solution.py:85
  12.2 1.3 %copy-start.1 = (bf16[5,3,5,64,64]{4,3,2,1,0:T(8,128)(2,1)S(1)}, bf16[5,3,5,64,64]{4,3,2,1,0:T(8,128)(2,1)}, u32[]{:S(2)}) copy-start(bf16[5,3,5,64,64]{4,3,2,1,0:T(8,128)(2,1)} %w_ref.2) | copy-start | bytes 1843204
  25.9 6.6 %collective-permute-start.2 = (bf16[1,1024,128]{2,1,0:T(8,128)(2,1)S(1)}, bf16[1,1024,128]{2,1,0:T(8,128)(2,1)S(1)}, u32[]{:S(2)}, u32[]{:S(2)}) collective-permute-start(bf16[1,1024,128]{2,1,0:T(8,128)(2,1)S(1)} %get-tuple-element.13), channel_id=1, source_target_pairs={{0,4},{4,8},{8,12},{12,0},{1,5},{5,9},{9,13},{13,1},{2,6},{6,10},{... | collective-permute-start | bytes 786440 | tf_op jit(solution)/shard_map/ppermute | solution.py:84
  26.1 8.5 %collective-permute-start.3 = (bf16[1,1024,128]{2,1,0:T(8,128)(2,1)S(1)}, bf16[1,1024,128]{2,1,0:T(8,128)(2,1)S(1)}, u32[]{:S(2)}, u32[]{:S(2)}) collective-permute-start(bf16[1,1024,128]{2,1,0:T(8,128)(2,1)S(1)} %get-tuple-element.12), channel_id=1, source_target_pairs={{4,0},{8,4},{12,8},{0,12},{5,1},{9,5},{13,9},{1,13},{6,2},{10,6},{... | collective-permute-start | bytes 786440 | tf_op jit(solution)/shard_map/ppermute | solution.py:85
  35.2 1.3 %copy-start.2 = (bf16[5,3,5,64,64]{4,3,2,1,0:T(8,128)(2,1)S(1)}, bf16[5,3,5,64,64]{4,3,2,1,0:T(8,128)(2,1)}, u32[]{:S(2)}) copy-start(bf16[5,3,5,64,64]{4,3,2,1,0:T(8,128)(2,1)} %w_ref.3) | copy-start | bytes 1843204
  49.4 8.1 %collective-permute-start.4 = (bf16[4,256,128]{2,1,0:T(8,128)(2,1)S(1)}, bf16[4,256,128]{2,1,0:T(8,128)(2,1)S(1)}, u32[]{:S(2)}, u32[]{:S(2)}) collective-permute-start(bf16[4,256,128]{2,1,0:T(8,128)(2,1)S(1)} %get-tuple-element.9), channel_id=1, source_target_pairs={{0,4},{4,8},{8,12},{12,0},{1,5},{5,9},{9,13},{13,1},{2,6},{6,10},{... | collective-permute-start | bytes 786440 | tf_op jit(solution)/shard_map/ppermute | solution.py:132
  49.6 9.5 %collective-permute-start.5 = (bf16[4,256,128]{2,1,0:T(8,128)(2,1)S(1)}, bf16[4,256,128]{2,1,0:T(8,128)(2,1)S(1)}, u32[]{:S(2)}, u32[]{:S(2)}) collective-permute-start(bf16[4,256,128]{2,1,0:T(8,128)(2,1)S(1)} %get-tuple-element.11), channel_id=1, source_target_pairs={{0,8},{4,12},{8,0},{12,4},{1,9},{5,13},{9,1},{13,5},{2,10},{6,14},... | collective-permute-start | bytes 786440 | tf_op jit(solution)/shard_map/ppermute | solution.py:132
  52.0 11.7 %collective-permute-start.6 = (bf16[4,256,128]{2,1,0:T(8,128)(2,1)S(1)}, bf16[4,256,128]{2,1,0:T(8,128)(2,1)}, u32[]{:S(2)}, u32[]{:S(2)}) collective-permute-start(bf16[4,256,128]{2,1,0:T(8,128)(2,1)S(1)} %get-tuple-element.10), channel_id=1, source_target_pairs={{0,12},{4,0},{8,4},{12,8},{1,13},{5,1},{9,5},{13,9},{2,14},{6,2},{... | collective-permute-start | bytes 786440 | tf_op jit(solution)/shard_map/ppermute | solution.py:132

commit v12 on v11

--- a/solution.py
+++ b/solution.py
@@ -32,7 +32,7 @@
             scratch_shapes=[pltpu.VMEM((3 * xs.shape[2], 5 * lanes), weights.dtype)],
         ),
         out_shape=jax.ShapeDtypeStruct((shots, rows, lanes), jnp.bfloat16),
-        compiler_params=pltpu.CompilerParams(vmem_limit_bytes=48 * 1024 * 1024),
+        compiler_params=pltpu.CompilerParams(vmem_limit_bytes=24 * 1024 * 1024),
         cost_estimate=pl.CostEstimate(
             flops=flops,
             transcendentals=0,

time: 66.5 us -> 62.9 us (0.946)
  Pallas kernels: 24.8 us -> 21 us
  other arithmetic: 11.1 us -> 9.58 us
  waiting for transfers between devices: 16.8 us -> 18.3 us
    pallas_call x2, Pallas kernels: 24.8 us -> 21 us  [spread_call(): pl.pallas_call(functools.partial(spread_kernel, dilation=dilation, pairs=...]
    concatenate x6, other arithmetic: 4.35 us -> 2.83 us  [stack_rows(): stacked = jnp.concatenate([before, volume, after], axis=2)]
    ppermute x2, waiting for transfers between devices: 2.23 us -> 3.74 us  [halos(): low = lax.ppermute(block[-1:], axis, forward)]
    unnamed x6 -> x8, local copies, waits for them, and re-layouts: 2.43 us -> 2.72 us
  transfers between devices with their start and end apart: 7 -> 7, of which waited for: 7 -> 7; matrix products, arithmetic and copies ran while one was open for 10% -> 8% of each run, Pallas kernels for 0% -> 0%
where the time goes in v12:
time: 62.9 us; the launch traced here: 62.7 us
  Pallas kernels  21 us (33%)
  waiting for transfers between devices  18.3 us (29%)
  other arithmetic  9.58 us (15%)
  starting transfers between devices  8.69 us (14%)
  local copies, waits for them, and re-layouts  4.89 us (8%)
    pallas_call x2, Pallas kernels, spread_call(): pl.pallas_call(functools.partial(spread_kernel, dilation=dilation, pairs=...  21 us
    ppermute x3, waiting for transfers between devices, body(): piece = lax.ppermute(piece, 'shot', pairs_list)  10.3 us
    ppermute x2, waiting for transfers between devices, halos(): high = lax.ppermute(block[:1], axis, backward)  4.31 us
    ppermute x2, starting transfers between devices, halos(): high = lax.ppermute(block[:1], axis, backward)  3.99 us
    ppermute x3, starting transfers between devices, body(): piece = lax.ppermute(piece, 'shot', pairs_list)  3.92 us
    ppermute x2, waiting for transfers between devices, halos(): low = lax.ppermute(block[-1:], axis, forward)  3.74 us
    concatenate x6, other arithmetic, stack_rows(): stacked = jnp.concatenate([before, volume, after], axis=2)  2.83 us
    unnamed x8, local copies, waits for them, and re-layouts  2.72 us
  transfers between devices with their start and end apart: 7, of which 7 were waited for; matrix products, arithmetic and copies ran while one was open for 8% of the time, Pallas kernels for 0%

profile of v12, /device:TPU:0, one launch (start us, length us, event | category | flops | bytes accessed | tf_op | source)
XLA Modules:
  0.0 62.7 jit_solution(8833116069219274032)
XLA Ops:
  0.0 0.0 copy-start
  0.0 0.8 %fusion.23 = s32[4]{0:T(128)S(1)} fusion(s32[16,1]{0,1:T(1,128)} %param.5, s32[]{:T(128)S(6)} %select_n.242), kind=kLoop, calls=%fused_computation.72 | loop fusion | bytes 36 | tf_op jit(solution)/shard_map/dynamic_slice | solution.py:111
  0.8 0.1 compare_convert_fusion
  0.9 0.3 copy-done
  1.2 0.7 %bitcast_multiply_fusion.res_ref = bf16[4,1024,128]{2,1,0:T(8,128)(2,1)S(1)} fusion(bf16[4,1024]{1,0:T(4,128)(2,1)S(1)} %compare_convert_fusion, bf16[1,128,4,8,128]{4,3,2,1,0:T(8,128)(2,1)S(1)} %copy-done), kind=kLoop, calls=%fused_computation.23 | loop fusion | flops 2097152 | bytes 2105344 | tf_op jit(solution)/shard_map/mul | solution.py:114
  2.0 0.5 collective-permute-start
  2.5 2.0 %collective-permute-start.1 = (bf16[1,1024,128]{2,1,0:T(8,128)(2,1)S(1)}, bf16[1,1024,128]{2,1,0:T(8,128)(2,1)S(1)}, u32[]{:S(2)}, u32[]{:S(2)}) collective-permute-start(bf16[1,1024,128]{2,1,0:T(8,128)(2,1)S(1)} %get-tuple-element.16), channel_id=1, source_target_pairs={{4,0},{8,4},{12,8},{0,12},{5,1},{9,5},{13,9},{1,13},{6,2},{10,6},{... | collective-permute-start | bytes 786440 | tf_op jit(solution)/shard_map/ppermute | solution.py:85
  4.5 0.4 fusion.27
  5.0 1.2 %pad_select_fusion.2 = (bf16[4,1024,128]{2,1,0:T(8,128)(2,1)S(1)}, bf16[4,1024,128]{2,1,0:T(8,128)(2,1)S(1)}) fusion(bf16[4,1023,128]{2,1,0:T(8,128)(2,1)S(1)} %get-tuple-element.19, pred[1024]{0:T(1024)(128)(4,1)S(1)} %fusion.19, bf16[4,1023,128]{2,1,0:T(8,128)(2,1)S(1)} %get-tuple-element.18, pred[1024]{0:T(1024)(128)(4,1)S(1)} %fusion.20), kind=kLoop, calls=%fused_computation.27 | loop fusion | flops 1048576 | bytes 4194304 | tf_op jit(solution)/shard_map/jit(_where)/select_n | solution.py:98
  6.2 1.9 %fusion.11.x0_ref.x1_ref.x2_ref = bf16[4,1056,384]{2,1,0:T(8,128)(2,1)} fusion(bf16[4,1024,128]{2,1,0:T(8,128)(2,1)S(1)} %get-tuple-element.38, bf16[4,1024,128]{2,1,0:T(8,128)(2,1)S(1)} %bitcast_multiply_fusion.res_ref, bf16[4,1024,128]{2,1,0:T(8,128)(2,1)S(1)} %get-tuple-element.39), kind=kLoop, calls=%fused_computation.15 | loop fusion | flops 19464192 | bytes 6389760 | tf_op jit(solution)/shard_map/concatenate | solution.py:99
  8.0 0.1 pad_add_fusion.scalars_ref
  8.1 0.6 collective-permute-done
  8.7 0.1 fusion.31
  8.8 2.3 %collective-permute-done.1 = bf16[1,1024,128]{2,1,0:T(8,128)(2,1)S(1)} collective-permute-done((bf16[1,1024,128]{2,1,0:T(8,128)(2,1)S(1)}, bf16[1,1024,128]{2,1,0:T(8,128)(2,1)S(1)}, u32[]{:S(2)}, u32[]{:S(2)}) %collective-permute-start.1) | collective-permute-done | bytes 262176 | tf_op jit(solution)/shard_map/ppermute | solution.py:85
  11.2 0.1 fusion.30
  11.3 0.0 copy-start.1
  11.3 0.9 %pad_select_fusion.8 = (bf16[1,1024,128]{2,1,0:T(8,128)(2,1)S(1)}, bf16[1,1024,128]{2,1,0:T(8,128)(2,1)S(1)}, bf16[1,1024,128]{2,1,0:T(8,128)(2,1)S(1)}, bf16[1,1024,128]{2,1,0:T(8,128)(2,1)S(1)}) fusion(bf16[1,1023,128]{2,1,0:T(8,128)(2,1)S(1)} %get-tuple-element.25, pred[1024]{0:T(1024)(128)(4,1)S(1)} %fusion.19, ...), kind=kLoop, calls=%fused_computation.47 | loop fusion | flops 524288 | bytes 2098176 | tf_op jit(solution)/shard_map/jit(_where)/select_n | solution.py:98
  12.2 0.0 copy-start.2
  12.2 0.1 select_maximum_fusion.4.hi_ref
  12.3 0.1 select_maximum_fusion.6.lo_ref
  12.4 0.8 %copy-done.1 = bf16[4,1056,384]{2,1,0:T(8,128)(2,1)S(1)} copy-done((bf16[4,1056,384]{2,1,0:T(8,128)(2,1)S(1)}, bf16[4,1056,384]{2,1,0:T(8,128)(2,1)}, u32[]{:S(2)}) %copy-start.1) | copy-done | bytes 3244056
  13.2 0.6 copy-done.2
  13.7 10.1 %shard_map.46.res_ref = bf16[4,1024,128]{2,1,0:T(8,128)(2,1)S(1)} custom-call(s32[5]{0:T(128)S(1)} %pad_add_fusion.scalars_ref, bf16[1,1056,384]{2,1,0:T(8,128)(2,1)S(1)} %select_maximum_fusion.6.lo_ref, bf16[4,1056,384]{2,1,0:T(8,128)(2,1)S(1)} %copy-done.1, bf16[4,1056,384]{2,1,0:T(8,128)(2,1)S(1)} %copy-done.1, bf16[4,1056,384]{2,1,0:T(8,128)(2,1)S(1)} %copy-done.1, ...), custom_call_target="tpu_custom_call" | custom-call | flops 6228541440 | bytes 7577600 | tf_op jit(solution)/shard_map/pallas_call | solution.py:15
  23.9 0.4 fusion.25
  24.4 0.2 collective-permute-start.2
  24.6 2.0 %collective-permute-start.3 = (bf16[1,1024,128]{2,1,0:T(8,128)(2,1)S(1)}, bf16[1,1024,128]{2,1,0:T(8,128)(2,1)S(1)}, u32[]{:S(2)}, u32[]{:S(2)}) collective-permute-start(bf16[1,1024,128]{2,1,0:T(8,128)(2,1)S(1)} %get-tuple-element.12), channel_id=1, source_target_pairs={{4,0},{8,4},{12,8},{0,12},{5,1},{9,5},{13,9},{1,13},{6,2},{10,6},{... | collective-permute-start | bytes 786440 | tf_op jit(solution)/shard_map/ppermute | solution.py:85
  26.6 0.3 pad_select_fusion
  26.9 0.4 pad_select_fusion.1
  27.3 0.5 fusion.9.x0_ref.x1_ref.x2_ref
  27.8 3.1 %collective-permute-done.2 = bf16[1,1024,128]{2,1,0:T(8,128)(2,1)S(1)} collective-permute-done((bf16[1,1024,128]{2,1,0:T(8,128)(2,1)S(1)}, bf16[1,1024,128]{2,1,0:T(8,128)(2,1)S(1)}, u32[]{:S(2)}, u32[]{:S(2)}) %collective-permute-start.2) | collective-permute-done | bytes 262176 | tf_op jit(solution)/shard_map/ppermute | solution.py:84
  31.0 0.1 fusion.29
  31.1 2.0 %collective-permute-done.3 = bf16[1,1024,128]{2,1,0:T(8,128)(2,1)S(1)} collective-permute-done((bf16[1,1024,128]{2,1,0:T(8,128)(2,1)S(1)}, bf16[1,1024,128]{2,1,0:T(8,128)(2,1)S(1)}, u32[]{:S(2)}, u32[]{:S(2)}) %collective-permute-start.3) | collective-permute-done | bytes 262176 | tf_op jit(solution)/shard_map/ppermute | solution.py:85
  33.1 0.1 fusion.28
  33.2 0.3 pad_select_fusion.5
  33.5 0.2 pad_select_fusion.4
  33.7 0.0 copy-start.3
  33.7 0.1 select_maximum_fusion.hi_ref
  33.8 0.1 select_maximum_fusion.2.lo_ref
  34.0 1.0 %copy-done.3 = bf16[5,3,5,64,64]{4,3,2,1,0:T(8,128)(2,1)S(1)} copy-done((bf16[5,3,5,64,64]{4,3,2,1,0:T(8,128)(2,1)S(1)}, bf16[5,3,5,64,64]{4,3,2,1,0:T(8,128)(2,1)}, u32[]{:S(2)}) %copy-start.3) | copy-done | bytes 614424
  35.0 10.9 %shard_map.47 = bf16[4,1024,128]{2,1,0:T(8,128)(2,1)S(1)} custom-call(s32[5]{0:T(128)S(1)} %pad_add_fusion.scalars_ref, bf16[1,1152,384]{2,1,0:T(8,128)(2,1)S(1)} %select_maximum_fusion.2.lo_ref, bf16[4,1152,384]{2,1,0:T(8,128)(2,1)S(1)} %fusion.9.x0_ref.x1_ref.x2_ref, bf16[4,1152,384]{2,1,0:T(8,128)(2,1)S(1)} %fusion.9.x0_ref.x1_ref.x2_ref, ...), custom_call_target="tpu_custom_call" | custom-call | flops 6794772480 | bytes 8019968 | tf_op jit(solution)/shard_map/pallas_call | solution.py:15
  45.8 0.1 constant_dynamic-slice_fusion.2
  45.9 0.2 collective-permute-start.4
  46.1 2.3 %collective-permute-start.5 = (bf16[4,256,128]{2,1,0:T(8,128)(2,1)S(1)}, bf16[4,256,128]{2,1,0:T(8,128)(2,1)S(1)}, u32[]{:S(2)}, u32[]{:S(2)}) collective-permute-start(bf16[4,256,128]{2,1,0:T(8,128)(2,1)S(1)} %get-tuple-element.11), channel_id=1, source_target_pairs={{0,8},{4,12},{8,0},{12,4},{1,9},{5,13},{9,1},{13,5},{2,10},{6,14},... | collective-permute-start | bytes 786440 | tf_op jit(solution)/shard_map/ppermute | solution.py:132
  48.5 1.4 %collective-permute-start.6 = (bf16[4,256,128]{2,1,0:T(8,128)(2,1)S(1)}, bf16[4,256,128]{2,1,0:T(8,128)(2,1)}, u32[]{:S(2)}, u32[]{:S(2)}) collective-permute-start(bf16[4,256,128]{2,1,0:T(8,128)(2,1)S(1)} %get-tuple-element.10), channel_id=1, source_target_pairs={{0,12},{4,0},{8,4},{12,8},{1,13},{5,1},{9,5},{13,9},{2,14},{6,2},{... | collective-permute-start | bytes 786440 | tf_op jit(solution)/shard_map/ppermute | solution.py:132
  49.8 4.2 %collective-permute-done.4 = bf16[4,256,128]{2,1,0:T(8,128)(2,1)S(1)} collective-permute-done((bf16[4,256,128]{2,1,0:T(8,128)(2,1)S(1)}, bf16[4,256,128]{2,1,0:T(8,128)(2,1)S(1)}, u32[]{:S(2)}, u32[]{:S(2)}) %collective-permute-start.4) | collective-permute-done | bytes 262176 | tf_op jit(solution)/shard_map/ppermute | solution.py:132
  54.0 1.6 %collective-permute-done.5 = bf16[4,256,128]{2,1,0:T(8,128)(2,1)S(1)} collective-permute-done((bf16[4,256,128]{2,1,0:T(8,128)(2,1)S(1)}, bf16[4,256,128]{2,1,0:T(8,128)(2,1)S(1)}, u32[]{:S(2)}, u32[]{:S(2)}) %collective-permute-start.5) | collective-permute-done | bytes 262176 | tf_op jit(solution)/shard_map/ppermute | solution.py:132
  55.6 4.5 %collective-permute-done.6 = bf16[4,256,128]{2,1,0:T(8,128)(2,1)} collective-permute-done((bf16[4,256,128]{2,1,0:T(8,128)(2,1)S(1)}, bf16[4,256,128]{2,1,0:T(8,128)(2,1)}, u32[]{:S(2)}, u32[]{:S(2)}) %collective-permute-start.6) | collective-permute-done | bytes 262176 | tf_op jit(solution)/shard_map/ppermute | solution.py:132
  60.1 1.3 %select_select_fusion.3 = (bf16[4,256,128]{2,1,0:T(8,128)(2,1)S(1)}, bf16[4,256,128]{2,1,0:T(8,128)(2,1)S(1)}, bf16[4,256,128]{2,1,0:T(8,128)(2,1)S(1)}, bf16[4,256,128]{2,1,0:T(8,128)(2,1)S(1)}) fusion(bf16[4,256,128]{2,1,0:T(8,128)(2,1)S(1)} %collective-permute-done.5, bf16[4,256,128]{2,1,0:T(8,128)(2,1)} %collective-permute-done.6, ...), kind=kLoop, calls=%fused_computation.42 | loop fusion | flops 1572864 | bytes 2097168 | tf_op jit(solution)/shard_map/select_n | solution.py:136
  61.4 1.3 %copy_bitcast_fusion = bf16[1,32,16,8,128]{4,3,2,1,0:T(8,128)(2,1)} fusion(bf16[4,256,128]{2,1,0:T(8,128)(2,1)S(1)} %get-tuple-element.6, bf16[4,256,128]{2,1,0:T(8,128)(2,1)S(1)} %get-tuple-element.7, bf16[4,256,128]{2,1,0:T(8,128)(2,1)S(1)} %get-tuple-element.8, bf16[4,256,128]{2,1,0:T(8,128)(2,1)S(1)} %get-tuple-element.5), kind=kLoop, calls=%fused_computation.24 | loop fusion | flops 1572864 | bytes 2097152 | tf_op jit(solution)/shard_map/broadcast_in_dim | solution.py:139
  (9 shorter events, 0.2 us)
Async XLA Ops:
  0.0 1.2 %copy-start = (bf16[1,128,4,8,128]{4,3,2,1,0:T(8,128)(2,1)S(1)}, bf16[1,128,4,8,128]{4,3,2,1,0:T(8,128)(2,1)}, u32[]{:S(2)}) copy-start(bf16[1,128,4,8,128]{4,3,2,1,0:T(8,128)(2,1)} %param.4) | copy-start | bytes 3145732
  2.0 6.7 %collective-permute-start = (bf16[1,1024,128]{2,1,0:T(8,128)(2,1)S(1)}, bf16[1,1024,128]{2,1,0:T(8,128)(2,1)S(1)}, u32[]{:S(2)}, u32[]{:S(2)}) collective-permute-start(bf16[1,1024,128]{2,1,0:T(8,128)(2,1)S(1)} %get-tuple-element.17), channel_id=1, source_target_pairs={{0,4},{4,8},{8,12},{12,0},{1,5},{5,9},{9,13},{13,1},{2,6},{6,10},{... | collective-permute-start | bytes 786440 | tf_op jit(solution)/shard_map/ppermute | solution.py:84
  2.5 8.6 %collective-permute-start.1 = (bf16[1,1024,128]{2,1,0:T(8,128)(2,1)S(1)}, bf16[1,1024,128]{2,1,0:T(8,128)(2,1)S(1)}, u32[]{:S(2)}, u32[]{:S(2)}) collective-permute-start(bf16[1,1024,128]{2,1,0:T(8,128)(2,1)S(1)} %get-tuple-element.16), channel_id=1, source_target_pairs={{4,0},{8,4},{12,8},{0,12},{5,1},{9,5},{13,9},{1,13},{6,2},{10,6},{... | collective-permute-start | bytes 786440 | tf_op jit(solution)/shard_map/ppermute | solution.py:85
  11.3 1.9 %copy-start.1 = (bf16[4,1056,384]{2,1,0:T(8,128)(2,1)S(1)}, bf16[4,1056,384]{2,1,0:T(8,128)(2,1)}, u32[]{:S(2)}) copy-start(bf16[4,1056,384]{2,1,0:T(8,128)(2,1)} %fusion.11.x0_ref.x1_ref.x2_ref) | copy-start | bytes 9732100
  12.2 1.6 %copy-start.2 = (bf16[5,3,5,64,64]{4,3,2,1,0:T(8,128)(2,1)S(1)}, bf16[5,3,5,64,64]{4,3,2,1,0:T(8,128)(2,1)}, u32[]{:S(2)}) copy-start(bf16[5,3,5,64,64]{4,3,2,1,0:T(8,128)(2,1)} %w_ref.2) | copy-start | bytes 1843204
  24.4 6.6 %collective-permute-start.2 = (bf16[1,1024,128]{2,1,0:T(8,128)(2,1)S(1)}, bf16[1,1024,128]{2,1,0:T(8,128)(2,1)S(1)}, u32[]{:S(2)}, u32[]{:S(2)}) collective-permute-start(bf16[1,1024,128]{2,1,0:T(8,128)(2,1)S(1)} %get-tuple-element.13), channel_id=1, source_target_pairs={{0,4},{4,8},{8,12},{12,0},{1,5},{5,9},{9,13},{13,1},{2,6},{6,10},{... | collective-permute-start | bytes 786440 | tf_op jit(solution)/shard_map/ppermute | solution.py:84
  24.6 8.5 %collective-permute-start.3 = (bf16[1,1024,128]{2,1,0:T(8,128)(2,1)S(1)}, bf16[1,1024,128]{2,1,0:T(8,128)(2,1)S(1)}, u32[]{:S(2)}, u32[]{:S(2)}) collective-permute-start(bf16[1,1024,128]{2,1,0:T(8,128)(2,1)S(1)} %get-tuple-element.12), channel_id=1, source_target_pairs={{4,0},{8,4},{12,8},{0,12},{5,1},{9,5},{13,9},{1,13},{6,2},{10,6},{... | collective-permute-start | bytes 786440 | tf_op jit(solution)/shard_map/ppermute | solution.py:85
  33.7 1.3 %copy-start.3 = (bf16[5,3,5,64,64]{4,3,2,1,0:T(8,128)(2,1)S(1)}, bf16[5,3,5,64,64]{4,3,2,1,0:T(8,128)(2,1)}, u32[]{:S(2)}) copy-start(bf16[5,3,5,64,64]{4,3,2,1,0:T(8,128)(2,1)} %w_ref.3) | copy-start | bytes 1843204
  45.9 8.1 %collective-permute-start.4 = (bf16[4,256,128]{2,1,0:T(8,128)(2,1)S(1)}, bf16[4,256,128]{2,1,0:T(8,128)(2,1)S(1)}, u32[]{:S(2)}, u32[]{:S(2)}) collective-permute-start(bf16[4,256,128]{2,1,0:T(8,128)(2,1)S(1)} %get-tuple-element.9), channel_id=1, source_target_pairs={{0,4},{4,8},{8,12},{12,0},{1,5},{5,9},{9,13},{13,1},{2,6},{6,10},{... | collective-permute-start | bytes 786440 | tf_op jit(solution)/shard_map/ppermute | solution.py:132
  46.1 9.5 %collective-permute-start.5 = (bf16[4,256,128]{2,1,0:T(8,128)(2,1)S(1)}, bf16[4,256,128]{2,1,0:T(8,128)(2,1)S(1)}, u32[]{:S(2)}, u32[]{:S(2)}) collective-permute-start(bf16[4,256,128]{2,1,0:T(8,128)(2,1)S(1)} %get-tuple-element.11), channel_id=1, source_target_pairs={{0,8},{4,12},{8,0},{12,4},{1,9},{5,13},{9,1},{13,5},{2,10},{6,14},... | collective-permute-start | bytes 786440 | tf_op jit(solution)/shard_map/ppermute | solution.py:132
  48.5 11.7 %collective-permute-start.6 = (bf16[4,256,128]{2,1,0:T(8,128)(2,1)S(1)}, bf16[4,256,128]{2,1,0:T(8,128)(2,1)}, u32[]{:S(2)}, u32[]{:S(2)}) collective-permute-start(bf16[4,256,128]{2,1,0:T(8,128)(2,1)S(1)} %get-tuple-element.10), channel_id=1, source_target_pairs={{0,12},{4,0},{8,4},{12,8},{1,13},{5,1},{9,5},{13,9},{2,14},{6,2},{... | collective-permute-start | bytes 786440 | tf_op jit(solution)/shard_map/ppermute | solution.py:132

commit v13 on v12

--- a/solution.py
+++ b/solution.py
@@ -8,46 +8,52 @@
 from jax.sharding import PartitionSpec as P
 
 
-def spread_call(low, xs, high, weights, flat, counts, dilation, pairs):
+def spread_call(low, xs, high, weights, flat, counts, dilation, pairs, first=0, stride=1, steps=None):
     shots, rows, lanes = flat.shape
+    steps = shots if steps is None else steps
     scalars = jnp.concatenate([jnp.zeros((1,), jnp.int32), counts])
-    flops = 2 * shots * 3 * xs.shape[1] * xs.shape[2] * 5 * lanes
+    flops = 2 * steps * 3 * xs.shape[1] * xs.shape[2] * 5 * lanes
     return pl.pallas_call(
-        functools.partial(spread_kernel, dilation=dilation, pairs=pairs),
+        functools.partial(spread_kernel, dilation=dilation, pairs=pairs, first=first, stride=stride, shots=shots),
         grid_spec=pltpu.PrefetchScalarGridSpec(
             num_scalar_prefetch=1,
-            grid=(shots,),
+            grid=(steps,),
             in_specs=[
                 pl.BlockSpec((1, xs.shape[1], xs.shape[2]), lambda s, c: (0, 0, 0)),
-                pl.BlockSpec((1, xs.shape[1], xs.shape[2]), lambda s, c: (jnp.maximum(s - 1, 0), 0, 0)),
-                pl.BlockSpec((1, xs.shape[1], xs.shape[2]), lambda s, c: (s, 0, 0)),
                 pl.BlockSpec(
-                    (1, xs.shape[1], xs.shape[2]), lambda s, c: (jnp.minimum(s + 1, shots - 1), 0, 0)
+                    (1, xs.shape[1], xs.shape[2]), lambda s, c: (jnp.maximum(first + s * stride - 1, 0), 0, 0)
+                ),
+                pl.BlockSpec((1, xs.shape[1], xs.shape[2]), lambda s, c: (first + s * stride, 0, 0)),
+                pl.BlockSpec(
+                    (1, xs.shape[1], xs.shape[2]),
+                    lambda s, c: (jnp.minimum(first + s * stride + 1, shots - 1), 0, 0),
                 ),
                 pl.BlockSpec((1, xs.shape[1], xs.shape[2]), lambda s, c: (0, 0, 0)),
                 pl.BlockSpec(weights.shape, lambda s, c: (0, 0, 0, 0, 0)),
-                pl.BlockSpec((1, rows, lanes), lambda s, c: (s, 0, 0)),
+                pl.BlockSpec((1, rows, lanes), lambda s, c: (first + s * stride, 0, 0)),
             ],
             out_specs=pl.BlockSpec((1, rows, lanes), lambda s, c: (s, 0, 0)),
             scratch_shapes=[pltpu.VMEM((3 * xs.shape[2], 5 * lanes), weights.dtype)],
         ),
-        out_shape=jax.ShapeDtypeStruct((shots, rows, lanes), jnp.bfloat16),
+        out_shape=jax.ShapeDtypeStruct((steps, rows, lanes), jnp.bfloat16),
         compiler_params=pltpu.CompilerParams(vmem_limit_bytes=24 * 1024 * 1024),
         cost_estimate=pl.CostEstimate(
             flops=flops,
             transcendentals=0,
-            bytes_accessed=(xs.size + low.size + high.size) * 2 + weights.size * 2 + 4 * shots * rows * lanes,
+            bytes_accessed=(xs.size + low.size + high.size) * 2 + weights.size * 2 + 4 * steps * rows * lanes,
         ),
     )(scalars, low, xs, xs, xs, high, weights, flat)
 
 
 def spread_kernel(
-    scalars_ref, lo_ref, x0_ref, x1_ref, x2_ref, hi_ref, w_ref, res_ref, out_ref, rhs_ref, *, dilation, pairs
+    scalars_ref, lo_ref, x0_ref, x1_ref, x2_ref, hi_ref, w_ref, res_ref, out_ref, rhs_ref, *, dilation, pairs,
+    first, stride, shots,
 ):
-    s = pl.program_id(0)
+    step = pl.program_id(0)
+    s = first + step * stride
     receiver_taps, shot_taps, time_taps, channels, _ = w_ref.shape
 
-    @pl.when(s == 0)
+    @pl.when(step == 0)
     def _():
         zero = jnp.zeros((channels, channels), rhs_ref.dtype)
         for b in range(shot_taps):
@@ -62,7 +68,7 @@
 
     rows, lanes = out_ref.shape[1:]
     first_shot = jnp.where(s == 0, lo_ref[0], x0_ref[0])
-    last_shot = jnp.where(s == pl.num_programs(0) - 1, hi_ref[0], x2_ref[0])
+    last_shot = jnp.where(s == shots - 1, hi_ref[0], x2_ref[0])
     lhs = jnp.concatenate([first_shot, x1_ref[0], last_shot], axis=1)
     spread = jnp.dot(lhs, rhs_ref[...], preferred_element_type=jnp.float32)
     total = None
@@ -120,9 +126,10 @@
     low2, high2 = halos(flat2, "shot")
     xs2 = stack_rows(flat2, 4, pairs)
     span = receivers // count
-    whole = spread_call(
-        stack_rows(low2, 4, pairs), xs2, stack_rows(high2, 4, pairs), second_weight, flat2, chosen, 4, pairs
-    )
+    halo2 = (stack_rows(low2, 4, pairs), xs2, stack_rows(high2, 4, pairs), second_weight, flat2, chosen, 4, pairs)
+    inner = spread_call(xs2, xs2, xs2, *halo2[3:], 1, 1, shot_local - 2)
+    edges = spread_call(*halo2, 0, shot_local - 1, 2)
+    whole = jnp.concatenate([edges[:1], inner, edges[1:]], axis=0)
     arrived = []
     for shift in range(count):
         target = lax.rem(me + shift, count)

time: 62.9 us -> 57.6 us (0.916)
  waiting for transfers between devices: 18.3 us -> 13.1 us
  local copies, waits for them, and re-layouts: 4.89 us -> 3.9 us
  Pallas kernels: 21 us -> 21.9 us
    ppermute x2, waiting for transfers between devices: 3.74 us -> 0.58 us  [halos(): low = lax.ppermute(block[-1:], axis, forward)]
    ppermute x2, waiting for transfers between devices: 4.31 us -> 2.29 us  [halos(): high = lax.ppermute(block[:1], axis, backward)]
    unnamed x8, local copies, waits for them, and re-layouts: 2.72 us -> 1.68 us
    pallas_call x2 -> x3, Pallas kernels: 21 us -> 21.9 us  [spread_call(): pl.pallas_call(functools.partial(spread_kernel, dilation=dilation, pairs=...]
  transfers between devices with their start and end apart: 7 -> 7, of which waited for: 7 -> 5; matrix products, arithmetic and copies ran while one was open for 8% -> 8% of each run, Pallas kernels for 0% -> 10%
where the time goes in v13:
time: 57.6 us; the launch traced here: 57.4 us
  Pallas kernels  21.9 us (38%)
  waiting for transfers between devices  13.1 us (23%)
  other arithmetic  9.71 us (17%)
  starting transfers between devices  8.4 us (15%)
  local copies, waits for them, and re-layouts  3.9 us (7%)
    pallas_call x3, Pallas kernels, spread_call(): pl.pallas_call(functools.partial(spread_kernel, dilation=dilation, pairs=...  21.9 us
    ppermute x3, waiting for transfers between devices, body(): piece = lax.ppermute(piece, 'shot', pairs_list)  10.3 us
    ppermute x2, starting transfers between devices, halos(): high = lax.ppermute(block[:1], axis, backward)  4.16 us
    ppermute x3, starting transfers between devices, body(): piece = lax.ppermute(piece, 'shot', pairs_list)  3.45 us
    concatenate x6, other arithmetic, stack_rows(): stacked = jnp.concatenate([before, volume, after], axis=2)  2.83 us
    select_n x4, other arithmetic, stack_rows(): after = jnp.where(phase == pairs - 1, jnp.zeros_like(after), after)  2.58 us
    ppermute x2, waiting for transfers between devices, halos(): high = lax.ppermute(block[:1], axis, backward)  2.29 us
    unnamed x8, local copies, waits for them, and re-layouts  1.68 us
  transfers between devices with their start and end apart: 7, of which 5 were waited for; matrix products, arithmetic and copies ran while one was open for 8% of the time, Pallas kernels for 10%

profile of v13, /device:TPU:0, one launch (start us, length us, event | category | flops | bytes accessed | tf_op | source)
XLA Modules:
  0.0 57.4 jit_solution(16181579314233214064)
XLA Ops:
  0.0 0.0 copy-start
  0.0 0.8 %fusion.23 = s32[4]{0:T(128)S(1)} fusion(s32[16,1]{0,1:T(1,128)} %param.5, s32[]{:T(128)S(6)} %select_n.242), kind=kLoop, calls=%fused_computation.73 | loop fusion | bytes 36 | tf_op jit(solution)/shard_map/dynamic_slice | solution.py:117
  0.8 0.1 compare_convert_fusion
  0.9 0.3 copy-done
  1.2 0.7 %bitcast_multiply_fusion.res_ref = bf16[4,1024,128]{2,1,0:T(8,128)(2,1)S(1)} fusion(bf16[4,1024]{1,0:T(4,128)(2,1)S(1)} %compare_convert_fusion, bf16[1,128,4,8,128]{4,3,2,1,0:T(8,128)(2,1)S(1)} %copy-done), kind=kLoop, calls=%fused_computation.24 | loop fusion | flops 2097152 | bytes 2105344 | tf_op jit(solution)/shard_map/mul | solution.py:120
  2.0 0.5 collective-permute-start
  2.5 2.0 %collective-permute-start.1 = (bf16[1,1024,128]{2,1,0:T(8,128)(2,1)S(1)}, bf16[1,1024,128]{2,1,0:T(8,128)(2,1)S(1)}, u32[]{:S(2)}, u32[]{:S(2)}) collective-permute-start(bf16[1,1024,128]{2,1,0:T(8,128)(2,1)S(1)} %get-tuple-element.16), channel_id=1, source_target_pairs={{4,0},{8,4},{12,8},{0,12},{5,1},{9,5},{13,9},{1,13},{6,2},{10,6},{... | collective-permute-start | bytes 786440 | tf_op jit(solution)/shard_map/ppermute | solution.py:91
  4.5 0.4 fusion.27
  5.0 1.2 %pad_select_fusion.2 = (bf16[4,1024,128]{2,1,0:T(8,128)(2,1)S(1)}, bf16[4,1024,128]{2,1,0:T(8,128)(2,1)S(1)}) fusion(bf16[4,1023,128]{2,1,0:T(8,128)(2,1)S(1)} %get-tuple-element.19, pred[1024]{0:T(1024)(128)(4,1)S(1)} %fusion.19, bf16[4,1023,128]{2,1,0:T(8,128)(2,1)S(1)} %get-tuple-element.18, pred[1024]{0:T(1024)(128)(4,1)S(1)} %fusion.20), kind=kLoop, calls=%fused_computation.28 | loop fusion | flops 1048576 | bytes 4194304 | tf_op jit(solution)/shard_map/jit(_where)/select_n | solution.py:104
  6.2 1.9 %fusion.11.x0_ref.x1_ref.x2_ref = bf16[4,1056,384]{2,1,0:T(8,128)(2,1)} fusion(bf16[4,1024,128]{2,1,0:T(8,128)(2,1)S(1)} %get-tuple-element.40, bf16[4,1024,128]{2,1,0:T(8,128)(2,1)S(1)} %bitcast_multiply_fusion.res_ref, bf16[4,1024,128]{2,1,0:T(8,128)(2,1)S(1)} %get-tuple-element.41), kind=kLoop, calls=%fused_computation.15 | loop fusion | flops 19464192 | bytes 6389760 | tf_op jit(solution)/shard_map/concatenate | solution.py:105
  8.1 0.1 pad_add_fusion.scalars_ref
  8.1 0.6 %collective-permute-done = bf16[1,1024,128]{2,1,0:T(8,128)(2,1)S(1)} collective-permute-done((bf16[1,1024,128]{2,1,0:T(8,128)(2,1)S(1)}, bf16[1,1024,128]{2,1,0:T(8,128)(2,1)S(1)}, u32[]{:S(2)}, u32[]{:S(2)}) %collective-permute-start) | collective-permute-done | bytes 262176 | tf_op jit(solution)/shard_map/ppermute | solution.py:90
  8.7 0.1 fusion.32
  8.8 2.3 %collective-permute-done.1 = bf16[1,1024,128]{2,1,0:T(8,128)(2,1)S(1)} collective-permute-done((bf16[1,1024,128]{2,1,0:T(8,128)(2,1)S(1)}, bf16[1,1024,128]{2,1,0:T(8,128)(2,1)S(1)}, u32[]{:S(2)}, u32[]{:S(2)}) %collective-permute-start.1) | collective-permute-done | bytes 262176 | tf_op jit(solution)/shard_map/ppermute | solution.py:91
  11.2 0.1 fusion.31
  11.3 0.0 copy-start.2
  11.3 0.9 %pad_select_fusion.8 = (bf16[1,1024,128]{2,1,0:T(8,128)(2,1)S(1)}, bf16[1,1024,128]{2,1,0:T(8,128)(2,1)S(1)}, bf16[1,1024,128]{2,1,0:T(8,128)(2,1)S(1)}, bf16[1,1024,128]{2,1,0:T(8,128)(2,1)S(1)}) fusion(bf16[1,1023,128]{2,1,0:T(8,128)(2,1)S(1)} %get-tuple-element.27, pred[1024]{0:T(1024)(128)(4,1)S(1)} %fusion.19, ...), kind=kLoop, calls=%fused_computation.48 | loop fusion | flops 524288 | bytes 2098176 | tf_op jit(solution)/shard_map/jit(_where)/select_n | solution.py:104
  12.2 0.0 copy-start.3
  12.2 0.1 select_maximum_fusion.4.hi_ref
  12.3 0.1 select_maximum_fusion.6.lo_ref
  12.4 0.8 %copy-done.2 = bf16[4,1056,384]{2,1,0:T(8,128)(2,1)S(1)} copy-done((bf16[4,1056,384]{2,1,0:T(8,128)(2,1)S(1)}, bf16[4,1056,384]{2,1,0:T(8,128)(2,1)}, u32[]{:S(2)}) %copy-start.2) | copy-done | bytes 3244056
  13.2 0.6 copy-done.3
  13.7 10.1 %shard_map.46.res_ref = bf16[4,1024,128]{2,1,0:T(8,128)(2,1)S(1)} custom-call(s32[5]{0:T(128)S(1)} %pad_add_fusion.scalars_ref, bf16[1,1056,384]{2,1,0:T(8,128)(2,1)S(1)} %select_maximum_fusion.6.lo_ref, bf16[4,1056,384]{2,1,0:T(8,128)(2,1)S(1)} %copy-done.2, bf16[4,1056,384]{2,1,0:T(8,128)(2,1)S(1)} %copy-done.2, bf16[4,1056,384]{2,1,0:T(8,128)(2,1)S(1)} %copy-done.2, ...), custom_call_target="tpu_custom_call" | custom-call | flops 6228541440 | bytes 7577600 | tf_op jit(solution)/shard_map/pallas_call | solution.py:16
  23.9 0.4 fusion.25
  24.4 0.3 pad_select_fusion
  24.7 0.4 pad_select_fusion.1
  25.1 0.2 collective-permute-start.2
  25.3 0.0 copy-start.1
  25.3 2.2 %collective-permute-start.3 = (bf16[1,1024,128]{2,1,0:T(8,128)(2,1)S(1)}, bf16[1,1024,128]{2,1,0:T(8,128)(2,1)S(1)}, u32[]{:S(2)}, u32[]{:S(2)}) collective-permute-start(bf16[1,1024,128]{2,1,0:T(8,128)(2,1)S(1)} %get-tuple-element.12), channel_id=1, source_target_pairs={{4,0},{8,4},{12,8},{0,12},{5,1},{9,5},{13,9},{1,13},{6,2},{10,6},{... | collective-permute-start | bytes 786440 | tf_op jit(solution)/shard_map/ppermute | solution.py:91
  27.5 0.5 fusion.9.x0_ref.x1_ref.x2_ref.lo_ref.hi_ref
  28.0 0.0 copy-done.1
  28.0 5.9 %shard_map.48 = bf16[2,1024,128]{2,1,0:T(8,128)(2,1)S(1)} custom-call(s32[5]{0:T(128)S(1)} %pad_add_fusion.scalars_ref, bf16[4,1152,384]{2,1,0:T(8,128)(2,1)S(1)} %fusion.9.x0_ref.x1_ref.x2_ref.lo_ref.hi_ref, bf16[4,1152,384]{2,1,0:T(8,128)(2,1)S(1)} %fusion.9.x0_ref.x1_ref.x2_ref.lo_ref.hi_ref, ...), custom_call_target="tpu_custom_call" | custom-call | flops 3397386240 | bytes 12279808 | tf_op jit(solution)/shard_map/pallas_call | solution.py:16
  33.9 0.0 collective-permute-done.2
  33.9 0.1 fusion.30
  34.0 0.0 collective-permute-done.3
  34.1 0.1 fusion.29
  34.2 0.3 pad_select_fusion.5
  34.5 0.2 pad_select_fusion.4
  34.7 0.1 select_maximum_fusion.hi_ref
  34.8 0.1 select_maximum_fusion.2.lo_ref
  34.9 5.9 %shard_map.47 = bf16[2,1024,128]{2,1,0:T(8,128)(2,1)S(1)} custom-call(s32[5]{0:T(128)S(1)} %pad_add_fusion.scalars_ref, bf16[1,1152,384]{2,1,0:T(8,128)(2,1)S(1)} %select_maximum_fusion.2.lo_ref, bf16[4,1152,384]{2,1,0:T(8,128)(2,1)S(1)} %fusion.9.x0_ref.x1_ref.x2_ref.lo_ref.hi_ref, bf16[4,1152,384]{2,1,0:T(8,128)(2,1)S(1)} %fusion.9.x0_ref.x1_ref.x2_ref.lo_ref.hi_ref, ...), custom_call_target="tpu_custom_call" | custom-call | flops 3397386240 | bytes 6971392 | tf_op jit(solution)/shard_map/pallas_call | solution.py:16
  40.9 0.1 pad_maximum_fusion
  41.0 0.1 constant_dynamic-slice_fusion.2
  41.1 1.1 %collective-permute-start.4 = (bf16[4,256,128]{2,1,0:T(8,128)(2,1)S(1)}, bf16[4,256,128]{2,1,0:T(8,128)(2,1)S(1)}, u32[]{:S(2)}, u32[]{:S(2)}) collective-permute-start(bf16[4,256,128]{2,1,0:T(8,128)(2,1)S(1)} %get-tuple-element.9), channel_id=1, source_target_pairs={{0,4},{4,8},{8,12},{12,0},{1,5},{5,9},{9,13},{13,1},{2,6},{6,10},{... | collective-permute-start | bytes 786440 | tf_op jit(solution)/shard_map/ppermute | solution.py:139
  42.2 1.0 %collective-permute-start.5 = (bf16[4,256,128]{2,1,0:T(8,128)(2,1)S(1)}, bf16[4,256,128]{2,1,0:T(8,128)(2,1)S(1)}, u32[]{:S(2)}, u32[]{:S(2)}) collective-permute-start(bf16[4,256,128]{2,1,0:T(8,128)(2,1)S(1)} %get-tuple-element.11), channel_id=1, source_target_pairs={{0,8},{4,12},{8,0},{12,4},{1,9},{5,13},{9,1},{13,5},{2,10},{6,14},... | collective-permute-start | bytes 786440 | tf_op jit(solution)/shard_map/ppermute | solution.py:139
  43.2 1.4 %collective-permute-start.6 = (bf16[4,256,128]{2,1,0:T(8,128)(2,1)S(1)}, bf16[4,256,128]{2,1,0:T(8,128)(2,1)}, u32[]{:S(2)}, u32[]{:S(2)}) collective-permute-start(bf16[4,256,128]{2,1,0:T(8,128)(2,1)S(1)} %get-tuple-element.10), channel_id=1, source_target_pairs={{0,12},{4,0},{8,4},{12,8},{1,13},{5,1},{9,5},{13,9},{2,14},{6,2},{... | collective-permute-start | bytes 786440 | tf_op jit(solution)/shard_map/ppermute | solution.py:139
  44.5 3.6 %collective-permute-done.4 = bf16[4,256,128]{2,1,0:T(8,128)(2,1)S(1)} collective-permute-done((bf16[4,256,128]{2,1,0:T(8,128)(2,1)S(1)}, bf16[4,256,128]{2,1,0:T(8,128)(2,1)S(1)}, u32[]{:S(2)}, u32[]{:S(2)}) %collective-permute-start.4) | collective-permute-done | bytes 262176 | tf_op jit(solution)/shard_map/ppermute | solution.py:139
  48.1 3.3 %collective-permute-done.5 = bf16[4,256,128]{2,1,0:T(8,128)(2,1)S(1)} collective-permute-done((bf16[4,256,128]{2,1,0:T(8,128)(2,1)S(1)}, bf16[4,256,128]{2,1,0:T(8,128)(2,1)S(1)}, u32[]{:S(2)}, u32[]{:S(2)}) %collective-permute-start.5) | collective-permute-done | bytes 262176 | tf_op jit(solution)/shard_map/ppermute | solution.py:139
  51.4 3.4 %collective-permute-done.6 = bf16[4,256,128]{2,1,0:T(8,128)(2,1)} collective-permute-done((bf16[4,256,128]{2,1,0:T(8,128)(2,1)S(1)}, bf16[4,256,128]{2,1,0:T(8,128)(2,1)}, u32[]{:S(2)}, u32[]{:S(2)}) %collective-permute-start.6) | collective-permute-done | bytes 262176 | tf_op jit(solution)/shard_map/ppermute | solution.py:139
  54.8 1.3 %select_select_fusion.3 = (bf16[4,256,128]{2,1,0:T(8,128)(2,1)S(1)}, bf16[4,256,128]{2,1,0:T(8,128)(2,1)S(1)}, bf16[4,256,128]{2,1,0:T(8,128)(2,1)S(1)}, bf16[4,256,128]{2,1,0:T(8,128)(2,1)S(1)}) fusion(bf16[4,256,128]{2,1,0:T(8,128)(2,1)S(1)} %collective-permute-done.5, bf16[4,256,128]{2,1,0:T(8,128)(2,1)} %collective-permute-done.6, ...), kind=kLoop, calls=%fused_computation.43 | loop fusion | flops 1572864 | bytes 2097168 | tf_op jit(solution)/shard_map/select_n | solution.py:143
  56.1 1.3 %copy_bitcast_fusion = bf16[1,32,16,8,128]{4,3,2,1,0:T(8,128)(2,1)} fusion(bf16[4,256,128]{2,1,0:T(8,128)(2,1)S(1)} %get-tuple-element.6, bf16[4,256,128]{2,1,0:T(8,128)(2,1)S(1)} %get-tuple-element.7, bf16[4,256,128]{2,1,0:T(8,128)(2,1)S(1)} %get-tuple-element.8, bf16[4,256,128]{2,1,0:T(8,128)(2,1)S(1)} %get-tuple-element.5), kind=kLoop, calls=%fused_computation.25 | loop fusion | flops 1572864 | bytes 2097152 | tf_op jit(solution)/shard_map/broadcast_in_dim | solution.py:146
  (10 shorter events, 0.2 us)
Async XLA Ops:
  0.0 1.2 %copy-start = (bf16[1,128,4,8,128]{4,3,2,1,0:T(8,128)(2,1)S(1)}, bf16[1,128,4,8,128]{4,3,2,1,0:T(8,128)(2,1)}, u32[]{:S(2)}) copy-start(bf16[1,128,4,8,128]{4,3,2,1,0:T(8,128)(2,1)} %param.4) | copy-start | bytes 3145732
  2.0 6.7 %collective-permute-start = (bf16[1,1024,128]{2,1,0:T(8,128)(2,1)S(1)}, bf16[1,1024,128]{2,1,0:T(8,128)(2,1)S(1)}, u32[]{:S(2)}, u32[]{:S(2)}) collective-permute-start(bf16[1,1024,128]{2,1,0:T(8,128)(2,1)S(1)} %get-tuple-element.17), channel_id=1, source_target_pairs={{0,4},{4,8},{8,12},{12,0},{1,5},{5,9},{9,13},{13,1},{2,6},{6,10},{... | collective-permute-start | bytes 786440 | tf_op jit(solution)/shard_map/ppermute | solution.py:90
  2.5 8.6 %collective-permute-start.1 = (bf16[1,1024,128]{2,1,0:T(8,128)(2,1)S(1)}, bf16[1,1024,128]{2,1,0:T(8,128)(2,1)S(1)}, u32[]{:S(2)}, u32[]{:S(2)}) collective-permute-start(bf16[1,1024,128]{2,1,0:T(8,128)(2,1)S(1)} %get-tuple-element.16), channel_id=1, source_target_pairs={{4,0},{8,4},{12,8},{0,12},{5,1},{9,5},{13,9},{1,13},{6,2},{10,6},{... | collective-permute-start | bytes 786440 | tf_op jit(solution)/shard_map/ppermute | solution.py:91
  11.3 1.9 %copy-start.2 = (bf16[4,1056,384]{2,1,0:T(8,128)(2,1)S(1)}, bf16[4,1056,384]{2,1,0:T(8,128)(2,1)}, u32[]{:S(2)}) copy-start(bf16[4,1056,384]{2,1,0:T(8,128)(2,1)} %fusion.11.x0_ref.x1_ref.x2_ref) | copy-start | bytes 9732100
  12.2 1.6 %copy-start.3 = (bf16[5,3,5,64,64]{4,3,2,1,0:T(8,128)(2,1)S(1)}, bf16[5,3,5,64,64]{4,3,2,1,0:T(8,128)(2,1)}, u32[]{:S(2)}) copy-start(bf16[5,3,5,64,64]{4,3,2,1,0:T(8,128)(2,1)} %w_ref.3) | copy-start | bytes 1843204
  25.1 8.8 %collective-permute-start.2 = (bf16[1,1024,128]{2,1,0:T(8,128)(2,1)S(1)}, bf16[1,1024,128]{2,1,0:T(8,128)(2,1)S(1)}, u32[]{:S(2)}, u32[]{:S(2)}) collective-permute-start(bf16[1,1024,128]{2,1,0:T(8,128)(2,1)S(1)} %get-tuple-element.13), channel_id=1, source_target_pairs={{0,4},{4,8},{8,12},{12,0},{1,5},{5,9},{9,13},{13,1},{2,6},{6,10},{... | collective-permute-start | bytes 786440 | tf_op jit(solution)/shard_map/ppermute | solution.py:90
  25.3 2.7 %copy-start.1 = (bf16[5,3,5,64,64]{4,3,2,1,0:T(8,128)(2,1)S(1)}, bf16[5,3,5,64,64]{4,3,2,1,0:T(8,128)(2,1)}, u32[]{:S(2)}) copy-start(bf16[5,3,5,64,64]{4,3,2,1,0:T(8,128)(2,1)} %w_ref.5) | copy-start | bytes 1843204
  25.3 8.7 %collective-permute-start.3 = (bf16[1,1024,128]{2,1,0:T(8,128)(2,1)S(1)}, bf16[1,1024,128]{2,1,0:T(8,128)(2,1)S(1)}, u32[]{:S(2)}, u32[]{:S(2)}) collective-permute-start(bf16[1,1024,128]{2,1,0:T(8,128)(2,1)S(1)} %get-tuple-element.12), channel_id=1, source_target_pairs={{4,0},{8,4},{12,8},{0,12},{5,1},{9,5},{13,9},{1,13},{6,2},{10,6},{... | collective-permute-start | bytes 786440 | tf_op jit(solution)/shard_map/ppermute | solution.py:91
  41.1 7.0 %collective-permute-start.4 = (bf16[4,256,128]{2,1,0:T(8,128)(2,1)S(1)}, bf16[4,256,128]{2,1,0:T(8,128)(2,1)S(1)}, u32[]{:S(2)}, u32[]{:S(2)}) collective-permute-start(bf16[4,256,128]{2,1,0:T(8,128)(2,1)S(1)} %get-tuple-element.9), channel_id=1, source_target_pairs={{0,4},{4,8},{8,12},{12,0},{1,5},{5,9},{9,13},{13,1},{2,6},{6,10},{... | collective-permute-start | bytes 786440 | tf_op jit(solution)/shard_map/ppermute | solution.py:139
  42.2 9.2 %collective-permute-start.5 = (bf16[4,256,128]{2,1,0:T(8,128)(2,1)S(1)}, bf16[4,256,128]{2,1,0:T(8,128)(2,1)S(1)}, u32[]{:S(2)}, u32[]{:S(2)}) collective-permute-start(bf16[4,256,128]{2,1,0:T(8,128)(2,1)S(1)} %get-tuple-element.11), channel_id=1, source_target_pairs={{0,8},{4,12},{8,0},{12,4},{1,9},{5,13},{9,1},{13,5},{2,10},{6,14},... | collective-permute-start | bytes 786440 | tf_op jit(solution)/shard_map/ppermute | solution.py:139
  43.2 11.7 %collective-permute-start.6 = (bf16[4,256,128]{2,1,0:T(8,128)(2,1)S(1)}, bf16[4,256,128]{2,1,0:T(8,128)(2,1)}, u32[]{:S(2)}, u32[]{:S(2)}) collective-permute-start(bf16[4,256,128]{2,1,0:T(8,128)(2,1)S(1)} %get-tuple-element.10), channel_id=1, source_target_pairs={{0,12},{4,0},{8,4},{12,8},{1,13},{5,1},{9,5},{13,9},{2,14},{6,2},{... | collective-permute-start | bytes 786440 | tf_op jit(solution)/shard_map/ppermute | solution.py:139
